TPU v7x, 128 devices: a whole 4x4x4 slice. The times are simulated.
128 devices in a mesh: leaf: 32 (over x, y, core), probe: 4 (over z).
Axes of the slice: x: 4, y: 4, z: 4, core: 2. Of those that a mesh axis runs over, the one named last changes fastest.
Arguments:
- child_updates: bfloat16 [1024, 512, 512], P('leaf'), may hold values from -0.25 to 0.25
- child_probes: bfloat16 [256, 524288], P('probe', 'leaf'), may hold values from -6 to 6
- child_dest: int32 [4096, 1], P('leaf'), may hold values from 0 to 31; in each aligned block of 128 rows (0 to 127, 128 to 255, ...) at most 8 rows name the same one
- child_rows: int32 [4096, 128], P('leaf'), may hold values from 0 to 2047
- parent_blocks: bfloat16 [2048, 128, 128], P('leaf'), may hold values from -0.5 to 0.5
- coupling: int32 [2048, 2], P('leaf'), may hold values from 0 to 15
- parent_probes: bfloat16 [256, 65536], P('probe', 'leaf'), may hold values from -6 to 6
- sketch: float32 [256, 128], P('probe'), may hold values from -0.375 to 0.375
- rank_one: int32 [32], P('leaf'), may hold values from 96 to 128, as said below
- rank_two: int32 [16], replicated, may hold values from 96 to 128, as said below
- rank_three: int32 [8], replicated, may hold values from 96 to 128, as said below
Outputs:
- basis_one: float32 [65536, 128], P(('leaf', 'probe'))
- basis_two: float32 [4096, 128], P('leaf')
- basis_three: float32 [4096, 128], P('leaf')
- top_sample: float32 [256, 4096], P('probe', 'leaf')
Inputs may be any that keep to these rules, and one draw needn't show every extreme that they name: `child_dest`: among the row blocks of one front group, no parent front is named by more than 8 blocks, and some parent front is named by exactly 8. `rank_one`: one node has rank 128. `rank_two`: one node has rank 128. `rank_three`: one node has rank 128.
All inputs are finite; a program needn't handle non-finite values.
Results may differ from a plain program's by a relative error of at most 0.0065.
Values may be sent and summed in bfloat16 or wider, within the bound.
No kernel may reach another device: no remote copies, remote signals or barrier semaphores. Data moves between devices by JAX's collectives and lax.ppermute only.
A program may use at most 192 MiB of HBM per device.

v0:
```python
import functools

import jax
import jax.numpy as jnp
from jax import lax
from jax.experimental import pallas as pl
from jax.experimental.pallas import tpu as pltpu
from jax.sharding import PartitionSpec as P

highest = lax.Precision.HIGHEST

SLOT_CAP = 8


def partner_2(block, axis, stride):
    count = lax.axis_size(axis)
    route = []
    for low in range(count):
        high = low | 1 << stride
        if high != low and high < count:
            route += [(low, high), (high, low)]
    return lax.ppermute(block, axis, route)


def butterfly_sum(block, axis):
    count = lax.axis_size(axis)
    stride = 0
    while 1 << stride < count:
        block = block + partner_2(block, axis, stride)
        stride += 1
    return block


def ordered_sum(block, axis):
    count = lax.axis_size(axis)
    gathered = gather_rows(block[None], axis)
    total = gathered[0]
    for member in range(1, count):
        total = total + gathered[member]
    return total


def gather_rows(block, axis):
    count = lax.axis_size(axis)
    index = lax.axis_index(axis)
    pieces = [block]
    for shift in range(1, count):
        route = [(j, (j + shift) % count) for j in range(count)]
        pieces.append(lax.ppermute(block, axis, route))
    stacked = jnp.stack(pieces)
    order = (index - jnp.arange(count, dtype=jnp.int32)) % count
    stacked = jnp.take(stacked, order, axis=0)
    return stacked.reshape((count * block.shape[0],) + block.shape[1:])


def extend_add_kernel(count_ref, load_ref, start_ref, out_ref, *, slots, probes):
    source = pl.program_id(0)
    lanes = load_ref.shape[2]
    high_count = out_ref.shape[0] // probes
    info = slots * probes

    @pl.when(source == 0)
    def _():
        out_ref[...] = start_ref[...]

    @pl.when(count_ref[source] > 0)
    def _():
        spread, hot = [], []
        for slot in range(slots):
            high = load_ref[0, pl.ds(info + slot, 1), :].astype(jnp.float32).astype(jnp.int32)
            low = load_ref[0, pl.ds(info + slots + slot, 1), :].astype(jnp.float32).astype(jnp.int32)
            vals = load_ref[0, pl.ds(slot * probes, probes), :]
            zero = jnp.zeros_like(vals)
            spread.append(
                jnp.concatenate([jnp.where(high == h, vals, zero) for h in range(high_count)], axis=0)
            )
            hot.append(
                (lax.broadcasted_iota(jnp.int32, (lanes, lanes), 0) == low).astype(jnp.bfloat16)
            )
        spread = jnp.concatenate(spread, axis=1)
        hot = jnp.concatenate(hot, axis=1)
        out_ref[...] += lax.dot_general(
            spread, hot, (((1,), (1,)), ((), ())), preferred_element_type=jnp.float32
        )


def extend_add(load, counts, start, slots, probes):
    sources, depth, lanes = load.shape
    kernel = functools.partial(extend_add_kernel, slots=slots, probes=probes)
    return pl.pallas_call(
        kernel,
        grid_spec=pltpu.PrefetchScalarGridSpec(
            num_scalar_prefetch=1,
            grid=(sources,),
            in_specs=[
                pl.BlockSpec((1, depth, lanes), lambda s, c: (s, 0, 0)),
                pl.BlockSpec(start.shape, lambda s, c: (0, 0)),
            ],
            out_specs=pl.BlockSpec(start.shape, lambda s, c: (0, 0)),
        ),
        out_shape=jax.ShapeDtypeStruct(start.shape, jnp.float32),
        compiler_params=pltpu.CompilerParams(dimension_semantics=("arbitrary",)),
    )(counts, load, start)


def exchange_shares(block, axis):
    count = lax.axis_size(axis)
    index = lax.axis_index(axis)
    got = [jnp.take(block, index, axis=1)]
    for shift in range(1, count):
        route = [(j, (j + shift) % count) for j in range(count)]
        outgoing = jnp.take(block, (index + shift) % count, axis=1)
        got.append(lax.ppermute(outgoing, axis, route))
    stacked = jnp.stack(got)
    order = (index - jnp.arange(count, dtype=jnp.int32)) % count
    stacked = jnp.take(stacked, order, axis=0)
    return stacked.reshape((count * block.shape[0],) + block.shape[2:])


def cholesky_inverse_kernel(gram_ref, inverse_ref, work_ref, rest_ref):
    order = gram_ref.shape[0]
    sub = lax.broadcasted_iota(jnp.int32, (order, order), 0)
    lane = lax.broadcasted_iota(jnp.int32, (order, order), 1)
    sub_one = lax.broadcasted_iota(jnp.int32, (order, 1), 0)
    lane_one = lax.broadcasted_iota(jnp.int32, (1, order), 1)
    work_ref[...] = gram_ref[...]
    rest_ref[...] = jnp.where(sub == lane, 1.0, 0.0).astype(jnp.float32)

    def step(j, carry):
        work = work_ref[...]
        column = jnp.sum(jnp.where(lane == j, work, 0.0), axis=1, keepdims=True)
        pivot = jnp.sum(jnp.where(sub_one == j, column, 0.0), axis=0, keepdims=True)
        scale = 1.0 / jnp.sqrt(pivot)
        column = jnp.where(sub_one >= j, column * scale, 0.0)
        row = jnp.where(lane_one >= j, work_ref[pl.ds(j, 1), :] * scale, 0.0)
        work_ref[...] = work - column * row
        solved = rest_ref[pl.ds(j, 1), :] * scale
        inverse_ref[pl.ds(j, 1), :] = solved
        rest_ref[...] = rest_ref[...] - column * solved
        return carry

    lax.fori_loop(0, order, step, 0)


def cholesky_inverse(gram_matrix):
    order = gram_matrix.shape[0]
    symmetric = (gram_matrix + gram_matrix.T) * 0.5
    return pl.pallas_call(
        cholesky_inverse_kernel,
        out_shape=jax.ShapeDtypeStruct((order, order), jnp.float32),
        scratch_shapes=[pltpu.VMEM((order, order), jnp.float32)] * 2,
    )(symmetric)


def basis_from_gram(sketched, gram_matrix, rank_limit):
    inverse = cholesky_inverse(gram_matrix)
    orthonormal = jnp.einsum("ra,ba->rb", sketched, inverse, precision=highest)
    columns = jnp.arange(sketched.shape[1], dtype=jnp.int32)
    return jnp.where(columns[None, :] < rank_limit, orthonormal, jnp.zeros_like(orthonormal))


def chol_basis(sketched, rank_limit):
    gram_matrix = jnp.einsum("ra,rb->ab", sketched, sketched, precision=highest)
    return basis_from_gram(sketched, gram_matrix, rank_limit)


def merge_level(own, partner, low_side, sketch_all, rank_limit):
    stacked = jnp.where(
        low_side,
        jnp.concatenate([own, partner], 1),
        jnp.concatenate([partner, own], 1),
    )
    sketched = jnp.einsum("pr,ps->rs", stacked, sketch_all, precision=highest)
    merged = chol_basis(sketched, rank_limit)
    return merged, jnp.dot(stacked, merged, precision=highest)


def on_device(
    child_updates,
    child_probes,
    child_dest,
    child_rows,
    parent_blocks,
    coupling,
    parent_probes,
    sketch,
    rank_one,
    rank_two,
    rank_three,
):
    leaf_count = lax.axis_size("leaf")
    probe_count = lax.axis_size("probe")
    leaf_index = lax.axis_index("leaf")
    probe_index = lax.axis_index("probe")
    local_probes = child_probes.shape[0]
    kid_count = child_updates.shape[0]
    kid_order = child_updates.shape[1]
    block_rows = child_rows.shape[1]
    block_count = child_rows.shape[0]
    front_rows = parent_probes.shape[1]
    rank_width = sketch.shape[1]

    updates = child_updates.reshape(kid_count, kid_order // block_rows, block_rows, kid_order)
    probe_cut = child_probes.reshape(local_probes, kid_count, kid_order)
    sampled = jnp.einsum("pck,cbik->cbpi", probe_cut, updates, preferred_element_type=jnp.float32)
    sampled = sampled.astype(jnp.bfloat16).reshape(block_count, local_probes, block_rows)

    targets = child_dest[:, 0]
    named = (targets[:, None] == jnp.arange(leaf_count, dtype=jnp.int32)[None, :]).astype(jnp.int32)
    earlier = jnp.cumsum(named, axis=0) - named
    slot = jnp.sum(earlier * named, axis=1)
    place = targets * SLOT_CAP + slot
    slot_count = leaf_count * SLOT_CAP
    source = jnp.full((slot_count,), block_count, jnp.int32).at[place].set(
        jnp.arange(block_count, dtype=jnp.int32)
    )
    filled = source < block_count
    source = jnp.minimum(source, block_count - 1)
    high = jnp.where(filled[:, None], child_rows[source] // block_rows, -1)
    low = jnp.where(filled[:, None], child_rows[source] % block_rows, 0)
    send_vals = jnp.where(filled[:, None, None], jnp.take(sampled, source, axis=0), jnp.bfloat16(0))
    half = SLOT_CAP
    info_rows = 16
    loads = []
    for part in range(1):
        picked_slots = slice(part * half, (part + 1) * half)
        vals = send_vals.reshape(leaf_count, SLOT_CAP, local_probes, block_rows)[:, picked_slots]
        info = jnp.concatenate(
            [
                high.reshape(leaf_count, SLOT_CAP, block_rows)[:, picked_slots],
                low.reshape(leaf_count, SLOT_CAP, block_rows)[:, picked_slots],
                jnp.zeros((leaf_count, info_rows - 2 * half, block_rows), jnp.int32),
            ],
            axis=1,
        ).astype(jnp.bfloat16)
        load = jnp.concatenate(
            [vals.reshape(leaf_count, half * local_probes, block_rows), info], axis=1
        )
        loads.append(lax.all_to_all(load, "leaf", 0, 0, tiled=True))

    pieces = parent_probes.reshape(local_probes, front_rows // block_rows, block_rows)
    picked = jnp.take(pieces, coupling[:, 1], axis=1)
    product = jnp.einsum("eik,pek->pei", parent_blocks, picked, preferred_element_type=jnp.float32)
    initial = (
        jnp.zeros(pieces.shape, jnp.float32)
        .at[:, coupling[:, 0]]
        .add(product)
        .reshape(local_probes, front_rows)
    )
    high_count = front_rows // block_rows
    spread = jnp.moveaxis(initial.reshape(local_probes, high_count, block_rows), 1, 0)
    spread = spread.reshape(high_count * local_probes, block_rows)
    for load in loads:
        counts = jnp.sum(load[:, half * local_probes, :1] >= 0, axis=1).astype(jnp.int32)
        spread = extend_add(load, counts, spread, half, local_probes)
    spread = spread.reshape(high_count, local_probes, block_rows)
    sample = jnp.moveaxis(spread, 0, 1).reshape(local_probes, front_rows)

    share_rows = front_rows // probe_count
    sketch_all = gather_rows(sketch, "probe")
    share_sample = exchange_shares(sample.reshape(local_probes, probe_count, share_rows), "probe")
    share_sketched = jnp.einsum("pr,ps->rs", share_sample, sketch_all, precision=highest)
    gram_one = ordered_sum(
        jnp.einsum("ra,rb->ab", share_sketched, share_sketched, precision=highest), "probe"
    )
    own_basis = basis_from_gram(share_sketched, gram_one, rank_one[0])
    passed_one = ordered_sum(jnp.dot(share_sample, own_basis, precision=highest), "probe")

    pair_bit = leaf_index % 2
    merged_two, passed_two = merge_level(
        passed_one, partner_2(passed_one, "leaf", 0), pair_bit == 0, sketch_all, rank_two[leaf_index // 2]
    )
    quad_bit = leaf_index // 2 % 2
    merged_three, passed_three = merge_level(
        passed_two, partner_2(passed_two, "leaf", 1), quad_bit == 0, sketch_all, rank_three[leaf_index // 4]
    )
    basis_two = lax.dynamic_slice_in_dim(merged_two, pair_bit * rank_width, rank_width, 0)
    basis_three = lax.dynamic_slice_in_dim(merged_three, quad_bit * rank_width, rank_width, 0)
    top = lax.dynamic_slice_in_dim(passed_three, probe_index * local_probes, local_probes, 0)
    return (own_basis, basis_two, basis_three, top)


def solution(mesh):
    return jax.shard_map(
        on_device,
        mesh=mesh,
        in_specs=(
            P("leaf", None, None),
            P("probe", "leaf"),
            P("leaf", None),
            P("leaf", None),
            P("leaf", None, None),
            P("leaf", None),
            P("probe", "leaf"),
            P("probe", None),
            P("leaf"),
            P(),
            P(),
        ),
        out_specs=(
            P(("leaf", "probe"), None),
            P("leaf", None),
            P("leaf", None),
            P("probe", "leaf"),
        ),
        check_vma=False,
    )
```

profile of v0, /device:TPU:1, one launch (start us, length us, event | category | flops | bytes accessed | tf_op | source)
XLA Modules:
  0.0 237.9 jit_solution(13292604072510744806)
XLA Ops:
  4.7 1.6 gather_fusion.1
  6.6 2.4 copy.47
  9.0 10.1 %fusion.3 = bf16[32,4,128,64]{2,3,1,0:T(8,128)(2,1)} fusion(bf16[32,4,128,512]{3,2,1,0:T(8,128)(2,1)} %bitcast.182, bf16[64,32,512,1]{2,1,0,3:T(8,128)(2,1)S(1)} %bitcast.155), kind=kOutput, calls=%fused_computation.14 | convolution fusion | flops 1074790400 | bytes 20971520 | tf_op jit(solution)/shard_map/pck,cbik->cbpi/dot_general | solution.py:205
  19.1 4.6 %gather_fusion = bf16[256,64,128]{2,1,0:T(8,128)(2,1)} fusion(bf16[128,64,128]{2,1,0:T(8,128)(2,1)} %bitcast.153, s32[1024]{0:T(1024)S(1)} %pad_clamp_fusion.2), kind=kCustom, calls=%fused_computation | custom fusion | bytes 8389632 | tf_op jit(solution)/shard_map/jit(_take)/gather | solution.py:221
  23.7 6.9 %fusion = bf16[32,512,128]{2,1,0:T(8,128)(2,1)S(1)} fusion(pred[32,512]{1,0:T(8,128)(4,1)S(1)} %broadcast_in_dim.173, pred[32,512]{1,0:T(8,128)(4,1)S(1)} %broadcast_in_dim.169, bf16[32,512,128]{2,1,0:T(8,128)(2,1)} %bitcast.152), kind=kLoop, calls=%fused_computation.11 | loop fusion | flops 4194304 | bytes 8421376 | tf_op jit(solution)/shard_map/jit(_where)/select_n | solution.py:221
  30.6 2.2 pad_maximum_fusion
  32.9 8.8 %all-to-all-start = ((bf16[32,528,128]{2,1,0:T(8,128)(2,1)}), bf16[32,528,128]{2,1,0:T(8,128)(2,1)}, u32[]{:S(2)}, u32[]{:S(2)}) async-start(bf16[32,528,128]{2,1,0:T(8,128)(2,1)} %pad_maximum_fusion), calls=%async_computation | async-start | bytes 8650752 | tf_op jit(solution)/shard_map/all_to_all | solution.py:239
  41.7 3.8 %collective-permute-start.5 = (f32[64,128]{1,0:T(8,128)S(1)}, f32[64,128]{1,0:T(8,128)S(1)}, u32[]{:S(2)}, u32[]{:S(2)}) collective-permute-start(f32[64,128]{1,0:T(8,128)S(1)} %copy-done.4), channel_id=1, source_target_pairs={{0,3},{1,0},{2,1},{3,2},{4,7},{5,4},{6,5},{7,6},{8,11},{9,8},{10,9... | collective-permute-start | bytes 98312 | tf_op jit(solution)/shard_map/ppermute | solution.py:49
  47.8 2.9 %fusion.6 = f32[64,64,128]{2,1,0:T(8,128)} fusion(bf16[64,128,128]{2,1,0:T(8,128)(2,1)S(1)} %copy-done, bf16[64,64,128]{2,1,0:T(8,128)(2,1)S(1)} %gather_fusion.2, pred[64]{0:T(512)(128)(4,1)S(1)} %and_bitcast_fusion), kind=kOutput, calls=%fused_computation.19 | convolution fusion | flops 134742016 | bytes 5242944 | tf_op jit(solution)/shard_map/eik,pek->pei/dot_general | solution.py:243
  51.5 7.0 %scatter_fusion = f32[64,16,128]{2,0,1:T(8,128)S(1)} fusion(f32[64,16,128]{2,0,1:T(8,128)S(1)} %broadcast_in_dim.179, s32[64]{0:T(128)S(1)} %get-tuple-element.23, f32[64,64,128]{2,1,0:T(8,128)} %fusion.6), kind=kCustom, calls=%fused_computation.8 | custom fusion | flops 524288 | bytes 6291712 | tf_op jit(solution)/shard_map/scatter-add | solution.py:247
  59.1 36.2 %all-to-all-done.load_ref = bf16[32,528,128]{2,1,0:T(8,128)(2,1)} async-done(((bf16[32,528,128]{2,1,0:T(8,128)(2,1)}), bf16[32,528,128]{2,1,0:T(8,128)(2,1)}, u32[]{:S(2)}, u32[]{:S(2)}) %all-to-all-start) | async-done | bytes 4325408 | tf_op jit(solution)/shard_map/all_to_all | solution.py:239
  95.3 2.0 fusion.40.count_ref
  97.3 28.9 %shard_map.138 = f32[1024,128]{1,0:T(8,128)} custom-call(s32[32]{0:T(128)} %fusion.40.count_ref, bf16[32,528,128]{2,1,0:T(8,128)(2,1)} %all-to-all-done.load_ref, f32[1024,128]{1,0:T(8,128)} %bitcast.151), custom_call_target="tpu_custom_call" | custom-call | tf_op jit(solution)/shard_map/pallas_call | solution.py:90
  126.2 1.3 copy.64
  128.3 4.0 %collective-permute-start.2 = (f32[64,512]{1,0:T(8,128)S(1)}, f32[64,512]{1,0:T(8,128)S(1)}, u32[]{:S(2)}, u32[]{:S(2)}) collective-permute-start(f32[64,512]{1,0:T(8,128)S(1)} %bitcast.166), channel_id=1, source_target_pairs={{0,3},{1,0},{2,1},{3,2},{4,7},{5,4},{6,5},{7,6},{8,11},{9,8},{10,9... | collective-permute-start | bytes 393224 | tf_op jit(solution)/shard_map/ppermute | solution.py:113
  133.2 4.6 %collective-permute-done.2 = f32[64,512]{1,0:T(8,128)S(1)} collective-permute-done((f32[64,512]{1,0:T(8,128)S(1)}, f32[64,512]{1,0:T(8,128)S(1)}, u32[]{:S(2)}, u32[]{:S(2)}) %collective-permute-start.2) | collective-permute-done | bytes 131104 | tf_op jit(solution)/shard_map/ppermute | solution.py:113
  137.8 3.9 %collective-permute-done = f32[64,512]{1,0:T(8,128)S(1)} collective-permute-done((f32[64,512]{1,0:T(8,128)S(1)}, f32[64,512]{1,0:T(8,128)S(1)}, u32[]{:S(2)}, u32[]{:S(2)}) %collective-permute-start) | collective-permute-done | bytes 131104 | tf_op jit(solution)/shard_map/ppermute | solution.py:113
  144.2 1.4 collective-permute-start.6
  145.7 1.5 collective-permute-done.8
  147.2 1.6 collective-permute-done.7
  152.9 18.4 %shard_map.139 = f32[128,128]{1,0:T(8,128)} custom-call(f32[128,128]{1,0:T(8,128)} %fusion.34.gram_ref), custom_call_target="tpu_custom_call" | custom-call | tf_op jit(solution)/shard_map/pallas_call | solution.py:148
  171.3 1.2 convolution_select_fusion
  173.2 2.3 collective-permute-start.11
  176.2 1.2 dynamic_slice.15
  177.4 1.2 dynamic_slice.17
  179.6 1.4 collective-permute-done.10
  181.0 1.6 collective-permute-done.9
  183.4 3.0 %collective-permute-start.12 = (f32[256,128]{1,0:T(8,128)S(1)}, f32[256,128]{1,0:T(8,128)S(1)}, u32[]{:S(2)}, u32[]{:S(2)}) collective-permute-start(f32[256,128]{1,0:T(8,128)S(1)} %fusion.22), channel_id=1, source_target_pairs={{0,4},{4,0},{8,12},{12,8},{16,20},{20,16},{24,28},{28,24},{32,36},... | collective-permute-start | bytes 393224 | tf_op jit(solution)/shard_map/ppermute | solution.py:22
  189.1 18.4 %shard_map.140 = f32[128,128]{1,0:T(8,128)} custom-call(f32[128,128]{1,0:T(8,128)} %fusion.36.gram_ref), custom_call_target="tpu_custom_call" | custom-call | tf_op jit(solution)/shard_map/pallas_call | solution.py:148
  209.1 2.3 collective-permute-start.13
  212.7 2.3 collective-permute-done.13
  216.5 18.4 %shard_map.141 = f32[128,128]{1,0:T(8,128)} custom-call(f32[128,128]{1,0:T(8,128)} %fusion.35.gram_ref), custom_call_target="tpu_custom_call" | custom-call | tf_op jit(solution)/shard_map/pallas_call | solution.py:148
  (100 shorter events, 28.2 us)
Async XLA Ops:
  0.6 47.2 %copy-start = (bf16[64,128,128]{2,1,0:T(8,128)(2,1)S(1)}, bf16[64,128,128]{2,1,0:T(8,128)(2,1)}, u32[]{:S(2)}) copy-start(bf16[64,128,128]{2,1,0:T(8,128)(2,1)} %param.17) | copy-start | bytes 6291460
  32.9 8.8 %copy-start.4 = (f32[64,128]{1,0:T(8,128)S(1)}, f32[64,128]{1,0:T(8,128)}, u32[]{:S(2)}) copy-start(f32[64,128]{1,0:T(8,128)} %param.20) | copy-start | bytes 98308
  32.9 14.0 %copy-start.5 = (s32[64,2]{0,1:T(2,128)S(1)}, s32[64,2]{0,1:T(2,128)}, u32[]{:S(2)}) copy-start(s32[64,2]{0,1:T(2,128)} %param.18) | copy-start | bytes 1540
  32.9 14.0 %copy-start.3 = (bf16[64,2048]{1,0:T(8,128)(2,1)S(1)}, bf16[64,2048]{1,0:T(8,128)(2,1)}, u32[]{:S(2)}) copy-start(bf16[64,2048]{1,0:T(8,128)(2,1)} %param.19) | copy-start | bytes 786436
  32.9 62.4 %all-to-all-start = ((bf16[32,528,128]{2,1,0:T(8,128)(2,1)}), bf16[32,528,128]{2,1,0:T(8,128)(2,1)}, u32[]{:S(2)}, u32[]{:S(2)}) async-start(bf16[32,528,128]{2,1,0:T(8,128)(2,1)} %pad_maximum_fusion), calls=%async_computation | async-start | bytes 8650752 | tf_op jit(solution)/shard_map/all_to_all | solution.py:239
  41.7 16.8 %collective-permute-start.5 = (f32[64,128]{1,0:T(8,128)S(1)}, f32[64,128]{1,0:T(8,128)S(1)}, u32[]{:S(2)}, u32[]{:S(2)}) collective-permute-start(f32[64,128]{1,0:T(8,128)S(1)} %copy-done.4), channel_id=1, source_target_pairs={{0,3},{1,0},{2,1},{3,2},{4,7},{5,4},{6,5},{7,6},{8,11},{9,8},{10,9... | collective-permute-start | bytes 98312 | tf_op jit(solution)/shard_map/ppermute | solution.py:49
  45.5 13.0 %collective-permute-start.4 = (f32[64,128]{1,0:T(8,128)S(1)}, f32[64,128]{1,0:T(8,128)S(1)}, u32[]{:S(2)}, u32[]{:S(2)}) collective-permute-start(f32[64,128]{1,0:T(8,128)S(1)} %copy-done.4), channel_id=1, source_target_pairs={{0,2},{1,3},{2,0},{3,1},{4,6},{5,7},{6,4},{7,5},{8,10},{9,11},{10,... | collective-permute-start | bytes 98312 | tf_op jit(solution)/shard_map/ppermute | solution.py:49
  45.5 13.0 %collective-permute-start.3 = (f32[64,128]{1,0:T(8,128)S(1)}, f32[64,128]{1,0:T(8,128)S(1)}, u32[]{:S(2)}, u32[]{:S(2)}) collective-permute-start(f32[64,128]{1,0:T(8,128)S(1)} %copy-done.4), channel_id=1, source_target_pairs={{0,1},{1,2},{2,3},{3,0},{4,5},{5,6},{6,7},{7,4},{8,9},{9,10},{10,1... | collective-permute-start | bytes 98312 | tf_op jit(solution)/shard_map/ppermute | solution.py:49
  58.5 38.8 %copy-start.1 = (f32[64,16,128]{2,0,1:T(8,128)}, f32[64,16,128]{2,0,1:T(8,128)S(1)}, u32[]{:S(2)}) copy-start(f32[64,16,128]{2,0,1:T(8,128)S(1)} %scatter_fusion) | copy-start | bytes 1572868
  128.3 9.5 %collective-permute-start.2 = (f32[64,512]{1,0:T(8,128)S(1)}, f32[64,512]{1,0:T(8,128)S(1)}, u32[]{:S(2)}, u32[]{:S(2)}) collective-permute-start(f32[64,512]{1,0:T(8,128)S(1)} %bitcast.166), channel_id=1, source_target_pairs={{0,3},{1,0},{2,1},{3,2},{4,7},{5,4},{6,5},{7,6},{8,11},{9,8},{10,9... | collective-permute-start | bytes 393224 | tf_op jit(solution)/shard_map/ppermute | solution.py:113
  132.3 39.0 %copy-start.6 = (pred[128]{0:T(512)(128)(4,1)S(1)}, pred[128]{0:T(512)(128)(4,1)}, u32[]{:S(2)}) copy-start(pred[128]{0:T(512)(128)(4,1)} %iota_compare_fusion.3) | copy-start | bytes 388
  132.3 5.5 %collective-permute-start.1 = (f32[64,512]{1,0:T(8,128)S(1)}, f32[64,512]{1,0:T(8,128)S(1)}, u32[]{:S(2)}, u32[]{:S(2)}) collective-permute-start(f32[64,512]{1,0:T(8,128)S(1)} %fusion.23), channel_id=1, source_target_pairs={{0,2},{1,3},{2,0},{3,1},{4,6},{5,7},{6,4},{7,5},{8,10},{9,11},{10,... | collective-permute-start | bytes 393224 | tf_op jit(solution)/shard_map/ppermute | solution.py:113
  132.4 9.3 %collective-permute-start = (f32[64,512]{1,0:T(8,128)S(1)}, f32[64,512]{1,0:T(8,128)S(1)}, u32[]{:S(2)}, u32[]{:S(2)}) collective-permute-start(f32[64,512]{1,0:T(8,128)S(1)} %fusion.24), channel_id=1, source_target_pairs={{0,1},{1,2},{2,3},{3,0},{4,5},{5,6},{6,7},{7,4},{8,9},{9,10},{10,1... | collective-permute-start | bytes 393224 | tf_op jit(solution)/shard_map/ppermute | solution.py:113
  144.0 3.2 %collective-permute-start.8 = (f32[1,128,128]{2,1,0:T(8,128)S(1)}, f32[1,128,128]{2,1,0:T(8,128)S(1)}, u32[]{:S(2)}, u32[]{:S(2)}) collective-permute-start(f32[1,128,128]{2,1,0:T(8,128)S(1)} %bitcast.162), channel_id=1, source_target_pairs={{0,3},{1,0},{2,1},{3,2},{4,7},{5,4},{6,5},{7,6},{8,11},{9,8},{10,9... | collective-permute-start | bytes 196616 | tf_op jit(solution)/shard_map/ppermute | solution.py:49
  144.1 4.7 %collective-permute-start.7 = (f32[1,128,128]{2,1,0:T(8,128)S(1)}, f32[1,128,128]{2,1,0:T(8,128)S(1)}, u32[]{:S(2)}, u32[]{:S(2)}) collective-permute-start(f32[1,128,128]{2,1,0:T(8,128)S(1)} %bitcast.163), channel_id=1, source_target_pairs={{0,2},{1,3},{2,0},{3,1},{4,6},{5,7},{6,4},{7,5},{8,10},{9,11},{10,... | collective-permute-start | bytes 196616 | tf_op jit(solution)/shard_map/ppermute | solution.py:49
  144.2 5.4 %collective-permute-start.6 = (f32[1,128,128]{2,1,0:T(8,128)S(1)}, f32[1,128,128]{2,1,0:T(8,128)S(1)}, u32[]{:S(2)}, u32[]{:S(2)}) collective-permute-start(f32[1,128,128]{2,1,0:T(8,128)S(1)} %bitcast.164), channel_id=1, source_target_pairs={{0,1},{1,2},{2,3},{3,0},{4,5},{5,6},{6,7},{7,4},{8,9},{9,10},{10,1... | collective-permute-start | bytes 196616 | tf_op jit(solution)/shard_map/ppermute | solution.py:49
  172.5 0.7 copy-start.2
  173.2 6.3 %collective-permute-start.11 = (f32[1,256,128]{2,1,0:T(8,128)S(1)}, f32[1,256,128]{2,1,0:T(8,128)S(1)}, u32[]{:S(2)}, u32[]{:S(2)}) collective-permute-start(f32[1,256,128]{2,1,0:T(8,128)S(1)} %bitcast.158), channel_id=1, source_target_pairs={{0,3},{1,0},{2,1},{3,2},{4,7},{5,4},{6,5},{7,6},{8,11},{9,8},{10,9... | collective-permute-start | bytes 393224 | tf_op jit(solution)/shard_map/ppermute | solution.py:49
  175.6 5.4 %collective-permute-start.10 = (f32[1,256,128]{2,1,0:T(8,128)S(1)}, f32[1,256,128]{2,1,0:T(8,128)S(1)}, u32[]{:S(2)}, u32[]{:S(2)}) collective-permute-start(f32[1,256,128]{2,1,0:T(8,128)S(1)} %bitcast.159), channel_id=1, source_target_pairs={{0,2},{1,3},{2,0},{3,1},{4,6},{5,7},{6,4},{7,5},{8,10},{9,11},{10,... | collective-permute-start | bytes 393224 | tf_op jit(solution)/shard_map/ppermute | solution.py:49
  175.6 7.0 %collective-permute-start.9 = (f32[1,256,128]{2,1,0:T(8,128)S(1)}, f32[1,256,128]{2,1,0:T(8,128)S(1)}, u32[]{:S(2)}, u32[]{:S(2)}) collective-permute-start(f32[1,256,128]{2,1,0:T(8,128)S(1)} %bitcast.160), channel_id=1, source_target_pairs={{0,1},{1,2},{2,3},{3,0},{4,5},{5,6},{6,7},{7,4},{8,9},{9,10},{10,1... | collective-permute-start | bytes 393224 | tf_op jit(solution)/shard_map/ppermute | solution.py:49
  183.4 4.0 %collective-permute-start.12 = (f32[256,128]{1,0:T(8,128)S(1)}, f32[256,128]{1,0:T(8,128)S(1)}, u32[]{:S(2)}, u32[]{:S(2)}) collective-permute-start(f32[256,128]{1,0:T(8,128)S(1)} %fusion.22), channel_id=1, source_target_pairs={{0,4},{4,0},{8,12},{12,8},{16,20},{20,16},{24,28},{28,24},{32,36},... | collective-permute-start | bytes 393224 | tf_op jit(solution)/shard_map/ppermute | solution.py:22
  209.1 5.9 %collective-permute-start.13 = (f32[256,128]{0,1:T(8,128)S(1)}, f32[256,128]{0,1:T(8,128)S(1)}, u32[]{:S(2)}, u32[]{:S(2)}) collective-permute-start(f32[256,128]{0,1:T(8,128)S(1)} %fusion.16), channel_id=1, source_target_pairs={{0,8},{8,0},{4,12},{12,4},{16,24},{24,16},{20,28},{28,20},{32,40},... | collective-permute-start | bytes 393224 | tf_op jit(solution)/shard_map/ppermute | solution.py:22
where the time goes:
time: 239 us; the launch traced here: 238 us
  Pallas kernels  84.2 us (35%)
  waiting for transfers between devices  55.1 us (23%)
  starting transfers between devices  28 us (12%)
  other arithmetic  26.7 us (11%)
  matrix products  21.4 us (9%)
  local copies, waits for them, and re-layouts  20.6 us (9%)
    pallas_call x3, Pallas kernels, cholesky_inverse(): pl.pallas_call(cholesky_inverse_kernel, out_shape=jax.ShapeDtypeStruct((o...  55.3 us
    all_to_all x1, waiting for transfers between devices, on_device(): loads.append(lax.all_to_all(load, 'leaf', 0, 0, tiled=True))  36.2 us
    pallas_call x1, Pallas kernels, extend_add(): pl.pallas_call(kernel, grid_spec=pltpu.PrefetchScalarGridSpec(num_scalar_...  28.9 us
    dot_general x1, matrix products, on_device(): jnp.einsum('pck,cbik->cbpi', probe_cut, updates, preferred_element_type=j...  10.1 us
    ppermute x9, starting transfers between devices, gather_rows(): pieces.append(lax.ppermute(block, axis, route))  9.02 us
    all_to_all x1, starting transfers between devices, on_device(): loads.append(lax.all_to_all(load, 'leaf', 0, 0, tiled=True))  8.75 us
    ppermute x3, waiting for transfers between devices, exchange_shares(): got.append(lax.ppermute(outgoing, axis, route))  8.56 us
    ppermute x9, waiting for transfers between devices, gather_rows(): pieces.append(lax.ppermute(block, axis, route))  7.22 us
  transfers between devices with their start and end apart: 15, of which 11 were waited for; matrix products, arithmetic and copies ran while one was open for 7% of the time, Pallas kernels for 0%

commit v1 on v0

--- a/solution.py
+++ b/solution.py
@@ -119,27 +119,33 @@
 
 def cholesky_inverse_kernel(gram_ref, inverse_ref, work_ref, rest_ref):
     order = gram_ref.shape[0]
+    tile = 8
     sub = lax.broadcasted_iota(jnp.int32, (order, order), 0)
     lane = lax.broadcasted_iota(jnp.int32, (order, order), 1)
-    sub_one = lax.broadcasted_iota(jnp.int32, (order, 1), 0)
     lane_one = lax.broadcasted_iota(jnp.int32, (1, order), 1)
     work_ref[...] = gram_ref[...]
     rest_ref[...] = jnp.where(sub == lane, 1.0, 0.0).astype(jnp.float32)
-
-    def step(j, carry):
-        work = work_ref[...]
-        column = jnp.sum(jnp.where(lane == j, work, 0.0), axis=1, keepdims=True)
-        pivot = jnp.sum(jnp.where(sub_one == j, column, 0.0), axis=0, keepdims=True)
-        scale = 1.0 / jnp.sqrt(pivot)
-        column = jnp.where(sub_one >= j, column * scale, 0.0)
-        row = jnp.where(lane_one >= j, work_ref[pl.ds(j, 1), :] * scale, 0.0)
-        work_ref[...] = work - column * row
-        solved = rest_ref[pl.ds(j, 1), :] * scale
-        inverse_ref[pl.ds(j, 1), :] = solved
-        rest_ref[...] = rest_ref[...] - column * solved
-        return carry
-
-    lax.fori_loop(0, order, step, 0)
+    inverse_ref[...] = jnp.zeros_like(inverse_ref)
+
+    for first in range(0, order, tile):
+        height = order - first
+        tail_lane = lax.broadcasted_iota(jnp.int32, (height, order), 1)
+        tail_sub = lax.broadcasted_iota(jnp.int32, (height, 1), 0) + first
+
+        def step(j, carry, first=first, tail_lane=tail_lane, tail_sub=tail_sub):
+            work = work_ref[first:, :]
+            column = jnp.sum(jnp.where(tail_lane == j, work, 0.0), axis=1, keepdims=True)
+            pivot = jnp.sum(jnp.where(tail_sub == j, column, 0.0), axis=0, keepdims=True)
+            scale = 1.0 / jnp.sqrt(pivot)
+            column = jnp.where(tail_sub >= j, column * scale, 0.0)
+            row = jnp.where(lane_one >= j, work_ref[pl.ds(j, 1), :] * scale, 0.0)
+            work_ref[first:, :] = work - column * row
+            solved = rest_ref[pl.ds(j, 1), :] * scale
+            inverse_ref[pl.ds(j, 1), :] = solved
+            rest_ref[first:, :] = rest_ref[first:, :] - column * solved
+            return carry
+
+        lax.fori_loop(first, first + tile, step, 0)
 
 
 def cholesky_inverse(gram_matrix):

time: 239 us -> 234 us (0.979)
  Pallas kernels: 84.2 us -> 79.2 us
    pallas_call x3, Pallas kernels: 55.3 us -> 50.4 us  [cholesky_inverse(): pl.pallas_call(cholesky_inverse_kernel, out_shape=jax.ShapeDtypeStruct((o...]
where the time goes in v1:
time: 234 us; the launch traced here: 233 us
  Pallas kernels  79.2 us (34%)
  waiting for transfers between devices  55.1 us (24%)
  starting transfers between devices  27.9 us (12%)
  other arithmetic  26.7 us (11%)
  matrix products  21.4 us (9%)
  local copies, waits for them, and re-layouts  20.6 us (9%)
    pallas_call x3, Pallas kernels, cholesky_inverse(): pl.pallas_call(cholesky_inverse_kernel, out_shape=jax.ShapeDtypeStruct((o...  50.4 us
    all_to_all x1, waiting for transfers between devices, on_device(): loads.append(lax.all_to_all(load, 'leaf', 0, 0, tiled=True))  36.2 us
    pallas_call x1, Pallas kernels, extend_add(): pl.pallas_call(kernel, grid_spec=pltpu.PrefetchScalarGridSpec(num_scalar_...  28.9 us
    dot_general x1, matrix products, on_device(): jnp.einsum('pck,cbik->cbpi', probe_cut, updates, preferred_element_type=j...  10.1 us
    ppermute x9, starting transfers between devices, gather_rows(): pieces.append(lax.ppermute(block, axis, route))  9.01 us
    all_to_all x1, starting transfers between devices, on_device(): loads.append(lax.all_to_all(load, 'leaf', 0, 0, tiled=True))  8.75 us
    ppermute x3, waiting for transfers between devices, exchange_shares(): got.append(lax.ppermute(outgoing, axis, route))  8.55 us
    ppermute x9, waiting for transfers between devices, gather_rows(): pieces.append(lax.ppermute(block, axis, route))  7.23 us
  transfers between devices with their start and end apart: 15, of which 11 were waited for; matrix products, arithmetic and copies ran while one was open for 7% of the time, Pallas kernels for 0%

profile of v1, /device:TPU:1, one launch (start us, length us, event | category | flops | bytes accessed | tf_op | source)
XLA Modules:
  0.0 232.9 jit_solution(1540429789229581566)
XLA Ops:
  4.7 1.6 gather_fusion.1
  6.6 2.4 %copy.47 = bf16[8,8,32,512]{3,2,1,0:T(8,128)(2,1)S(1)} copy(bf16[8,8,32,512]{3,1,2,0:T(8,128)(2,1)} %bitcast.154) | data formatting | bytes 4194304
  9.0 10.1 %fusion.3 = bf16[32,4,128,64]{2,3,1,0:T(8,128)(2,1)} fusion(bf16[32,4,128,512]{3,2,1,0:T(8,128)(2,1)} %bitcast.182, bf16[64,32,512,1]{2,1,0,3:T(8,128)(2,1)S(1)} %bitcast.155), kind=kOutput, calls=%fused_computation.14 | convolution fusion | flops 1074790400 | bytes 20971520 | tf_op jit(solution)/shard_map/pck,cbik->cbpi/dot_general | solution.py:211
  19.1 4.6 %gather_fusion = bf16[256,64,128]{2,1,0:T(8,128)(2,1)} fusion(bf16[128,64,128]{2,1,0:T(8,128)(2,1)} %bitcast.153, s32[1024]{0:T(1024)S(1)} %pad_clamp_fusion.2), kind=kCustom, calls=%fused_computation | custom fusion | bytes 8389632 | tf_op jit(solution)/shard_map/jit(_take)/gather | solution.py:227
  23.7 6.9 %fusion = bf16[32,512,128]{2,1,0:T(8,128)(2,1)S(1)} fusion(pred[32,512]{1,0:T(8,128)(4,1)S(1)} %broadcast_in_dim.173, pred[32,512]{1,0:T(8,128)(4,1)S(1)} %broadcast_in_dim.169, bf16[32,512,128]{2,1,0:T(8,128)(2,1)} %bitcast.152), kind=kLoop, calls=%fused_computation.11 | loop fusion | flops 4194304 | bytes 8421376 | tf_op jit(solution)/shard_map/jit(_where)/select_n | solution.py:227
  30.6 2.2 pad_maximum_fusion
  32.9 8.8 %all-to-all-start = ((bf16[32,528,128]{2,1,0:T(8,128)(2,1)}), bf16[32,528,128]{2,1,0:T(8,128)(2,1)}, u32[]{:S(2)}, u32[]{:S(2)}) async-start(bf16[32,528,128]{2,1,0:T(8,128)(2,1)} %pad_maximum_fusion), calls=%async_computation | async-start | bytes 8650752 | tf_op jit(solution)/shard_map/all_to_all | solution.py:245
  41.7 3.8 %collective-permute-start.5 = (f32[64,128]{1,0:T(8,128)S(1)}, f32[64,128]{1,0:T(8,128)S(1)}, u32[]{:S(2)}, u32[]{:S(2)}) collective-permute-start(f32[64,128]{1,0:T(8,128)S(1)} %copy-done.4), channel_id=1, source_target_pairs={{0,3},{1,0},{2,1},{3,2},{4,7},{5,4},{6,5},{7,6},{8,11},{9,8},{10,9... | collective-permute-start | bytes 98312 | tf_op jit(solution)/shard_map/ppermute | solution.py:49
  47.8 2.9 %fusion.6 = f32[64,64,128]{2,1,0:T(8,128)} fusion(bf16[64,128,128]{2,1,0:T(8,128)(2,1)S(1)} %copy-done, bf16[64,64,128]{2,1,0:T(8,128)(2,1)S(1)} %gather_fusion.2, pred[64]{0:T(512)(128)(4,1)S(1)} %and_bitcast_fusion), kind=kOutput, calls=%fused_computation.19 | convolution fusion | flops 134742016 | bytes 5242944 | tf_op jit(solution)/shard_map/eik,pek->pei/dot_general | solution.py:249
  51.5 7.0 %scatter_fusion = f32[64,16,128]{2,0,1:T(8,128)S(1)} fusion(f32[64,16,128]{2,0,1:T(8,128)S(1)} %broadcast_in_dim.179, s32[64]{0:T(128)S(1)} %get-tuple-element.23, f32[64,64,128]{2,1,0:T(8,128)} %fusion.6), kind=kCustom, calls=%fused_computation.8 | custom fusion | flops 524288 | bytes 6291712 | tf_op jit(solution)/shard_map/scatter-add | solution.py:253
  59.1 36.2 %all-to-all-done.load_ref = bf16[32,528,128]{2,1,0:T(8,128)(2,1)} async-done(((bf16[32,528,128]{2,1,0:T(8,128)(2,1)}), bf16[32,528,128]{2,1,0:T(8,128)(2,1)}, u32[]{:S(2)}, u32[]{:S(2)}) %all-to-all-start) | async-done | bytes 4325408 | tf_op jit(solution)/shard_map/all_to_all | solution.py:245
  95.3 2.0 fusion.40.count_ref
  97.3 28.9 %shard_map.138 = f32[1024,128]{1,0:T(8,128)} custom-call(s32[32]{0:T(128)} %fusion.40.count_ref, bf16[32,528,128]{2,1,0:T(8,128)(2,1)} %all-to-all-done.load_ref, f32[1024,128]{1,0:T(8,128)} %bitcast.151), custom_call_target="tpu_custom_call" | custom-call | tf_op jit(solution)/shard_map/pallas_call | solution.py:90
  126.2 1.3 copy.64
  128.3 4.0 %collective-permute-start.2 = (f32[64,512]{1,0:T(8,128)S(1)}, f32[64,512]{1,0:T(8,128)S(1)}, u32[]{:S(2)}, u32[]{:S(2)}) collective-permute-start(f32[64,512]{1,0:T(8,128)S(1)} %bitcast.166), channel_id=1, source_target_pairs={{0,3},{1,0},{2,1},{3,2},{4,7},{5,4},{6,5},{7,6},{8,11},{9,8},{10,9... | collective-permute-start | bytes 393224 | tf_op jit(solution)/shard_map/ppermute | solution.py:113
  133.2 4.6 %collective-permute-done.2 = f32[64,512]{1,0:T(8,128)S(1)} collective-permute-done((f32[64,512]{1,0:T(8,128)S(1)}, f32[64,512]{1,0:T(8,128)S(1)}, u32[]{:S(2)}, u32[]{:S(2)}) %collective-permute-start.2) | collective-permute-done | bytes 131104 | tf_op jit(solution)/shard_map/ppermute | solution.py:113
  137.8 3.9 %collective-permute-done = f32[64,512]{1,0:T(8,128)S(1)} collective-permute-done((f32[64,512]{1,0:T(8,128)S(1)}, f32[64,512]{1,0:T(8,128)S(1)}, u32[]{:S(2)}, u32[]{:S(2)}) %collective-permute-start) | collective-permute-done | bytes 131104 | tf_op jit(solution)/shard_map/ppermute | solution.py:113
  144.2 1.4 collective-permute-start.6
  145.7 1.5 collective-permute-done.8
  147.2 1.6 collective-permute-done.7
  152.9 16.8 %shard_map.139 = f32[128,128]{1,0:T(8,128)} custom-call(f32[128,128]{1,0:T(8,128)} %fusion.34.gram_ref), custom_call_target="tpu_custom_call" | custom-call | tf_op jit(solution)/shard_map/pallas_call | solution.py:154
  169.7 1.2 convolution_select_fusion
  171.6 2.3 collective-permute-start.11
  174.6 1.2 dynamic_slice.15
  175.8 1.2 dynamic_slice.17
  177.9 1.4 collective-permute-done.10
  179.3 1.6 collective-permute-done.9
  181.7 3.0 %collective-permute-start.12 = (f32[256,128]{1,0:T(8,128)S(1)}, f32[256,128]{1,0:T(8,128)S(1)}, u32[]{:S(2)}, u32[]{:S(2)}) collective-permute-start(f32[256,128]{1,0:T(8,128)S(1)} %fusion.22), channel_id=1, source_target_pairs={{0,4},{4,0},{8,12},{12,8},{16,20},{20,16},{24,28},{28,24},{32,36},... | collective-permute-start | bytes 393224 | tf_op jit(solution)/shard_map/ppermute | solution.py:22
  187.5 16.8 %shard_map.140 = f32[128,128]{1,0:T(8,128)} custom-call(f32[128,128]{1,0:T(8,128)} %fusion.36.gram_ref), custom_call_target="tpu_custom_call" | custom-call | tf_op jit(solution)/shard_map/pallas_call | solution.py:154
  205.8 2.3 collective-permute-start.13
  209.4 2.3 collective-permute-done.13
  213.1 16.8 %shard_map.141 = f32[128,128]{1,0:T(8,128)} custom-call(f32[128,128]{1,0:T(8,128)} %fusion.35.gram_ref), custom_call_target="tpu_custom_call" | custom-call | tf_op jit(solution)/shard_map/pallas_call | solution.py:154
  (100 shorter events, 28.2 us)
Async XLA Ops:
  0.6 47.2 %copy-start = (bf16[64,128,128]{2,1,0:T(8,128)(2,1)S(1)}, bf16[64,128,128]{2,1,0:T(8,128)(2,1)}, u32[]{:S(2)}) copy-start(bf16[64,128,128]{2,1,0:T(8,128)(2,1)} %param.17) | copy-start | bytes 6291460
  32.9 8.8 %copy-start.4 = (f32[64,128]{1,0:T(8,128)S(1)}, f32[64,128]{1,0:T(8,128)}, u32[]{:S(2)}) copy-start(f32[64,128]{1,0:T(8,128)} %param.20) | copy-start | bytes 98308
  32.9 14.0 %copy-start.5 = (s32[64,2]{0,1:T(2,128)S(1)}, s32[64,2]{0,1:T(2,128)}, u32[]{:S(2)}) copy-start(s32[64,2]{0,1:T(2,128)} %param.18) | copy-start | bytes 1540
  32.9 14.0 %copy-start.3 = (bf16[64,2048]{1,0:T(8,128)(2,1)S(1)}, bf16[64,2048]{1,0:T(8,128)(2,1)}, u32[]{:S(2)}) copy-start(bf16[64,2048]{1,0:T(8,128)(2,1)} %param.19) | copy-start | bytes 786436
  32.9 62.4 %all-to-all-start = ((bf16[32,528,128]{2,1,0:T(8,128)(2,1)}), bf16[32,528,128]{2,1,0:T(8,128)(2,1)}, u32[]{:S(2)}, u32[]{:S(2)}) async-start(bf16[32,528,128]{2,1,0:T(8,128)(2,1)} %pad_maximum_fusion), calls=%async_computation | async-start | bytes 8650752 | tf_op jit(solution)/shard_map/all_to_all | solution.py:245
  41.7 16.8 %collective-permute-start.5 = (f32[64,128]{1,0:T(8,128)S(1)}, f32[64,128]{1,0:T(8,128)S(1)}, u32[]{:S(2)}, u32[]{:S(2)}) collective-permute-start(f32[64,128]{1,0:T(8,128)S(1)} %copy-done.4), channel_id=1, source_target_pairs={{0,3},{1,0},{2,1},{3,2},{4,7},{5,4},{6,5},{7,6},{8,11},{9,8},{10,9... | collective-permute-start | bytes 98312 | tf_op jit(solution)/shard_map/ppermute | solution.py:49
  45.5 13.0 %collective-permute-start.4 = (f32[64,128]{1,0:T(8,128)S(1)}, f32[64,128]{1,0:T(8,128)S(1)}, u32[]{:S(2)}, u32[]{:S(2)}) collective-permute-start(f32[64,128]{1,0:T(8,128)S(1)} %copy-done.4), channel_id=1, source_target_pairs={{0,2},{1,3},{2,0},{3,1},{4,6},{5,7},{6,4},{7,5},{8,10},{9,11},{10,... | collective-permute-start | bytes 98312 | tf_op jit(solution)/shard_map/ppermute | solution.py:49
  45.5 13.0 %collective-permute-start.3 = (f32[64,128]{1,0:T(8,128)S(1)}, f32[64,128]{1,0:T(8,128)S(1)}, u32[]{:S(2)}, u32[]{:S(2)}) collective-permute-start(f32[64,128]{1,0:T(8,128)S(1)} %copy-done.4), channel_id=1, source_target_pairs={{0,1},{1,2},{2,3},{3,0},{4,5},{5,6},{6,7},{7,4},{8,9},{9,10},{10,1... | collective-permute-start | bytes 98312 | tf_op jit(solution)/shard_map/ppermute | solution.py:49
  58.5 38.8 %copy-start.1 = (f32[64,16,128]{2,0,1:T(8,128)}, f32[64,16,128]{2,0,1:T(8,128)S(1)}, u32[]{:S(2)}) copy-start(f32[64,16,128]{2,0,1:T(8,128)S(1)} %scatter_fusion) | copy-start | bytes 1572868
  128.3 9.5 %collective-permute-start.2 = (f32[64,512]{1,0:T(8,128)S(1)}, f32[64,512]{1,0:T(8,128)S(1)}, u32[]{:S(2)}, u32[]{:S(2)}) collective-permute-start(f32[64,512]{1,0:T(8,128)S(1)} %bitcast.166), channel_id=1, source_target_pairs={{0,3},{1,0},{2,1},{3,2},{4,7},{5,4},{6,5},{7,6},{8,11},{9,8},{10,9... | collective-permute-start | bytes 393224 | tf_op jit(solution)/shard_map/ppermute | solution.py:113
  132.3 37.4 %copy-start.6 = (pred[128]{0:T(512)(128)(4,1)S(1)}, pred[128]{0:T(512)(128)(4,1)}, u32[]{:S(2)}) copy-start(pred[128]{0:T(512)(128)(4,1)} %iota_compare_fusion.3) | copy-start | bytes 388
  132.3 5.5 %collective-permute-start.1 = (f32[64,512]{1,0:T(8,128)S(1)}, f32[64,512]{1,0:T(8,128)S(1)}, u32[]{:S(2)}, u32[]{:S(2)}) collective-permute-start(f32[64,512]{1,0:T(8,128)S(1)} %fusion.23), channel_id=1, source_target_pairs={{0,2},{1,3},{2,0},{3,1},{4,6},{5,7},{6,4},{7,5},{8,10},{9,11},{10,... | collective-permute-start | bytes 393224 | tf_op jit(solution)/shard_map/ppermute | solution.py:113
  132.4 9.3 %collective-permute-start = (f32[64,512]{1,0:T(8,128)S(1)}, f32[64,512]{1,0:T(8,128)S(1)}, u32[]{:S(2)}, u32[]{:S(2)}) collective-permute-start(f32[64,512]{1,0:T(8,128)S(1)} %fusion.24), channel_id=1, source_target_pairs={{0,1},{1,2},{2,3},{3,0},{4,5},{5,6},{6,7},{7,4},{8,9},{9,10},{10,1... | collective-permute-start | bytes 393224 | tf_op jit(solution)/shard_map/ppermute | solution.py:113
  144.0 3.2 %collective-permute-start.8 = (f32[1,128,128]{2,1,0:T(8,128)S(1)}, f32[1,128,128]{2,1,0:T(8,128)S(1)}, u32[]{:S(2)}, u32[]{:S(2)}) collective-permute-start(f32[1,128,128]{2,1,0:T(8,128)S(1)} %bitcast.162), channel_id=1, source_target_pairs={{0,3},{1,0},{2,1},{3,2},{4,7},{5,4},{6,5},{7,6},{8,11},{9,8},{10,9... | collective-permute-start | bytes 196616 | tf_op jit(solution)/shard_map/ppermute | solution.py:49
  144.1 4.7 %collective-permute-start.7 = (f32[1,128,128]{2,1,0:T(8,128)S(1)}, f32[1,128,128]{2,1,0:T(8,128)S(1)}, u32[]{:S(2)}, u32[]{:S(2)}) collective-permute-start(f32[1,128,128]{2,1,0:T(8,128)S(1)} %bitcast.163), channel_id=1, source_target_pairs={{0,2},{1,3},{2,0},{3,1},{4,6},{5,7},{6,4},{7,5},{8,10},{9,11},{10,... | collective-permute-start | bytes 196616 | tf_op jit(solution)/shard_map/ppermute | solution.py:49
  144.2 5.4 %collective-permute-start.6 = (f32[1,128,128]{2,1,0:T(8,128)S(1)}, f32[1,128,128]{2,1,0:T(8,128)S(1)}, u32[]{:S(2)}, u32[]{:S(2)}) collective-permute-start(f32[1,128,128]{2,1,0:T(8,128)S(1)} %bitcast.164), channel_id=1, source_target_pairs={{0,1},{1,2},{2,3},{3,0},{4,5},{5,6},{6,7},{7,4},{8,9},{9,10},{10,1... | collective-permute-start | bytes 196616 | tf_op jit(solution)/shard_map/ppermute | solution.py:49
  170.9 0.7 copy-start.2
  171.6 6.3 %collective-permute-start.11 = (f32[1,256,128]{2,1,0:T(8,128)S(1)}, f32[1,256,128]{2,1,0:T(8,128)S(1)}, u32[]{:S(2)}, u32[]{:S(2)}) collective-permute-start(f32[1,256,128]{2,1,0:T(8,128)S(1)} %bitcast.158), channel_id=1, source_target_pairs={{0,3},{1,0},{2,1},{3,2},{4,7},{5,4},{6,5},{7,6},{8,11},{9,8},{10,9... | collective-permute-start | bytes 393224 | tf_op jit(solution)/shard_map/ppermute | solution.py:49
  173.9 5.4 %collective-permute-start.10 = (f32[1,256,128]{2,1,0:T(8,128)S(1)}, f32[1,256,128]{2,1,0:T(8,128)S(1)}, u32[]{:S(2)}, u32[]{:S(2)}) collective-permute-start(f32[1,256,128]{2,1,0:T(8,128)S(1)} %bitcast.159), channel_id=1, source_target_pairs={{0,2},{1,3},{2,0},{3,1},{4,6},{5,7},{6,4},{7,5},{8,10},{9,11},{10,... | collective-permute-start | bytes 393224 | tf_op jit(solution)/shard_map/ppermute | solution.py:49
  174.0 7.0 %collective-permute-start.9 = (f32[1,256,128]{2,1,0:T(8,128)S(1)}, f32[1,256,128]{2,1,0:T(8,128)S(1)}, u32[]{:S(2)}, u32[]{:S(2)}) collective-permute-start(f32[1,256,128]{2,1,0:T(8,128)S(1)} %bitcast.160), channel_id=1, source_target_pairs={{0,1},{1,2},{2,3},{3,0},{4,5},{5,6},{6,7},{7,4},{8,9},{9,10},{10,1... | collective-permute-start | bytes 393224 | tf_op jit(solution)/shard_map/ppermute | solution.py:49
  181.7 4.0 %collective-permute-start.12 = (f32[256,128]{1,0:T(8,128)S(1)}, f32[256,128]{1,0:T(8,128)S(1)}, u32[]{:S(2)}, u32[]{:S(2)}) collective-permute-start(f32[256,128]{1,0:T(8,128)S(1)} %fusion.22), channel_id=1, source_target_pairs={{0,4},{4,0},{8,12},{12,8},{16,20},{20,16},{24,28},{28,24},{32,36},... | collective-permute-start | bytes 393224 | tf_op jit(solution)/shard_map/ppermute | solution.py:22
  205.8 5.8 %collective-permute-start.13 = (f32[256,128]{0,1:T(8,128)S(1)}, f32[256,128]{0,1:T(8,128)S(1)}, u32[]{:S(2)}, u32[]{:S(2)}) collective-permute-start(f32[256,128]{0,1:T(8,128)S(1)} %fusion.16), channel_id=1, source_target_pairs={{0,8},{8,0},{4,12},{12,4},{16,24},{24,16},{20,28},{28,20},{32,40},... | collective-permute-start | bytes 393224 | tf_op jit(solution)/shard_map/ppermute | solution.py:22

commit v2 on v1

--- a/solution.py
+++ b/solution.py
@@ -134,11 +134,12 @@
 
         def step(j, carry, first=first, tail_lane=tail_lane, tail_sub=tail_sub):
             work = work_ref[first:, :]
+            pivot_row = work_ref[pl.ds(j, 1), :]
+            pivot = jnp.sum(jnp.where(lane_one == j, pivot_row, 0.0), axis=1, keepdims=True)
             column = jnp.sum(jnp.where(tail_lane == j, work, 0.0), axis=1, keepdims=True)
-            pivot = jnp.sum(jnp.where(tail_sub == j, column, 0.0), axis=0, keepdims=True)
-            scale = 1.0 / jnp.sqrt(pivot)
+            scale = lax.rsqrt(pivot)
             column = jnp.where(tail_sub >= j, column * scale, 0.0)
-            row = jnp.where(lane_one >= j, work_ref[pl.ds(j, 1), :] * scale, 0.0)
+            row = jnp.where(lane_one >= j, pivot_row * scale, 0.0)
             work_ref[first:, :] = work - column * row
             solved = rest_ref[pl.ds(j, 1), :] * scale
             inverse_ref[pl.ds(j, 1), :] = solved

time: 234 us -> 226 us (0.966)
  Pallas kernels: 79.2 us -> 70.8 us
    pallas_call x3, Pallas kernels: 50.4 us -> 41.9 us  [cholesky_inverse(): pl.pallas_call(cholesky_inverse_kernel, out_shape=jax.ShapeDtypeStruct((o...]
where the time goes in v2:
time: 226 us; the launch traced here: 224 us
  Pallas kernels  70.8 us (31%)
  waiting for transfers between devices  55.1 us (24%)
  starting transfers between devices  28 us (12%)
  other arithmetic  26.7 us (12%)
  matrix products  21.4 us (9%)
  local copies, waits for them, and re-layouts  20.6 us (9%)
    pallas_call x3, Pallas kernels, cholesky_inverse(): pl.pallas_call(cholesky_inverse_kernel, out_shape=jax.ShapeDtypeStruct((o...  41.9 us
    all_to_all x1, waiting for transfers between devices, on_device(): loads.append(lax.all_to_all(load, 'leaf', 0, 0, tiled=True))  36.2 us
    pallas_call x1, Pallas kernels, extend_add(): pl.pallas_call(kernel, grid_spec=pltpu.PrefetchScalarGridSpec(num_scalar_...  28.9 us
    dot_general x1, matrix products, on_device(): jnp.einsum('pck,cbik->cbpi', probe_cut, updates, preferred_element_type=j...  10.1 us
    ppermute x9, starting transfers between devices, gather_rows(): pieces.append(lax.ppermute(block, axis, route))  9.01 us
    all_to_all x1, starting transfers between devices, on_device(): loads.append(lax.all_to_all(load, 'leaf', 0, 0, tiled=True))  8.76 us
    ppermute x3, waiting for transfers between devices, exchange_shares(): got.append(lax.ppermute(outgoing, axis, route))  8.54 us
    ppermute x9, waiting for transfers between devices, gather_rows(): pieces.append(lax.ppermute(block, axis, route))  7.22 us
  transfers between devices with their start and end apart: 15, of which 11 were waited for; matrix products, arithmetic and copies ran while one was open for 7% of the time, Pallas kernels for 0%

profile of v2, /device:TPU:1, one launch (start us, length us, event | category | flops | bytes accessed | tf_op | source)
XLA Modules:
  0.0 224.5 jit_solution(2498590337590066240)
XLA Ops:
  4.7 1.6 gather_fusion.1
  6.6 2.4 %copy.47 = bf16[8,8,32,512]{3,2,1,0:T(8,128)(2,1)S(1)} copy(bf16[8,8,32,512]{3,1,2,0:T(8,128)(2,1)} %bitcast.154) | data formatting | bytes 4194304
  9.0 10.1 %fusion.3 = bf16[32,4,128,64]{2,3,1,0:T(8,128)(2,1)} fusion(bf16[32,4,128,512]{3,2,1,0:T(8,128)(2,1)} %bitcast.182, bf16[64,32,512,1]{2,1,0,3:T(8,128)(2,1)S(1)} %bitcast.155), kind=kOutput, calls=%fused_computation.14 | convolution fusion | flops 1074790400 | bytes 20971520 | tf_op jit(solution)/shard_map/pck,cbik->cbpi/dot_general | solution.py:212
  19.1 4.6 %gather_fusion = bf16[256,64,128]{2,1,0:T(8,128)(2,1)} fusion(bf16[128,64,128]{2,1,0:T(8,128)(2,1)} %bitcast.153, s32[1024]{0:T(1024)S(1)} %pad_clamp_fusion.2), kind=kCustom, calls=%fused_computation | custom fusion | bytes 8389632 | tf_op jit(solution)/shard_map/jit(_take)/gather | solution.py:228
  23.7 6.9 %fusion = bf16[32,512,128]{2,1,0:T(8,128)(2,1)S(1)} fusion(pred[32,512]{1,0:T(8,128)(4,1)S(1)} %broadcast_in_dim.173, pred[32,512]{1,0:T(8,128)(4,1)S(1)} %broadcast_in_dim.169, bf16[32,512,128]{2,1,0:T(8,128)(2,1)} %bitcast.152), kind=kLoop, calls=%fused_computation.11 | loop fusion | flops 4194304 | bytes 8421376 | tf_op jit(solution)/shard_map/jit(_where)/select_n | solution.py:228
  30.6 2.2 %pad_maximum_fusion = bf16[32,528,128]{2,1,0:T(8,128)(2,1)} fusion(bf16[32,8,128]{2,1,0:T(8,128)(2,1)S(1)} %get-tuple-element.21, bf16[32,8,128]{2,1,0:T(8,128)(2,1)S(1)} %get-tuple-element.20, bf16[32,512,128]{2,1,0:T(8,128)(2,1)S(1)} %fusion), kind=kLoop, calls=%fused_computation.9 | loop fusion | flops 12976128 | bytes 8650752 | tf_op jit(solution)/shard_map/concatenate | solution.py:243
  32.9 8.8 %all-to-all-start = ((bf16[32,528,128]{2,1,0:T(8,128)(2,1)}), bf16[32,528,128]{2,1,0:T(8,128)(2,1)}, u32[]{:S(2)}, u32[]{:S(2)}) async-start(bf16[32,528,128]{2,1,0:T(8,128)(2,1)} %pad_maximum_fusion), calls=%async_computation | async-start | bytes 8650752 | tf_op jit(solution)/shard_map/all_to_all | solution.py:246
  41.7 3.8 %collective-permute-start.5 = (f32[64,128]{1,0:T(8,128)S(1)}, f32[64,128]{1,0:T(8,128)S(1)}, u32[]{:S(2)}, u32[]{:S(2)}) collective-permute-start(f32[64,128]{1,0:T(8,128)S(1)} %copy-done.4), channel_id=1, source_target_pairs={{0,3},{1,0},{2,1},{3,2},{4,7},{5,4},{6,5},{7,6},{8,11},{9,8},{10,9... | collective-permute-start | bytes 98312 | tf_op jit(solution)/shard_map/ppermute | solution.py:49
  47.8 2.9 %fusion.6 = f32[64,64,128]{2,1,0:T(8,128)} fusion(bf16[64,128,128]{2,1,0:T(8,128)(2,1)S(1)} %copy-done, bf16[64,64,128]{2,1,0:T(8,128)(2,1)S(1)} %gather_fusion.2, pred[64]{0:T(512)(128)(4,1)S(1)} %and_bitcast_fusion), kind=kOutput, calls=%fused_computation.19 | convolution fusion | flops 134742016 | bytes 5242944 | tf_op jit(solution)/shard_map/eik,pek->pei/dot_general | solution.py:250
  51.5 7.0 %scatter_fusion = f32[64,16,128]{2,0,1:T(8,128)S(1)} fusion(f32[64,16,128]{2,0,1:T(8,128)S(1)} %broadcast_in_dim.179, s32[64]{0:T(128)S(1)} %get-tuple-element.23, f32[64,64,128]{2,1,0:T(8,128)} %fusion.6), kind=kCustom, calls=%fused_computation.8 | custom fusion | flops 524288 | bytes 6291712 | tf_op jit(solution)/shard_map/scatter-add | solution.py:254
  59.1 36.2 %all-to-all-done.load_ref = bf16[32,528,128]{2,1,0:T(8,128)(2,1)} async-done(((bf16[32,528,128]{2,1,0:T(8,128)(2,1)}), bf16[32,528,128]{2,1,0:T(8,128)(2,1)}, u32[]{:S(2)}, u32[]{:S(2)}) %all-to-all-start) | async-done | bytes 4325408 | tf_op jit(solution)/shard_map/all_to_all | solution.py:246
  95.3 2.0 fusion.40.count_ref
  97.3 28.9 %shard_map.138 = f32[1024,128]{1,0:T(8,128)} custom-call(s32[32]{0:T(128)} %fusion.40.count_ref, bf16[32,528,128]{2,1,0:T(8,128)(2,1)} %all-to-all-done.load_ref, f32[1024,128]{1,0:T(8,128)} %bitcast.151), custom_call_target="tpu_custom_call" | custom-call | tf_op jit(solution)/shard_map/pallas_call | solution.py:90
  126.2 1.3 copy.64
  128.3 4.0 %collective-permute-start.2 = (f32[64,512]{1,0:T(8,128)S(1)}, f32[64,512]{1,0:T(8,128)S(1)}, u32[]{:S(2)}, u32[]{:S(2)}) collective-permute-start(f32[64,512]{1,0:T(8,128)S(1)} %bitcast.166), channel_id=1, source_target_pairs={{0,3},{1,0},{2,1},{3,2},{4,7},{5,4},{6,5},{7,6},{8,11},{9,8},{10,9... | collective-permute-start | bytes 393224 | tf_op jit(solution)/shard_map/ppermute | solution.py:113
  133.2 4.6 %collective-permute-done.2 = f32[64,512]{1,0:T(8,128)S(1)} collective-permute-done((f32[64,512]{1,0:T(8,128)S(1)}, f32[64,512]{1,0:T(8,128)S(1)}, u32[]{:S(2)}, u32[]{:S(2)}) %collective-permute-start.2) | collective-permute-done | bytes 131104 | tf_op jit(solution)/shard_map/ppermute | solution.py:113
  137.8 3.9 %collective-permute-done = f32[64,512]{1,0:T(8,128)S(1)} collective-permute-done((f32[64,512]{1,0:T(8,128)S(1)}, f32[64,512]{1,0:T(8,128)S(1)}, u32[]{:S(2)}, u32[]{:S(2)}) %collective-permute-start) | collective-permute-done | bytes 131104 | tf_op jit(solution)/shard_map/ppermute | solution.py:113
  144.2 1.4 collective-permute-start.6
  145.7 1.5 collective-permute-done.8
  147.2 1.6 collective-permute-done.7
  152.9 14.0 %shard_map.139 = f32[128,128]{1,0:T(8,128)} custom-call(f32[128,128]{1,0:T(8,128)} %fusion.34.gram_ref), custom_call_target="tpu_custom_call" | custom-call | tf_op jit(solution)/shard_map/pallas_call | solution.py:155
  166.8 1.2 convolution_select_fusion
  168.8 2.3 %collective-permute-start.11 = (f32[1,256,128]{2,1,0:T(8,128)S(1)}, f32[1,256,128]{2,1,0:T(8,128)S(1)}, u32[]{:S(2)}, u32[]{:S(2)}) collective-permute-start(f32[1,256,128]{2,1,0:T(8,128)S(1)} %bitcast.158), channel_id=1, source_target_pairs={{0,3},{1,0},{2,1},{3,2},{4,7},{5,4},{6,5},{7,6},{8,11},{9,8},{10,9... | collective-permute-start | bytes 393224 | tf_op jit(solution)/shard_map/ppermute | solution.py:49
  171.7 1.2 dynamic_slice.15
  173.0 1.2 dynamic_slice.17
  175.1 1.4 collective-permute-done.10
  176.5 1.6 collective-permute-done.9
  178.9 3.0 %collective-permute-start.12 = (f32[256,128]{1,0:T(8,128)S(1)}, f32[256,128]{1,0:T(8,128)S(1)}, u32[]{:S(2)}, u32[]{:S(2)}) collective-permute-start(f32[256,128]{1,0:T(8,128)S(1)} %fusion.22), channel_id=1, source_target_pairs={{0,4},{4,0},{8,12},{12,8},{16,20},{20,16},{24,28},{28,24},{32,36},... | collective-permute-start | bytes 393224 | tf_op jit(solution)/shard_map/ppermute | solution.py:22
  184.6 14.0 %shard_map.140 = f32[128,128]{1,0:T(8,128)} custom-call(f32[128,128]{1,0:T(8,128)} %fusion.36.gram_ref), custom_call_target="tpu_custom_call" | custom-call | tf_op jit(solution)/shard_map/pallas_call | solution.py:155
  200.1 2.4 %collective-permute-start.13 = (f32[256,128]{0,1:T(8,128)S(1)}, f32[256,128]{0,1:T(8,128)S(1)}, u32[]{:S(2)}, u32[]{:S(2)}) collective-permute-start(f32[256,128]{0,1:T(8,128)S(1)} %fusion.16), channel_id=1, source_target_pairs={{0,8},{8,0},{4,12},{12,4},{16,24},{24,16},{20,28},{28,20},{32,40},... | collective-permute-start | bytes 393224 | tf_op jit(solution)/shard_map/ppermute | solution.py:22
  203.7 2.3 %collective-permute-done.13 = f32[256,128]{0,1:T(8,128)S(1)} collective-permute-done((f32[256,128]{0,1:T(8,128)S(1)}, f32[256,128]{0,1:T(8,128)S(1)}, u32[]{:S(2)}, u32[]{:S(2)}) %collective-permute-start.13) | collective-permute-done | bytes 131104 | tf_op jit(solution)/shard_map/ppermute | solution.py:22
  207.5 14.0 %shard_map.141 = f32[128,128]{1,0:T(8,128)} custom-call(f32[128,128]{1,0:T(8,128)} %fusion.35.gram_ref), custom_call_target="tpu_custom_call" | custom-call | tf_op jit(solution)/shard_map/pallas_call | solution.py:155
  (100 shorter events, 28.2 us)
Async XLA Ops:
  0.6 47.2 %copy-start = (bf16[64,128,128]{2,1,0:T(8,128)(2,1)S(1)}, bf16[64,128,128]{2,1,0:T(8,128)(2,1)}, u32[]{:S(2)}) copy-start(bf16[64,128,128]{2,1,0:T(8,128)(2,1)} %param.17) | copy-start | bytes 6291460
  32.9 8.8 %copy-start.4 = (f32[64,128]{1,0:T(8,128)S(1)}, f32[64,128]{1,0:T(8,128)}, u32[]{:S(2)}) copy-start(f32[64,128]{1,0:T(8,128)} %param.20) | copy-start | bytes 98308
  32.9 14.0 %copy-start.5 = (s32[64,2]{0,1:T(2,128)S(1)}, s32[64,2]{0,1:T(2,128)}, u32[]{:S(2)}) copy-start(s32[64,2]{0,1:T(2,128)} %param.18) | copy-start | bytes 1540
  32.9 14.0 %copy-start.3 = (bf16[64,2048]{1,0:T(8,128)(2,1)S(1)}, bf16[64,2048]{1,0:T(8,128)(2,1)}, u32[]{:S(2)}) copy-start(bf16[64,2048]{1,0:T(8,128)(2,1)} %param.19) | copy-start | bytes 786436
  32.9 62.4 %all-to-all-start = ((bf16[32,528,128]{2,1,0:T(8,128)(2,1)}), bf16[32,528,128]{2,1,0:T(8,128)(2,1)}, u32[]{:S(2)}, u32[]{:S(2)}) async-start(bf16[32,528,128]{2,1,0:T(8,128)(2,1)} %pad_maximum_fusion), calls=%async_computation | async-start | bytes 8650752 | tf_op jit(solution)/shard_map/all_to_all | solution.py:246
  41.7 16.8 %collective-permute-start.5 = (f32[64,128]{1,0:T(8,128)S(1)}, f32[64,128]{1,0:T(8,128)S(1)}, u32[]{:S(2)}, u32[]{:S(2)}) collective-permute-start(f32[64,128]{1,0:T(8,128)S(1)} %copy-done.4), channel_id=1, source_target_pairs={{0,3},{1,0},{2,1},{3,2},{4,7},{5,4},{6,5},{7,6},{8,11},{9,8},{10,9... | collective-permute-start | bytes 98312 | tf_op jit(solution)/shard_map/ppermute | solution.py:49
  45.5 13.0 %collective-permute-start.4 = (f32[64,128]{1,0:T(8,128)S(1)}, f32[64,128]{1,0:T(8,128)S(1)}, u32[]{:S(2)}, u32[]{:S(2)}) collective-permute-start(f32[64,128]{1,0:T(8,128)S(1)} %copy-done.4), channel_id=1, source_target_pairs={{0,2},{1,3},{2,0},{3,1},{4,6},{5,7},{6,4},{7,5},{8,10},{9,11},{10,... | collective-permute-start | bytes 98312 | tf_op jit(solution)/shard_map/ppermute | solution.py:49
  45.5 13.0 %collective-permute-start.3 = (f32[64,128]{1,0:T(8,128)S(1)}, f32[64,128]{1,0:T(8,128)S(1)}, u32[]{:S(2)}, u32[]{:S(2)}) collective-permute-start(f32[64,128]{1,0:T(8,128)S(1)} %copy-done.4), channel_id=1, source_target_pairs={{0,1},{1,2},{2,3},{3,0},{4,5},{5,6},{6,7},{7,4},{8,9},{9,10},{10,1... | collective-permute-start | bytes 98312 | tf_op jit(solution)/shard_map/ppermute | solution.py:49
  58.5 38.8 %copy-start.1 = (f32[64,16,128]{2,0,1:T(8,128)}, f32[64,16,128]{2,0,1:T(8,128)S(1)}, u32[]{:S(2)}) copy-start(f32[64,16,128]{2,0,1:T(8,128)S(1)} %scatter_fusion) | copy-start | bytes 1572868
  128.3 9.5 %collective-permute-start.2 = (f32[64,512]{1,0:T(8,128)S(1)}, f32[64,512]{1,0:T(8,128)S(1)}, u32[]{:S(2)}, u32[]{:S(2)}) collective-permute-start(f32[64,512]{1,0:T(8,128)S(1)} %bitcast.166), channel_id=1, source_target_pairs={{0,3},{1,0},{2,1},{3,2},{4,7},{5,4},{6,5},{7,6},{8,11},{9,8},{10,9... | collective-permute-start | bytes 393224 | tf_op jit(solution)/shard_map/ppermute | solution.py:113
  132.3 34.5 %copy-start.6 = (pred[128]{0:T(512)(128)(4,1)S(1)}, pred[128]{0:T(512)(128)(4,1)}, u32[]{:S(2)}) copy-start(pred[128]{0:T(512)(128)(4,1)} %iota_compare_fusion.3) | copy-start | bytes 388
  132.3 5.5 %collective-permute-start.1 = (f32[64,512]{1,0:T(8,128)S(1)}, f32[64,512]{1,0:T(8,128)S(1)}, u32[]{:S(2)}, u32[]{:S(2)}) collective-permute-start(f32[64,512]{1,0:T(8,128)S(1)} %fusion.23), channel_id=1, source_target_pairs={{0,2},{1,3},{2,0},{3,1},{4,6},{5,7},{6,4},{7,5},{8,10},{9,11},{10,... | collective-permute-start | bytes 393224 | tf_op jit(solution)/shard_map/ppermute | solution.py:113
  132.4 9.3 %collective-permute-start = (f32[64,512]{1,0:T(8,128)S(1)}, f32[64,512]{1,0:T(8,128)S(1)}, u32[]{:S(2)}, u32[]{:S(2)}) collective-permute-start(f32[64,512]{1,0:T(8,128)S(1)} %fusion.24), channel_id=1, source_target_pairs={{0,1},{1,2},{2,3},{3,0},{4,5},{5,6},{6,7},{7,4},{8,9},{9,10},{10,1... | collective-permute-start | bytes 393224 | tf_op jit(solution)/shard_map/ppermute | solution.py:113
  144.0 3.2 %collective-permute-start.8 = (f32[1,128,128]{2,1,0:T(8,128)S(1)}, f32[1,128,128]{2,1,0:T(8,128)S(1)}, u32[]{:S(2)}, u32[]{:S(2)}) collective-permute-start(f32[1,128,128]{2,1,0:T(8,128)S(1)} %bitcast.162), channel_id=1, source_target_pairs={{0,3},{1,0},{2,1},{3,2},{4,7},{5,4},{6,5},{7,6},{8,11},{9,8},{10,9... | collective-permute-start | bytes 196616 | tf_op jit(solution)/shard_map/ppermute | solution.py:49
  144.1 4.7 %collective-permute-start.7 = (f32[1,128,128]{2,1,0:T(8,128)S(1)}, f32[1,128,128]{2,1,0:T(8,128)S(1)}, u32[]{:S(2)}, u32[]{:S(2)}) collective-permute-start(f32[1,128,128]{2,1,0:T(8,128)S(1)} %bitcast.163), channel_id=1, source_target_pairs={{0,2},{1,3},{2,0},{3,1},{4,6},{5,7},{6,4},{7,5},{8,10},{9,11},{10,... | collective-permute-start | bytes 196616 | tf_op jit(solution)/shard_map/ppermute | solution.py:49
  144.2 5.4 %collective-permute-start.6 = (f32[1,128,128]{2,1,0:T(8,128)S(1)}, f32[1,128,128]{2,1,0:T(8,128)S(1)}, u32[]{:S(2)}, u32[]{:S(2)}) collective-permute-start(f32[1,128,128]{2,1,0:T(8,128)S(1)} %bitcast.164), channel_id=1, source_target_pairs={{0,1},{1,2},{2,3},{3,0},{4,5},{5,6},{6,7},{7,4},{8,9},{9,10},{10,1... | collective-permute-start | bytes 196616 | tf_op jit(solution)/shard_map/ppermute | solution.py:49
  168.1 0.7 copy-start.2
  168.8 6.3 %collective-permute-start.11 = (f32[1,256,128]{2,1,0:T(8,128)S(1)}, f32[1,256,128]{2,1,0:T(8,128)S(1)}, u32[]{:S(2)}, u32[]{:S(2)}) collective-permute-start(f32[1,256,128]{2,1,0:T(8,128)S(1)} %bitcast.158), channel_id=1, source_target_pairs={{0,3},{1,0},{2,1},{3,2},{4,7},{5,4},{6,5},{7,6},{8,11},{9,8},{10,9... | collective-permute-start | bytes 393224 | tf_op jit(solution)/shard_map/ppermute | solution.py:49
  171.1 5.4 %collective-permute-start.10 = (f32[1,256,128]{2,1,0:T(8,128)S(1)}, f32[1,256,128]{2,1,0:T(8,128)S(1)}, u32[]{:S(2)}, u32[]{:S(2)}) collective-permute-start(f32[1,256,128]{2,1,0:T(8,128)S(1)} %bitcast.159), channel_id=1, source_target_pairs={{0,2},{1,3},{2,0},{3,1},{4,6},{5,7},{6,4},{7,5},{8,10},{9,11},{10,... | collective-permute-start | bytes 393224 | tf_op jit(solution)/shard_map/ppermute | solution.py:49
  171.1 7.0 %collective-permute-start.9 = (f32[1,256,128]{2,1,0:T(8,128)S(1)}, f32[1,256,128]{2,1,0:T(8,128)S(1)}, u32[]{:S(2)}, u32[]{:S(2)}) collective-permute-start(f32[1,256,128]{2,1,0:T(8,128)S(1)} %bitcast.160), channel_id=1, source_target_pairs={{0,1},{1,2},{2,3},{3,0},{4,5},{5,6},{6,7},{7,4},{8,9},{9,10},{10,1... | collective-permute-start | bytes 393224 | tf_op jit(solution)/shard_map/ppermute | solution.py:49
  178.9 4.0 %collective-permute-start.12 = (f32[256,128]{1,0:T(8,128)S(1)}, f32[256,128]{1,0:T(8,128)S(1)}, u32[]{:S(2)}, u32[]{:S(2)}) collective-permute-start(f32[256,128]{1,0:T(8,128)S(1)} %fusion.22), channel_id=1, source_target_pairs={{0,4},{4,0},{8,12},{12,8},{16,20},{20,16},{24,28},{28,24},{32,36},... | collective-permute-start | bytes 393224 | tf_op jit(solution)/shard_map/ppermute | solution.py:22
  200.1 5.9 %collective-permute-start.13 = (f32[256,128]{0,1:T(8,128)S(1)}, f32[256,128]{0,1:T(8,128)S(1)}, u32[]{:S(2)}, u32[]{:S(2)}) collective-permute-start(f32[256,128]{0,1:T(8,128)S(1)} %fusion.16), channel_id=1, source_target_pairs={{0,8},{8,0},{4,12},{12,4},{16,24},{24,16},{20,28},{28,20},{32,40},... | collective-permute-start | bytes 393224 | tf_op jit(solution)/shard_map/ppermute | solution.py:22

commit v3 on v2

--- a/solution.py
+++ b/solution.py
@@ -146,7 +146,7 @@
             rest_ref[first:, :] = rest_ref[first:, :] - column * solved
             return carry
 
-        lax.fori_loop(first, first + tile, step, 0)
+        lax.fori_loop(first, first + tile, step, 0, unroll=True)
 
 
 def cholesky_inverse(gram_matrix):

time: 226 us -> 224 us (level)
  no operation moved by 1% of the time
where the time goes in v3:
time: 224 us; the launch traced here: 223 us
  Pallas kernels  69 us (31%)
  waiting for transfers between devices  55.1 us (25%)
  starting transfers between devices  28.2 us (13%)
  other arithmetic  26.7 us (12%)
  matrix products  21.4 us (10%)
  local copies, waits for them, and re-layouts  20.6 us (9%)
    pallas_call x3, Pallas kernels, cholesky_inverse(): pl.pallas_call(cholesky_inverse_kernel, out_shape=jax.ShapeDtypeStruct((o...  40.1 us
    all_to_all x1, waiting for transfers between devices, on_device(): loads.append(lax.all_to_all(load, 'leaf', 0, 0, tiled=True))  36.2 us
    pallas_call x1, Pallas kernels, extend_add(): pl.pallas_call(kernel, grid_spec=pltpu.PrefetchScalarGridSpec(num_scalar_...  28.9 us
    dot_general x1, matrix products, on_device(): jnp.einsum('pck,cbik->cbpi', probe_cut, updates, preferred_element_type=j...  10.1 us
    ppermute x9, starting transfers between devices, gather_rows(): pieces.append(lax.ppermute(block, axis, route))  9.01 us
    all_to_all x1, starting transfers between devices, on_device(): loads.append(lax.all_to_all(load, 'leaf', 0, 0, tiled=True))  8.75 us
    ppermute x3, waiting for transfers between devices, exchange_shares(): got.append(lax.ppermute(outgoing, axis, route))  8.55 us
    ppermute x9, waiting for transfers between devices, gather_rows(): pieces.append(lax.ppermute(block, axis, route))  7.22 us
  transfers between devices with their start and end apart: 15, of which 11 were waited for; matrix products, arithmetic and copies ran while one was open for 7% of the time, Pallas kernels for 0%

profile of v3, /device:TPU:1, one launch (start us, length us, event | category | flops | bytes accessed | tf_op | source)
XLA Modules:
  0.0 222.9 jit_solution(16997162685048373150)
XLA Ops:
  4.7 1.6 gather_fusion.1
  6.6 2.4 %copy.47 = bf16[8,8,32,512]{3,2,1,0:T(8,128)(2,1)S(1)} copy(bf16[8,8,32,512]{3,1,2,0:T(8,128)(2,1)} %bitcast.154) | data formatting | bytes 4194304
  9.0 10.1 %fusion.3 = bf16[32,4,128,64]{2,3,1,0:T(8,128)(2,1)} fusion(bf16[32,4,128,512]{3,2,1,0:T(8,128)(2,1)} %bitcast.182, bf16[64,32,512,1]{2,1,0,3:T(8,128)(2,1)S(1)} %bitcast.155), kind=kOutput, calls=%fused_computation.14 | convolution fusion | flops 1074790400 | bytes 20971520 | tf_op jit(solution)/shard_map/pck,cbik->cbpi/dot_general | solution.py:212
  19.1 4.6 %gather_fusion = bf16[256,64,128]{2,1,0:T(8,128)(2,1)} fusion(bf16[128,64,128]{2,1,0:T(8,128)(2,1)} %bitcast.153, s32[1024]{0:T(1024)S(1)} %pad_clamp_fusion.2), kind=kCustom, calls=%fused_computation | custom fusion | bytes 8389632 | tf_op jit(solution)/shard_map/jit(_take)/gather | solution.py:228
  23.7 6.9 %fusion = bf16[32,512,128]{2,1,0:T(8,128)(2,1)S(1)} fusion(pred[32,512]{1,0:T(8,128)(4,1)S(1)} %broadcast_in_dim.173, pred[32,512]{1,0:T(8,128)(4,1)S(1)} %broadcast_in_dim.169, bf16[32,512,128]{2,1,0:T(8,128)(2,1)} %bitcast.152), kind=kLoop, calls=%fused_computation.11 | loop fusion | flops 4194304 | bytes 8421376 | tf_op jit(solution)/shard_map/jit(_where)/select_n | solution.py:228
  30.6 2.2 %pad_maximum_fusion = bf16[32,528,128]{2,1,0:T(8,128)(2,1)} fusion(bf16[32,8,128]{2,1,0:T(8,128)(2,1)S(1)} %get-tuple-element.21, bf16[32,8,128]{2,1,0:T(8,128)(2,1)S(1)} %get-tuple-element.20, bf16[32,512,128]{2,1,0:T(8,128)(2,1)S(1)} %fusion), kind=kLoop, calls=%fused_computation.9 | loop fusion | flops 12976128 | bytes 8650752 | tf_op jit(solution)/shard_map/concatenate | solution.py:243
  32.9 8.8 %all-to-all-start = ((bf16[32,528,128]{2,1,0:T(8,128)(2,1)}), bf16[32,528,128]{2,1,0:T(8,128)(2,1)}, u32[]{:S(2)}, u32[]{:S(2)}) async-start(bf16[32,528,128]{2,1,0:T(8,128)(2,1)} %pad_maximum_fusion), calls=%async_computation | async-start | bytes 8650752 | tf_op jit(solution)/shard_map/all_to_all | solution.py:246
  41.7 3.8 %collective-permute-start.5 = (f32[64,128]{1,0:T(8,128)S(1)}, f32[64,128]{1,0:T(8,128)S(1)}, u32[]{:S(2)}, u32[]{:S(2)}) collective-permute-start(f32[64,128]{1,0:T(8,128)S(1)} %copy-done.4), channel_id=1, source_target_pairs={{0,3},{1,0},{2,1},{3,2},{4,7},{5,4},{6,5},{7,6},{8,11},{9,8},{10,9... | collective-permute-start | bytes 98312 | tf_op jit(solution)/shard_map/ppermute | solution.py:49
  47.8 2.9 %fusion.6 = f32[64,64,128]{2,1,0:T(8,128)} fusion(bf16[64,128,128]{2,1,0:T(8,128)(2,1)S(1)} %copy-done, bf16[64,64,128]{2,1,0:T(8,128)(2,1)S(1)} %gather_fusion.2, pred[64]{0:T(512)(128)(4,1)S(1)} %and_bitcast_fusion), kind=kOutput, calls=%fused_computation.19 | convolution fusion | flops 134742016 | bytes 5242944 | tf_op jit(solution)/shard_map/eik,pek->pei/dot_general | solution.py:250
  51.5 7.0 %scatter_fusion = f32[64,16,128]{2,0,1:T(8,128)S(1)} fusion(f32[64,16,128]{2,0,1:T(8,128)S(1)} %broadcast_in_dim.179, s32[64]{0:T(128)S(1)} %get-tuple-element.23, f32[64,64,128]{2,1,0:T(8,128)} %fusion.6), kind=kCustom, calls=%fused_computation.8 | custom fusion | flops 524288 | bytes 6291712 | tf_op jit(solution)/shard_map/scatter-add | solution.py:254
  59.1 36.2 %all-to-all-done.load_ref = bf16[32,528,128]{2,1,0:T(8,128)(2,1)} async-done(((bf16[32,528,128]{2,1,0:T(8,128)(2,1)}), bf16[32,528,128]{2,1,0:T(8,128)(2,1)}, u32[]{:S(2)}, u32[]{:S(2)}) %all-to-all-start) | async-done | bytes 4325408 | tf_op jit(solution)/shard_map/all_to_all | solution.py:246
  95.3 2.0 fusion.40.count_ref
  97.3 28.9 %shard_map.138 = f32[1024,128]{1,0:T(8,128)} custom-call(s32[32]{0:T(128)} %fusion.40.count_ref, bf16[32,528,128]{2,1,0:T(8,128)(2,1)} %all-to-all-done.load_ref, f32[1024,128]{1,0:T(8,128)} %bitcast.151), custom_call_target="tpu_custom_call" | custom-call | tf_op jit(solution)/shard_map/pallas_call | solution.py:90
  126.2 1.3 copy.64
  128.3 4.0 %collective-permute-start.2 = (f32[64,512]{1,0:T(8,128)S(1)}, f32[64,512]{1,0:T(8,128)S(1)}, u32[]{:S(2)}, u32[]{:S(2)}) collective-permute-start(f32[64,512]{1,0:T(8,128)S(1)} %bitcast.166), channel_id=1, source_target_pairs={{0,3},{1,0},{2,1},{3,2},{4,7},{5,4},{6,5},{7,6},{8,11},{9,8},{10,9... | collective-permute-start | bytes 393224 | tf_op jit(solution)/shard_map/ppermute | solution.py:113
  133.2 4.6 %collective-permute-done.2 = f32[64,512]{1,0:T(8,128)S(1)} collective-permute-done((f32[64,512]{1,0:T(8,128)S(1)}, f32[64,512]{1,0:T(8,128)S(1)}, u32[]{:S(2)}, u32[]{:S(2)}) %collective-permute-start.2) | collective-permute-done | bytes 131104 | tf_op jit(solution)/shard_map/ppermute | solution.py:113
  137.8 3.9 %collective-permute-done = f32[64,512]{1,0:T(8,128)S(1)} collective-permute-done((f32[64,512]{1,0:T(8,128)S(1)}, f32[64,512]{1,0:T(8,128)S(1)}, u32[]{:S(2)}, u32[]{:S(2)}) %collective-permute-start) | collective-permute-done | bytes 131104 | tf_op jit(solution)/shard_map/ppermute | solution.py:113
  144.2 1.4 collective-permute-start.6
  145.7 1.5 collective-permute-done.8
  147.2 1.6 collective-permute-done.7
  152.9 13.4 %shard_map.139 = f32[128,128]{1,0:T(8,128)} custom-call(f32[128,128]{1,0:T(8,128)} %fusion.34.gram_ref), custom_call_target="tpu_custom_call" | custom-call | tf_op jit(solution)/shard_map/pallas_call | solution.py:155
  166.2 1.2 convolution_select_fusion
  168.2 2.3 %collective-permute-start.11 = (f32[1,256,128]{2,1,0:T(8,128)S(1)}, f32[1,256,128]{2,1,0:T(8,128)S(1)}, u32[]{:S(2)}, u32[]{:S(2)}) collective-permute-start(f32[1,256,128]{2,1,0:T(8,128)S(1)} %bitcast.158), channel_id=1, source_target_pairs={{0,3},{1,0},{2,1},{3,2},{4,7},{5,4},{6,5},{7,6},{8,11},{9,8},{10,9... | collective-permute-start | bytes 393224 | tf_op jit(solution)/shard_map/ppermute | solution.py:49
  171.1 1.2 dynamic_slice.15
  172.4 1.2 dynamic_slice.17
  174.5 1.4 collective-permute-done.10
  175.9 1.6 collective-permute-done.9
  178.3 3.2 %collective-permute-start.12 = (f32[256,128]{1,0:T(8,128)S(1)}, f32[256,128]{1,0:T(8,128)S(1)}, u32[]{:S(2)}, u32[]{:S(2)}) collective-permute-start(f32[256,128]{1,0:T(8,128)S(1)} %fusion.22), channel_id=1, source_target_pairs={{0,4},{4,0},{8,12},{12,8},{16,20},{20,16},{24,28},{28,24},{32,36},... | collective-permute-start | bytes 393224 | tf_op jit(solution)/shard_map/ppermute | solution.py:22
  184.3 13.4 %shard_map.140 = f32[128,128]{1,0:T(8,128)} custom-call(f32[128,128]{1,0:T(8,128)} %fusion.36.gram_ref), custom_call_target="tpu_custom_call" | custom-call | tf_op jit(solution)/shard_map/pallas_call | solution.py:155
  199.2 2.3 %collective-permute-start.13 = (f32[256,128]{0,1:T(8,128)S(1)}, f32[256,128]{0,1:T(8,128)S(1)}, u32[]{:S(2)}, u32[]{:S(2)}) collective-permute-start(f32[256,128]{0,1:T(8,128)S(1)} %fusion.16), channel_id=1, source_target_pairs={{0,8},{8,0},{4,12},{12,4},{16,24},{24,16},{20,28},{28,20},{32,40},... | collective-permute-start | bytes 393224 | tf_op jit(solution)/shard_map/ppermute | solution.py:22
  202.7 2.3 %collective-permute-done.13 = f32[256,128]{0,1:T(8,128)S(1)} collective-permute-done((f32[256,128]{0,1:T(8,128)S(1)}, f32[256,128]{0,1:T(8,128)S(1)}, u32[]{:S(2)}, u32[]{:S(2)}) %collective-permute-start.13) | collective-permute-done | bytes 131104 | tf_op jit(solution)/shard_map/ppermute | solution.py:22
  206.5 13.4 %shard_map.141 = f32[128,128]{1,0:T(8,128)} custom-call(f32[128,128]{1,0:T(8,128)} %fusion.35.gram_ref), custom_call_target="tpu_custom_call" | custom-call | tf_op jit(solution)/shard_map/pallas_call | solution.py:155
  (100 shorter events, 28.2 us)
Async XLA Ops:
  0.6 47.2 %copy-start = (bf16[64,128,128]{2,1,0:T(8,128)(2,1)S(1)}, bf16[64,128,128]{2,1,0:T(8,128)(2,1)}, u32[]{:S(2)}) copy-start(bf16[64,128,128]{2,1,0:T(8,128)(2,1)} %param.17) | copy-start | bytes 6291460
  32.9 8.8 %copy-start.4 = (f32[64,128]{1,0:T(8,128)S(1)}, f32[64,128]{1,0:T(8,128)}, u32[]{:S(2)}) copy-start(f32[64,128]{1,0:T(8,128)} %param.20) | copy-start | bytes 98308
  32.9 14.0 %copy-start.5 = (s32[64,2]{0,1:T(2,128)S(1)}, s32[64,2]{0,1:T(2,128)}, u32[]{:S(2)}) copy-start(s32[64,2]{0,1:T(2,128)} %param.18) | copy-start | bytes 1540
  32.9 14.0 %copy-start.3 = (bf16[64,2048]{1,0:T(8,128)(2,1)S(1)}, bf16[64,2048]{1,0:T(8,128)(2,1)}, u32[]{:S(2)}) copy-start(bf16[64,2048]{1,0:T(8,128)(2,1)} %param.19) | copy-start | bytes 786436
  32.9 62.4 %all-to-all-start = ((bf16[32,528,128]{2,1,0:T(8,128)(2,1)}), bf16[32,528,128]{2,1,0:T(8,128)(2,1)}, u32[]{:S(2)}, u32[]{:S(2)}) async-start(bf16[32,528,128]{2,1,0:T(8,128)(2,1)} %pad_maximum_fusion), calls=%async_computation | async-start | bytes 8650752 | tf_op jit(solution)/shard_map/all_to_all | solution.py:246
  41.7 16.8 %collective-permute-start.5 = (f32[64,128]{1,0:T(8,128)S(1)}, f32[64,128]{1,0:T(8,128)S(1)}, u32[]{:S(2)}, u32[]{:S(2)}) collective-permute-start(f32[64,128]{1,0:T(8,128)S(1)} %copy-done.4), channel_id=1, source_target_pairs={{0,3},{1,0},{2,1},{3,2},{4,7},{5,4},{6,5},{7,6},{8,11},{9,8},{10,9... | collective-permute-start | bytes 98312 | tf_op jit(solution)/shard_map/ppermute | solution.py:49
  45.5 13.0 %collective-permute-start.4 = (f32[64,128]{1,0:T(8,128)S(1)}, f32[64,128]{1,0:T(8,128)S(1)}, u32[]{:S(2)}, u32[]{:S(2)}) collective-permute-start(f32[64,128]{1,0:T(8,128)S(1)} %copy-done.4), channel_id=1, source_target_pairs={{0,2},{1,3},{2,0},{3,1},{4,6},{5,7},{6,4},{7,5},{8,10},{9,11},{10,... | collective-permute-start | bytes 98312 | tf_op jit(solution)/shard_map/ppermute | solution.py:49
  45.5 13.0 %collective-permute-start.3 = (f32[64,128]{1,0:T(8,128)S(1)}, f32[64,128]{1,0:T(8,128)S(1)}, u32[]{:S(2)}, u32[]{:S(2)}) collective-permute-start(f32[64,128]{1,0:T(8,128)S(1)} %copy-done.4), channel_id=1, source_target_pairs={{0,1},{1,2},{2,3},{3,0},{4,5},{5,6},{6,7},{7,4},{8,9},{9,10},{10,1... | collective-permute-start | bytes 98312 | tf_op jit(solution)/shard_map/ppermute | solution.py:49
  58.5 38.8 %copy-start.1 = (f32[64,16,128]{2,0,1:T(8,128)}, f32[64,16,128]{2,0,1:T(8,128)S(1)}, u32[]{:S(2)}) copy-start(f32[64,16,128]{2,0,1:T(8,128)S(1)} %scatter_fusion) | copy-start | bytes 1572868
  128.3 9.5 %collective-permute-start.2 = (f32[64,512]{1,0:T(8,128)S(1)}, f32[64,512]{1,0:T(8,128)S(1)}, u32[]{:S(2)}, u32[]{:S(2)}) collective-permute-start(f32[64,512]{1,0:T(8,128)S(1)} %bitcast.166), channel_id=1, source_target_pairs={{0,3},{1,0},{2,1},{3,2},{4,7},{5,4},{6,5},{7,6},{8,11},{9,8},{10,9... | collective-permute-start | bytes 393224 | tf_op jit(solution)/shard_map/ppermute | solution.py:113
  132.3 33.9 %copy-start.6 = (pred[128]{0:T(512)(128)(4,1)S(1)}, pred[128]{0:T(512)(128)(4,1)}, u32[]{:S(2)}) copy-start(pred[128]{0:T(512)(128)(4,1)} %iota_compare_fusion.3) | copy-start | bytes 388
  132.3 5.5 %collective-permute-start.1 = (f32[64,512]{1,0:T(8,128)S(1)}, f32[64,512]{1,0:T(8,128)S(1)}, u32[]{:S(2)}, u32[]{:S(2)}) collective-permute-start(f32[64,512]{1,0:T(8,128)S(1)} %fusion.23), channel_id=1, source_target_pairs={{0,2},{1,3},{2,0},{3,1},{4,6},{5,7},{6,4},{7,5},{8,10},{9,11},{10,... | collective-permute-start | bytes 393224 | tf_op jit(solution)/shard_map/ppermute | solution.py:113
  132.4 9.3 %collective-permute-start = (f32[64,512]{1,0:T(8,128)S(1)}, f32[64,512]{1,0:T(8,128)S(1)}, u32[]{:S(2)}, u32[]{:S(2)}) collective-permute-start(f32[64,512]{1,0:T(8,128)S(1)} %fusion.24), channel_id=1, source_target_pairs={{0,1},{1,2},{2,3},{3,0},{4,5},{5,6},{6,7},{7,4},{8,9},{9,10},{10,1... | collective-permute-start | bytes 393224 | tf_op jit(solution)/shard_map/ppermute | solution.py:113
  144.0 3.2 %collective-permute-start.8 = (f32[1,128,128]{2,1,0:T(8,128)S(1)}, f32[1,128,128]{2,1,0:T(8,128)S(1)}, u32[]{:S(2)}, u32[]{:S(2)}) collective-permute-start(f32[1,128,128]{2,1,0:T(8,128)S(1)} %bitcast.162), channel_id=1, source_target_pairs={{0,3},{1,0},{2,1},{3,2},{4,7},{5,4},{6,5},{7,6},{8,11},{9,8},{10,9... | collective-permute-start | bytes 196616 | tf_op jit(solution)/shard_map/ppermute | solution.py:49
  144.1 4.7 %collective-permute-start.7 = (f32[1,128,128]{2,1,0:T(8,128)S(1)}, f32[1,128,128]{2,1,0:T(8,128)S(1)}, u32[]{:S(2)}, u32[]{:S(2)}) collective-permute-start(f32[1,128,128]{2,1,0:T(8,128)S(1)} %bitcast.163), channel_id=1, source_target_pairs={{0,2},{1,3},{2,0},{3,1},{4,6},{5,7},{6,4},{7,5},{8,10},{9,11},{10,... | collective-permute-start | bytes 196616 | tf_op jit(solution)/shard_map/ppermute | solution.py:49
  144.2 5.4 %collective-permute-start.6 = (f32[1,128,128]{2,1,0:T(8,128)S(1)}, f32[1,128,128]{2,1,0:T(8,128)S(1)}, u32[]{:S(2)}, u32[]{:S(2)}) collective-permute-start(f32[1,128,128]{2,1,0:T(8,128)S(1)} %bitcast.164), channel_id=1, source_target_pairs={{0,1},{1,2},{2,3},{3,0},{4,5},{5,6},{6,7},{7,4},{8,9},{9,10},{10,1... | collective-permute-start | bytes 196616 | tf_op jit(solution)/shard_map/ppermute | solution.py:49
  167.5 0.7 copy-start.2
  168.2 6.3 %collective-permute-start.11 = (f32[1,256,128]{2,1,0:T(8,128)S(1)}, f32[1,256,128]{2,1,0:T(8,128)S(1)}, u32[]{:S(2)}, u32[]{:S(2)}) collective-permute-start(f32[1,256,128]{2,1,0:T(8,128)S(1)} %bitcast.158), channel_id=1, source_target_pairs={{0,3},{1,0},{2,1},{3,2},{4,7},{5,4},{6,5},{7,6},{8,11},{9,8},{10,9... | collective-permute-start | bytes 393224 | tf_op jit(solution)/shard_map/ppermute | solution.py:49
  170.5 5.4 %collective-permute-start.10 = (f32[1,256,128]{2,1,0:T(8,128)S(1)}, f32[1,256,128]{2,1,0:T(8,128)S(1)}, u32[]{:S(2)}, u32[]{:S(2)}) collective-permute-start(f32[1,256,128]{2,1,0:T(8,128)S(1)} %bitcast.159), channel_id=1, source_target_pairs={{0,2},{1,3},{2,0},{3,1},{4,6},{5,7},{6,4},{7,5},{8,10},{9,11},{10,... | collective-permute-start | bytes 393224 | tf_op jit(solution)/shard_map/ppermute | solution.py:49
  170.5 7.0 %collective-permute-start.9 = (f32[1,256,128]{2,1,0:T(8,128)S(1)}, f32[1,256,128]{2,1,0:T(8,128)S(1)}, u32[]{:S(2)}, u32[]{:S(2)}) collective-permute-start(f32[1,256,128]{2,1,0:T(8,128)S(1)} %bitcast.160), channel_id=1, source_target_pairs={{0,1},{1,2},{2,3},{3,0},{4,5},{5,6},{6,7},{7,4},{8,9},{9,10},{10,1... | collective-permute-start | bytes 393224 | tf_op jit(solution)/shard_map/ppermute | solution.py:49
  178.3 4.2 %collective-permute-start.12 = (f32[256,128]{1,0:T(8,128)S(1)}, f32[256,128]{1,0:T(8,128)S(1)}, u32[]{:S(2)}, u32[]{:S(2)}) collective-permute-start(f32[256,128]{1,0:T(8,128)S(1)} %fusion.22), channel_id=1, source_target_pairs={{0,4},{4,0},{8,12},{12,8},{16,20},{20,16},{24,28},{28,24},{32,36},... | collective-permute-start | bytes 393224 | tf_op jit(solution)/shard_map/ppermute | solution.py:22
  199.2 5.8 %collective-permute-start.13 = (f32[256,128]{0,1:T(8,128)S(1)}, f32[256,128]{0,1:T(8,128)S(1)}, u32[]{:S(2)}, u32[]{:S(2)}) collective-permute-start(f32[256,128]{0,1:T(8,128)S(1)} %fusion.16), channel_id=1, source_target_pairs={{0,8},{8,0},{4,12},{12,4},{16,24},{24,16},{20,28},{28,20},{32,40},... | collective-permute-start | bytes 393224 | tf_op jit(solution)/shard_map/ppermute | solution.py:22

commit v4 on v3

--- a/solution.py
+++ b/solution.py
@@ -225,7 +225,7 @@
     source = jnp.minimum(source, block_count - 1)
     high = jnp.where(filled[:, None], child_rows[source] // block_rows, -1)
     low = jnp.where(filled[:, None], child_rows[source] % block_rows, 0)
-    send_vals = jnp.where(filled[:, None, None], jnp.take(sampled, source, axis=0), jnp.bfloat16(0))
+    send_vals = jnp.take(sampled, source, axis=0)
     half = SLOT_CAP
     info_rows = 16
     loads = []

time: 224 us -> 224 us (level)
  transfers between devices with their start and end apart: 15 -> 15, of which waited for: 11 -> 10; matrix products, arithmetic and copies ran while one was open for 7% -> 8% of each run, Pallas kernels for 0% -> 0%
where the time goes in v4:
time: 224 us; the launch traced here: 222 us
  Pallas kernels  69 us (31%)
  waiting for transfers between devices  56.9 us (25%)
  starting transfers between devices  26.3 us (12%)
  other arithmetic  25.9 us (12%)
  matrix products  21.4 us (10%)
  local copies, waits for them, and re-layouts  21 us (9%)
    pallas_call x3, Pallas kernels, cholesky_inverse(): pl.pallas_call(cholesky_inverse_kernel, out_shape=jax.ShapeDtypeStruct((o...  40.1 us
    all_to_all x1, waiting for transfers between devices, on_device(): loads.append(lax.all_to_all(load, 'leaf', 0, 0, tiled=True))  36.2 us
    pallas_call x1, Pallas kernels, extend_add(): pl.pallas_call(kernel, grid_spec=pltpu.PrefetchScalarGridSpec(num_scalar_...  28.9 us
    dot_general x1, matrix products, on_device(): jnp.einsum('pck,cbik->cbpi', probe_cut, updates, preferred_element_type=j...  10.1 us
    ppermute x9, waiting for transfers between devices, gather_rows(): pieces.append(lax.ppermute(block, axis, route))  8.9 us
    all_to_all x1, starting transfers between devices, on_device(): loads.append(lax.all_to_all(load, 'leaf', 0, 0, tiled=True))  8.76 us
    ppermute x3, waiting for transfers between devices, exchange_shares(): got.append(lax.ppermute(outgoing, axis, route))  8.74 us
    ppermute x9, starting transfers between devices, gather_rows(): pieces.append(lax.ppermute(block, axis, route))  8.35 us
  transfers between devices with their start and end apart: 15, of which 10 were waited for; matrix products, arithmetic and copies ran while one was open for 8% of the time, Pallas kernels for 0%

profile of v4, /device:TPU:1, one launch (start us, length us, event | category | flops | bytes accessed | tf_op | source)
XLA Modules:
  0.0 222.3 jit_solution(16736328581868089454)
XLA Ops:
  4.7 3.7 %copy.47 = bf16[8,8,32,512]{3,2,1,0:T(8,128)(2,1)} copy(bf16[8,8,32,512]{3,1,2,0:T(8,128)(2,1)} %bitcast.152) | data formatting | bytes 4194304
  9.1 10.1 %fusion.2 = bf16[32,4,128,64]{2,3,1,0:T(8,128)(2,1)} fusion(bf16[32,4,128,512]{3,2,1,0:T(8,128)(2,1)} %bitcast.180, bf16[64,32,512,1]{2,1,0,3:T(8,128)(2,1)} %bitcast.153), kind=kOutput, calls=%fused_computation.13 | convolution fusion | flops 1074790400 | bytes 20971520 | tf_op jit(solution)/shard_map/pck,cbik->cbpi/dot_general | solution.py:212
  19.3 4.6 %gather_fusion = bf16[256,64,128]{2,1,0:T(8,128)(2,1)} fusion(bf16[128,64,128]{2,1,0:T(8,128)(2,1)} %bitcast.151, s32[1024]{0:T(1024)S(1)} %pad_clamp_fusion.2), kind=kCustom, calls=%fused_computation | custom fusion | bytes 8389632 | tf_op jit(solution)/shard_map/jit(_take)/gather | solution.py:228
  24.0 6.1 %bitcast_select_fusion = bf16[32,512,128]{2,1,0:T(8,128)(2,1)S(1)} fusion(pred[32,512]{1,0:T(8,128)(4,1)S(1)} %broadcast_in_dim.152, bf16[32,512,128]{2,1,0:T(8,128)(2,1)} %bitcast.150), kind=kLoop, calls=%fused_computation.10 | loop fusion | flops 2097152 | bytes 8404992 | tf_op jit(solution)/shard_map/jit(_take)/select_n | solution.py:228
  30.1 2.2 %pad_maximum_fusion = bf16[32,528,128]{2,1,0:T(8,128)(2,1)} fusion(bf16[32,8,128]{2,1,0:T(8,128)(2,1)S(1)} %get-tuple-element.21, bf16[32,8,128]{2,1,0:T(8,128)(2,1)S(1)} %get-tuple-element.20, bf16[32,512,128]{2,1,0:T(8,128)(2,1)S(1)} %bitcast_select_fusion), kind=kLoop, calls=%fused_computation.9 | loop fusion | flops 12976128 | bytes 8650752 | tf_op jit(solution)/shard_map/concatenate | solution.py:243
  32.4 8.8 %all-to-all-start = ((bf16[32,528,128]{2,1,0:T(8,128)(2,1)}), bf16[32,528,128]{2,1,0:T(8,128)(2,1)}, u32[]{:S(2)}, u32[]{:S(2)}) async-start(bf16[32,528,128]{2,1,0:T(8,128)(2,1)} %pad_maximum_fusion), calls=%async_computation | async-start | bytes 8650752 | tf_op jit(solution)/shard_map/all_to_all | solution.py:246
  41.2 3.8 %collective-permute-start.5 = (f32[64,128]{1,0:T(8,128)S(1)}, f32[64,128]{1,0:T(8,128)S(1)}, u32[]{:S(2)}, u32[]{:S(2)}) collective-permute-start(f32[64,128]{1,0:T(8,128)S(1)} %copy-done.5), channel_id=1, source_target_pairs={{0,3},{1,0},{2,1},{3,2},{4,7},{5,4},{6,5},{7,6},{8,11},{9,8},{10,9... | collective-permute-start | bytes 98312 | tf_op jit(solution)/shard_map/ppermute | solution.py:49
  47.3 2.9 %fusion.5 = f32[64,64,128]{2,1,0:T(8,128)} fusion(bf16[64,128,128]{2,1,0:T(8,128)(2,1)S(1)} %copy-done, bf16[64,64,128]{2,1,0:T(8,128)(2,1)S(1)} %gather_fusion.2, pred[64]{0:T(512)(128)(4,1)S(1)} %and_bitcast_fusion), kind=kOutput, calls=%fused_computation.18 | convolution fusion | flops 134742016 | bytes 5242944 | tf_op jit(solution)/shard_map/eik,pek->pei/dot_general | solution.py:250
  50.9 7.0 %scatter_fusion = f32[64,16,128]{2,0,1:T(8,128)S(1)} fusion(f32[64,16,128]{2,0,1:T(8,128)S(1)} %broadcast_in_dim.158, s32[64]{0:T(128)S(1)} %get-tuple-element.23, f32[64,64,128]{2,1,0:T(8,128)} %fusion.5), kind=kCustom, calls=%fused_computation.8 | custom fusion | flops 524288 | bytes 6291712 | tf_op jit(solution)/shard_map/scatter-add | solution.py:254
  58.6 36.2 %all-to-all-done.load_ref = bf16[32,528,128]{2,1,0:T(8,128)(2,1)} async-done(((bf16[32,528,128]{2,1,0:T(8,128)(2,1)}), bf16[32,528,128]{2,1,0:T(8,128)(2,1)}, u32[]{:S(2)}, u32[]{:S(2)}) %all-to-all-start) | async-done | bytes 4325408 | tf_op jit(solution)/shard_map/all_to_all | solution.py:246
  94.8 2.0 fusion.39.count_ref
  96.8 28.9 %shard_map.138 = f32[1024,128]{1,0:T(8,128)} custom-call(s32[32]{0:T(128)} %fusion.39.count_ref, bf16[32,528,128]{2,1,0:T(8,128)(2,1)} %all-to-all-done.load_ref, f32[1024,128]{1,0:T(8,128)} %bitcast.149), custom_call_target="tpu_custom_call" | custom-call | tf_op jit(solution)/shard_map/pallas_call | solution.py:90
  125.7 1.3 copy.64
  127.8 3.8 %collective-permute-start.2 = (f32[64,512]{1,0:T(8,128)S(1)}, f32[64,512]{1,0:T(8,128)S(1)}, u32[]{:S(2)}, u32[]{:S(2)}) collective-permute-start(f32[64,512]{1,0:T(8,128)S(1)} %bitcast.164), channel_id=1, source_target_pairs={{0,3},{1,0},{2,1},{3,2},{4,7},{5,4},{6,5},{7,6},{8,11},{9,8},{10,9... | collective-permute-start | bytes 393224 | tf_op jit(solution)/shard_map/ppermute | solution.py:113
  132.7 4.4 %collective-permute-done.2 = f32[64,512]{1,0:T(8,128)S(1)} collective-permute-done((f32[64,512]{1,0:T(8,128)S(1)}, f32[64,512]{1,0:T(8,128)S(1)}, u32[]{:S(2)}, u32[]{:S(2)}) %collective-permute-start.2) | collective-permute-done | bytes 131104 | tf_op jit(solution)/shard_map/ppermute | solution.py:113
  137.1 4.3 %collective-permute-done = f32[64,512]{1,0:T(8,128)S(1)} collective-permute-done((f32[64,512]{1,0:T(8,128)S(1)}, f32[64,512]{1,0:T(8,128)S(1)}, u32[]{:S(2)}, u32[]{:S(2)}) %collective-permute-start) | collective-permute-done | bytes 131104 | tf_op jit(solution)/shard_map/ppermute | solution.py:113
  143.9 1.4 collective-permute-start.6
  145.4 1.5 collective-permute-done.8
  146.9 1.6 collective-permute-done.7
  152.8 13.4 %shard_map.139 = f32[128,128]{1,0:T(8,128)} custom-call(f32[128,128]{1,0:T(8,128)} %fusion.33.gram_ref), custom_call_target="tpu_custom_call" | custom-call | tf_op jit(solution)/shard_map/pallas_call | solution.py:155
  166.2 1.2 convolution_select_fusion
  168.1 1.7 collective-permute-start.11
  170.4 1.2 dynamic_slice.15
  171.7 1.3 dynamic_slice.17
  173.6 1.6 collective-permute-done.10
  175.2 3.1 %collective-permute-done.9 = f32[1,256,128]{2,1,0:T(8,128)S(1)} collective-permute-done((f32[1,256,128]{2,1,0:T(8,128)S(1)}, f32[1,256,128]{2,1,0:T(8,128)S(1)}, u32[]{:S(2)}, u32[]{:S(2)}) %collective-permute-start.9) | collective-permute-done | bytes 131104 | tf_op jit(solution)/shard_map/ppermute | solution.py:49
  179.0 2.0 collective-permute-start.12
  183.8 13.4 %shard_map.140 = f32[128,128]{1,0:T(8,128)} custom-call(f32[128,128]{1,0:T(8,128)} %fusion.35.gram_ref), custom_call_target="tpu_custom_call" | custom-call | tf_op jit(solution)/shard_map/pallas_call | solution.py:155
  198.7 2.3 %collective-permute-start.13 = (f32[256,128]{0,1:T(8,128)S(1)}, f32[256,128]{0,1:T(8,128)S(1)}, u32[]{:S(2)}, u32[]{:S(2)}) collective-permute-start(f32[256,128]{0,1:T(8,128)S(1)} %fusion.15), channel_id=1, source_target_pairs={{0,8},{8,0},{4,12},{12,4},{16,24},{24,16},{20,28},{28,20},{32,40},... | collective-permute-start | bytes 393224 | tf_op jit(solution)/shard_map/ppermute | solution.py:22
  202.3 2.2 collective-permute-done.13
  206.0 13.3 %shard_map.141 = f32[128,128]{1,0:T(8,128)} custom-call(f32[128,128]{1,0:T(8,128)} %fusion.34.gram_ref), custom_call_target="tpu_custom_call" | custom-call | tf_op jit(solution)/shard_map/pallas_call | solution.py:155
  219.4 1.1 convolution_select_fusion.1
  (100 shorter events, 27.9 us)
Async XLA Ops:
  0.6 46.6 %copy-start = (bf16[64,128,128]{2,1,0:T(8,128)(2,1)S(1)}, bf16[64,128,128]{2,1,0:T(8,128)(2,1)}, u32[]{:S(2)}) copy-start(bf16[64,128,128]{2,1,0:T(8,128)(2,1)} %param.17) | copy-start | bytes 6291460
  0.6 7.8 %copy-start.2 = (s32[128,128]{1,0:T(8,128)S(1)}, s32[128,128]{1,0:T(8,128)}, u32[]{:S(2)}) copy-start(s32[128,128]{1,0:T(8,128)} %param.16) | copy-start | bytes 196612
  32.4 8.8 %copy-start.5 = (f32[64,128]{1,0:T(8,128)S(1)}, f32[64,128]{1,0:T(8,128)}, u32[]{:S(2)}) copy-start(f32[64,128]{1,0:T(8,128)} %param.20) | copy-start | bytes 98308
  32.4 14.0 %copy-start.6 = (s32[64,2]{0,1:T(2,128)S(1)}, s32[64,2]{0,1:T(2,128)}, u32[]{:S(2)}) copy-start(s32[64,2]{0,1:T(2,128)} %param.18) | copy-start | bytes 1540
  32.4 14.0 %copy-start.4 = (bf16[64,2048]{1,0:T(8,128)(2,1)S(1)}, bf16[64,2048]{1,0:T(8,128)(2,1)}, u32[]{:S(2)}) copy-start(bf16[64,2048]{1,0:T(8,128)(2,1)} %param.19) | copy-start | bytes 786436
  32.4 62.4 %all-to-all-start = ((bf16[32,528,128]{2,1,0:T(8,128)(2,1)}), bf16[32,528,128]{2,1,0:T(8,128)(2,1)}, u32[]{:S(2)}, u32[]{:S(2)}) async-start(bf16[32,528,128]{2,1,0:T(8,128)(2,1)} %pad_maximum_fusion), calls=%async_computation | async-start | bytes 8650752 | tf_op jit(solution)/shard_map/all_to_all | solution.py:246
  41.2 16.8 %collective-permute-start.5 = (f32[64,128]{1,0:T(8,128)S(1)}, f32[64,128]{1,0:T(8,128)S(1)}, u32[]{:S(2)}, u32[]{:S(2)}) collective-permute-start(f32[64,128]{1,0:T(8,128)S(1)} %copy-done.5), channel_id=1, source_target_pairs={{0,3},{1,0},{2,1},{3,2},{4,7},{5,4},{6,5},{7,6},{8,11},{9,8},{10,9... | collective-permute-start | bytes 98312 | tf_op jit(solution)/shard_map/ppermute | solution.py:49
  45.0 13.0 %collective-permute-start.4 = (f32[64,128]{1,0:T(8,128)S(1)}, f32[64,128]{1,0:T(8,128)S(1)}, u32[]{:S(2)}, u32[]{:S(2)}) collective-permute-start(f32[64,128]{1,0:T(8,128)S(1)} %copy-done.5), channel_id=1, source_target_pairs={{0,2},{1,3},{2,0},{3,1},{4,6},{5,7},{6,4},{7,5},{8,10},{9,11},{10,... | collective-permute-start | bytes 98312 | tf_op jit(solution)/shard_map/ppermute | solution.py:49
  45.0 13.0 %collective-permute-start.3 = (f32[64,128]{1,0:T(8,128)S(1)}, f32[64,128]{1,0:T(8,128)S(1)}, u32[]{:S(2)}, u32[]{:S(2)}) collective-permute-start(f32[64,128]{1,0:T(8,128)S(1)} %copy-done.5), channel_id=1, source_target_pairs={{0,1},{1,2},{2,3},{3,0},{4,5},{5,6},{6,7},{7,4},{8,9},{9,10},{10,1... | collective-permute-start | bytes 98312 | tf_op jit(solution)/shard_map/ppermute | solution.py:49
  57.9 38.9 %copy-start.1 = (f32[64,16,128]{2,0,1:T(8,128)}, f32[64,16,128]{2,0,1:T(8,128)S(1)}, u32[]{:S(2)}) copy-start(f32[64,16,128]{2,0,1:T(8,128)S(1)} %scatter_fusion) | copy-start | bytes 1572868
  127.8 9.3 %collective-permute-start.2 = (f32[64,512]{1,0:T(8,128)S(1)}, f32[64,512]{1,0:T(8,128)S(1)}, u32[]{:S(2)}, u32[]{:S(2)}) collective-permute-start(f32[64,512]{1,0:T(8,128)S(1)} %bitcast.164), channel_id=1, source_target_pairs={{0,3},{1,0},{2,1},{3,2},{4,7},{5,4},{6,5},{7,6},{8,11},{9,8},{10,9... | collective-permute-start | bytes 393224 | tf_op jit(solution)/shard_map/ppermute | solution.py:113
  131.6 34.6 %copy-start.7 = (pred[128]{0:T(512)(128)(4,1)S(1)}, pred[128]{0:T(512)(128)(4,1)}, u32[]{:S(2)}) copy-start(pred[128]{0:T(512)(128)(4,1)} %iota_compare_fusion.3) | copy-start | bytes 388
  131.6 5.5 %collective-permute-start.1 = (f32[64,512]{1,0:T(8,128)S(1)}, f32[64,512]{1,0:T(8,128)S(1)}, u32[]{:S(2)}, u32[]{:S(2)}) collective-permute-start(f32[64,512]{1,0:T(8,128)S(1)} %fusion.22), channel_id=1, source_target_pairs={{0,2},{1,3},{2,0},{3,1},{4,6},{5,7},{6,4},{7,5},{8,10},{9,11},{10,... | collective-permute-start | bytes 393224 | tf_op jit(solution)/shard_map/ppermute | solution.py:113
  131.7 9.7 %collective-permute-start = (f32[64,512]{1,0:T(8,128)S(1)}, f32[64,512]{1,0:T(8,128)S(1)}, u32[]{:S(2)}, u32[]{:S(2)}) collective-permute-start(f32[64,512]{1,0:T(8,128)S(1)} %fusion.23), channel_id=1, source_target_pairs={{0,1},{1,2},{2,3},{3,0},{4,5},{5,6},{6,7},{7,4},{8,9},{9,10},{10,1... | collective-permute-start | bytes 393224 | tf_op jit(solution)/shard_map/ppermute | solution.py:113
  143.7 3.2 %collective-permute-start.8 = (f32[1,128,128]{2,1,0:T(8,128)S(1)}, f32[1,128,128]{2,1,0:T(8,128)S(1)}, u32[]{:S(2)}, u32[]{:S(2)}) collective-permute-start(f32[1,128,128]{2,1,0:T(8,128)S(1)} %bitcast.160), channel_id=1, source_target_pairs={{0,3},{1,0},{2,1},{3,2},{4,7},{5,4},{6,5},{7,6},{8,11},{9,8},{10,9... | collective-permute-start | bytes 196616 | tf_op jit(solution)/shard_map/ppermute | solution.py:49
  143.8 4.7 %collective-permute-start.7 = (f32[1,128,128]{2,1,0:T(8,128)S(1)}, f32[1,128,128]{2,1,0:T(8,128)S(1)}, u32[]{:S(2)}, u32[]{:S(2)}) collective-permute-start(f32[1,128,128]{2,1,0:T(8,128)S(1)} %bitcast.161), channel_id=1, source_target_pairs={{0,2},{1,3},{2,0},{3,1},{4,6},{5,7},{6,4},{7,5},{8,10},{9,11},{10,... | collective-permute-start | bytes 196616 | tf_op jit(solution)/shard_map/ppermute | solution.py:49
  143.9 5.7 %collective-permute-start.6 = (f32[1,128,128]{2,1,0:T(8,128)S(1)}, f32[1,128,128]{2,1,0:T(8,128)S(1)}, u32[]{:S(2)}, u32[]{:S(2)}) collective-permute-start(f32[1,128,128]{2,1,0:T(8,128)S(1)} %bitcast.162), channel_id=1, source_target_pairs={{0,1},{1,2},{2,3},{3,0},{4,5},{5,6},{6,7},{7,4},{8,9},{9,10},{10,1... | collective-permute-start | bytes 196616 | tf_op jit(solution)/shard_map/ppermute | solution.py:49
  167.4 0.7 copy-start.3
  168.1 5.5 %collective-permute-start.11 = (f32[1,256,128]{2,1,0:T(8,128)S(1)}, f32[1,256,128]{2,1,0:T(8,128)S(1)}, u32[]{:S(2)}, u32[]{:S(2)}) collective-permute-start(f32[1,256,128]{2,1,0:T(8,128)S(1)} %bitcast.156), channel_id=1, source_target_pairs={{0,3},{1,0},{2,1},{3,2},{4,7},{5,4},{6,5},{7,6},{8,11},{9,8},{10,9... | collective-permute-start | bytes 393224 | tf_op jit(solution)/shard_map/ppermute | solution.py:49
  169.8 5.4 %collective-permute-start.10 = (f32[1,256,128]{2,1,0:T(8,128)S(1)}, f32[1,256,128]{2,1,0:T(8,128)S(1)}, u32[]{:S(2)}, u32[]{:S(2)}) collective-permute-start(f32[1,256,128]{2,1,0:T(8,128)S(1)} %bitcast.157), channel_id=1, source_target_pairs={{0,2},{1,3},{2,0},{3,1},{4,6},{5,7},{6,4},{7,5},{8,10},{9,11},{10,... | collective-permute-start | bytes 393224 | tf_op jit(solution)/shard_map/ppermute | solution.py:49
  170.2 8.1 %collective-permute-start.9 = (f32[1,256,128]{2,1,0:T(8,128)S(1)}, f32[1,256,128]{2,1,0:T(8,128)S(1)}, u32[]{:S(2)}, u32[]{:S(2)}) collective-permute-start(f32[1,256,128]{2,1,0:T(8,128)S(1)} %bitcast.158), channel_id=1, source_target_pairs={{0,1},{1,2},{2,3},{3,0},{4,5},{5,6},{6,7},{7,4},{8,9},{9,10},{10,1... | collective-permute-start | bytes 393224 | tf_op jit(solution)/shard_map/ppermute | solution.py:49
  179.0 3.0 %collective-permute-start.12 = (f32[256,128]{1,0:T(8,128)S(1)}, f32[256,128]{1,0:T(8,128)S(1)}, u32[]{:S(2)}, u32[]{:S(2)}) collective-permute-start(f32[256,128]{1,0:T(8,128)S(1)} %fusion.21), channel_id=1, source_target_pairs={{0,4},{4,0},{8,12},{12,8},{16,20},{20,16},{24,28},{28,24},{32,36},... | collective-permute-start | bytes 393224 | tf_op jit(solution)/shard_map/ppermute | solution.py:22
  198.7 5.8 %collective-permute-start.13 = (f32[256,128]{0,1:T(8,128)S(1)}, f32[256,128]{0,1:T(8,128)S(1)}, u32[]{:S(2)}, u32[]{:S(2)}) collective-permute-start(f32[256,128]{0,1:T(8,128)S(1)} %fusion.15), channel_id=1, source_target_pairs={{0,8},{8,0},{4,12},{12,4},{16,24},{24,16},{20,28},{28,20},{32,40},... | collective-permute-start | bytes 393224 | tf_op jit(solution)/shard_map/ppermute | solution.py:22

commit v5 on v4

--- a/solution.py
+++ b/solution.py
@@ -136,10 +136,11 @@
             work = work_ref[first:, :]
             pivot_row = work_ref[pl.ds(j, 1), :]
             pivot = jnp.sum(jnp.where(lane_one == j, pivot_row, 0.0), axis=1, keepdims=True)
-            column = jnp.sum(jnp.where(tail_lane == j, work, 0.0), axis=1, keepdims=True)
+            kept = jnp.where(lane_one >= j, pivot_row, 0.0)
+            column = jnp.transpose(jnp.broadcast_to(kept, (tile, order)))[first:, 0:1]
             scale = lax.rsqrt(pivot)
-            column = jnp.where(tail_sub >= j, column * scale, 0.0)
-            row = jnp.where(lane_one >= j, pivot_row * scale, 0.0)
+            column = column * scale
+            row = kept * scale
             work_ref[first:, :] = work - column * row
             solved = rest_ref[pl.ds(j, 1), :] * scale
             inverse_ref[pl.ds(j, 1), :] = solved

time: 224 us -> 256 us (1.14)
  Pallas kernels: 69 us -> 101 us
    pallas_call x3, Pallas kernels: 40.1 us -> 71.9 us  [cholesky_inverse(): pl.pallas_call(cholesky_inverse_kernel, out_shape=jax.ShapeDtypeStruct((o...]
  transfers between devices with their start and end apart: 15 -> 15, of which waited for: 10 -> 10; matrix products, arithmetic and copies ran while one was open for 8% -> 7% of each run, Pallas kernels for 0% -> 0%
where the time goes in v5:
time: 256 us; the launch traced here: 254 us
  Pallas kernels  101 us (39%)
  waiting for transfers between devices  56.9 us (22%)
  starting transfers between devices  26.5 us (10%)
  other arithmetic  25.9 us (10%)
  matrix products  21.4 us (8%)
  local copies, waits for them, and re-layouts  20.9 us (8%)
    pallas_call x3, Pallas kernels, cholesky_inverse(): pl.pallas_call(cholesky_inverse_kernel, out_shape=jax.ShapeDtypeStruct((o...  71.9 us
    all_to_all x1, waiting for transfers between devices, on_device(): loads.append(lax.all_to_all(load, 'leaf', 0, 0, tiled=True))  36.2 us
    pallas_call x1, Pallas kernels, extend_add(): pl.pallas_call(kernel, grid_spec=pltpu.PrefetchScalarGridSpec(num_scalar_...  28.9 us
    dot_general x1, matrix products, on_device(): jnp.einsum('pck,cbik->cbpi', probe_cut, updates, preferred_element_type=j...  10.1 us
    ppermute x9, waiting for transfers between devices, gather_rows(): pieces.append(lax.ppermute(block, axis, route))  8.91 us
    all_to_all x1, starting transfers between devices, on_device(): loads.append(lax.all_to_all(load, 'leaf', 0, 0, tiled=True))  8.76 us
    ppermute x3, waiting for transfers between devices, exchange_shares(): got.append(lax.ppermute(outgoing, axis, route))  8.74 us
    ppermute x9, starting transfers between devices, gather_rows(): pieces.append(lax.ppermute(block, axis, route))  8.33 us
  transfers between devices with their start and end apart: 15, of which 10 were waited for; matrix products, arithmetic and copies ran while one was open for 7% of the time, Pallas kernels for 0%

profile of v5, /device:TPU:1, one launch (start us, length us, event | category | flops | bytes accessed | tf_op | source)
XLA Modules:
  0.0 254.4 jit_solution(2422891585362353433)
XLA Ops:
  4.7 3.7 %copy.47 = bf16[8,8,32,512]{3,2,1,0:T(8,128)(2,1)} copy(bf16[8,8,32,512]{3,1,2,0:T(8,128)(2,1)} %bitcast.152) | data formatting | bytes 4194304
  9.1 10.1 %fusion.2 = bf16[32,4,128,64]{2,3,1,0:T(8,128)(2,1)} fusion(bf16[32,4,128,512]{3,2,1,0:T(8,128)(2,1)} %bitcast.180, bf16[64,32,512,1]{2,1,0,3:T(8,128)(2,1)} %bitcast.153), kind=kOutput, calls=%fused_computation.13 | convolution fusion | flops 1074790400 | bytes 20971520 | tf_op jit(solution)/shard_map/pck,cbik->cbpi/dot_general | solution.py:213
  19.3 4.6 %gather_fusion = bf16[256,64,128]{2,1,0:T(8,128)(2,1)} fusion(bf16[128,64,128]{2,1,0:T(8,128)(2,1)} %bitcast.151, s32[1024]{0:T(1024)S(1)} %pad_clamp_fusion.2), kind=kCustom, calls=%fused_computation | custom fusion | bytes 8389632 | tf_op jit(solution)/shard_map/jit(_take)/gather | solution.py:229
  24.0 6.1 %bitcast_select_fusion = bf16[32,512,128]{2,1,0:T(8,128)(2,1)S(1)} fusion(pred[32,512]{1,0:T(8,128)(4,1)S(1)} %broadcast_in_dim.152, bf16[32,512,128]{2,1,0:T(8,128)(2,1)} %bitcast.150), kind=kLoop, calls=%fused_computation.10 | loop fusion | flops 2097152 | bytes 8404992 | tf_op jit(solution)/shard_map/jit(_take)/select_n | solution.py:229
  30.1 2.2 pad_maximum_fusion
  32.4 8.8 %all-to-all-start = ((bf16[32,528,128]{2,1,0:T(8,128)(2,1)}), bf16[32,528,128]{2,1,0:T(8,128)(2,1)}, u32[]{:S(2)}, u32[]{:S(2)}) async-start(bf16[32,528,128]{2,1,0:T(8,128)(2,1)} %pad_maximum_fusion), calls=%async_computation | async-start | bytes 8650752 | tf_op jit(solution)/shard_map/all_to_all | solution.py:247
  41.2 3.8 %collective-permute-start.5 = (f32[64,128]{1,0:T(8,128)S(1)}, f32[64,128]{1,0:T(8,128)S(1)}, u32[]{:S(2)}, u32[]{:S(2)}) collective-permute-start(f32[64,128]{1,0:T(8,128)S(1)} %copy-done.5), channel_id=1, source_target_pairs={{0,3},{1,0},{2,1},{3,2},{4,7},{5,4},{6,5},{7,6},{8,11},{9,8},{10,9... | collective-permute-start | bytes 98312 | tf_op jit(solution)/shard_map/ppermute | solution.py:49
  47.3 2.9 %fusion.5 = f32[64,64,128]{2,1,0:T(8,128)} fusion(bf16[64,128,128]{2,1,0:T(8,128)(2,1)S(1)} %copy-done, bf16[64,64,128]{2,1,0:T(8,128)(2,1)S(1)} %gather_fusion.2, pred[64]{0:T(512)(128)(4,1)S(1)} %and_bitcast_fusion), kind=kOutput, calls=%fused_computation.18 | convolution fusion | flops 134742016 | bytes 5242944 | tf_op jit(solution)/shard_map/eik,pek->pei/dot_general | solution.py:251
  50.9 7.0 %scatter_fusion = f32[64,16,128]{2,0,1:T(8,128)S(1)} fusion(f32[64,16,128]{2,0,1:T(8,128)S(1)} %broadcast_in_dim.158, s32[64]{0:T(128)S(1)} %get-tuple-element.23, f32[64,64,128]{2,1,0:T(8,128)} %fusion.5), kind=kCustom, calls=%fused_computation.8 | custom fusion | flops 524288 | bytes 6291712 | tf_op jit(solution)/shard_map/scatter-add | solution.py:255
  58.6 36.2 %all-to-all-done.load_ref = bf16[32,528,128]{2,1,0:T(8,128)(2,1)} async-done(((bf16[32,528,128]{2,1,0:T(8,128)(2,1)}), bf16[32,528,128]{2,1,0:T(8,128)(2,1)}, u32[]{:S(2)}, u32[]{:S(2)}) %all-to-all-start) | async-done | bytes 4325408 | tf_op jit(solution)/shard_map/all_to_all | solution.py:247
  94.8 2.0 fusion.39.count_ref
  96.8 28.9 %shard_map.138 = f32[1024,128]{1,0:T(8,128)} custom-call(s32[32]{0:T(128)} %fusion.39.count_ref, bf16[32,528,128]{2,1,0:T(8,128)(2,1)} %all-to-all-done.load_ref, f32[1024,128]{1,0:T(8,128)} %bitcast.149), custom_call_target="tpu_custom_call" | custom-call | tf_op jit(solution)/shard_map/pallas_call | solution.py:90
  125.7 1.3 copy.64
  127.8 3.8 %collective-permute-start.2 = (f32[64,512]{1,0:T(8,128)S(1)}, f32[64,512]{1,0:T(8,128)S(1)}, u32[]{:S(2)}, u32[]{:S(2)}) collective-permute-start(f32[64,512]{1,0:T(8,128)S(1)} %bitcast.164), channel_id=1, source_target_pairs={{0,3},{1,0},{2,1},{3,2},{4,7},{5,4},{6,5},{7,6},{8,11},{9,8},{10,9... | collective-permute-start | bytes 393224 | tf_op jit(solution)/shard_map/ppermute | solution.py:113
  132.7 4.4 %collective-permute-done.2 = f32[64,512]{1,0:T(8,128)S(1)} collective-permute-done((f32[64,512]{1,0:T(8,128)S(1)}, f32[64,512]{1,0:T(8,128)S(1)}, u32[]{:S(2)}, u32[]{:S(2)}) %collective-permute-start.2) | collective-permute-done | bytes 131104 | tf_op jit(solution)/shard_map/ppermute | solution.py:113
  137.1 4.3 %collective-permute-done = f32[64,512]{1,0:T(8,128)S(1)} collective-permute-done((f32[64,512]{1,0:T(8,128)S(1)}, f32[64,512]{1,0:T(8,128)S(1)}, u32[]{:S(2)}, u32[]{:S(2)}) %collective-permute-start) | collective-permute-done | bytes 131104 | tf_op jit(solution)/shard_map/ppermute | solution.py:113
  143.9 1.4 collective-permute-start.6
  145.4 1.5 collective-permute-done.8
  146.9 1.6 collective-permute-done.7
  152.8 24.0 %shard_map.139 = f32[128,128]{1,0:T(8,128)} custom-call(f32[128,128]{1,0:T(8,128)} %fusion.33.gram_ref), custom_call_target="tpu_custom_call" | custom-call | tf_op jit(solution)/shard_map/pallas_call | solution.py:156
  176.8 1.2 convolution_select_fusion
  178.7 1.6 collective-permute-start.11
  181.0 1.2 dynamic_slice.15
  182.3 1.3 dynamic_slice.17
  184.2 1.6 collective-permute-done.10
  185.8 3.1 %collective-permute-done.9 = f32[1,256,128]{2,1,0:T(8,128)S(1)} collective-permute-done((f32[1,256,128]{2,1,0:T(8,128)S(1)}, f32[1,256,128]{2,1,0:T(8,128)S(1)}, u32[]{:S(2)}, u32[]{:S(2)}) %collective-permute-start.9) | collective-permute-done | bytes 131104 | tf_op jit(solution)/shard_map/ppermute | solution.py:49
  189.6 2.0 collective-permute-start.12
  194.4 24.0 %shard_map.140 = f32[128,128]{1,0:T(8,128)} custom-call(f32[128,128]{1,0:T(8,128)} %fusion.35.gram_ref), custom_call_target="tpu_custom_call" | custom-call | tf_op jit(solution)/shard_map/pallas_call | solution.py:156
  218.4 1.1 convolution_select_fusion.2
  219.9 2.5 collective-permute-start.13
  223.8 2.2 collective-permute-done.13
  227.5 24.0 %shard_map.141 = f32[128,128]{1,0:T(8,128)} custom-call(f32[128,128]{1,0:T(8,128)} %fusion.34.gram_ref), custom_call_target="tpu_custom_call" | custom-call | tf_op jit(solution)/shard_map/pallas_call | solution.py:156
  (100 shorter events, 27.9 us)
Async XLA Ops:
  0.6 46.6 %copy-start = (bf16[64,128,128]{2,1,0:T(8,128)(2,1)S(1)}, bf16[64,128,128]{2,1,0:T(8,128)(2,1)}, u32[]{:S(2)}) copy-start(bf16[64,128,128]{2,1,0:T(8,128)(2,1)} %param.17) | copy-start | bytes 6291460
  0.6 7.8 %copy-start.2 = (s32[128,128]{1,0:T(8,128)S(1)}, s32[128,128]{1,0:T(8,128)}, u32[]{:S(2)}) copy-start(s32[128,128]{1,0:T(8,128)} %param.16) | copy-start | bytes 196612
  32.4 8.8 %copy-start.5 = (f32[64,128]{1,0:T(8,128)S(1)}, f32[64,128]{1,0:T(8,128)}, u32[]{:S(2)}) copy-start(f32[64,128]{1,0:T(8,128)} %param.20) | copy-start | bytes 98308
  32.4 14.0 %copy-start.6 = (s32[64,2]{0,1:T(2,128)S(1)}, s32[64,2]{0,1:T(2,128)}, u32[]{:S(2)}) copy-start(s32[64,2]{0,1:T(2,128)} %param.18) | copy-start | bytes 1540
  32.4 14.0 %copy-start.4 = (bf16[64,2048]{1,0:T(8,128)(2,1)S(1)}, bf16[64,2048]{1,0:T(8,128)(2,1)}, u32[]{:S(2)}) copy-start(bf16[64,2048]{1,0:T(8,128)(2,1)} %param.19) | copy-start | bytes 786436
  32.4 62.4 %all-to-all-start = ((bf16[32,528,128]{2,1,0:T(8,128)(2,1)}), bf16[32,528,128]{2,1,0:T(8,128)(2,1)}, u32[]{:S(2)}, u32[]{:S(2)}) async-start(bf16[32,528,128]{2,1,0:T(8,128)(2,1)} %pad_maximum_fusion), calls=%async_computation | async-start | bytes 8650752 | tf_op jit(solution)/shard_map/all_to_all | solution.py:247
  41.2 16.8 %collective-permute-start.5 = (f32[64,128]{1,0:T(8,128)S(1)}, f32[64,128]{1,0:T(8,128)S(1)}, u32[]{:S(2)}, u32[]{:S(2)}) collective-permute-start(f32[64,128]{1,0:T(8,128)S(1)} %copy-done.5), channel_id=1, source_target_pairs={{0,3},{1,0},{2,1},{3,2},{4,7},{5,4},{6,5},{7,6},{8,11},{9,8},{10,9... | collective-permute-start | bytes 98312 | tf_op jit(solution)/shard_map/ppermute | solution.py:49
  45.0 13.0 %collective-permute-start.4 = (f32[64,128]{1,0:T(8,128)S(1)}, f32[64,128]{1,0:T(8,128)S(1)}, u32[]{:S(2)}, u32[]{:S(2)}) collective-permute-start(f32[64,128]{1,0:T(8,128)S(1)} %copy-done.5), channel_id=1, source_target_pairs={{0,2},{1,3},{2,0},{3,1},{4,6},{5,7},{6,4},{7,5},{8,10},{9,11},{10,... | collective-permute-start | bytes 98312 | tf_op jit(solution)/shard_map/ppermute | solution.py:49
  45.0 13.0 %collective-permute-start.3 = (f32[64,128]{1,0:T(8,128)S(1)}, f32[64,128]{1,0:T(8,128)S(1)}, u32[]{:S(2)}, u32[]{:S(2)}) collective-permute-start(f32[64,128]{1,0:T(8,128)S(1)} %copy-done.5), channel_id=1, source_target_pairs={{0,1},{1,2},{2,3},{3,0},{4,5},{5,6},{6,7},{7,4},{8,9},{9,10},{10,1... | collective-permute-start | bytes 98312 | tf_op jit(solution)/shard_map/ppermute | solution.py:49
  58.0 38.9 %copy-start.1 = (f32[64,16,128]{2,0,1:T(8,128)}, f32[64,16,128]{2,0,1:T(8,128)S(1)}, u32[]{:S(2)}) copy-start(f32[64,16,128]{2,0,1:T(8,128)S(1)} %scatter_fusion) | copy-start | bytes 1572868
  127.8 9.3 %collective-permute-start.2 = (f32[64,512]{1,0:T(8,128)S(1)}, f32[64,512]{1,0:T(8,128)S(1)}, u32[]{:S(2)}, u32[]{:S(2)}) collective-permute-start(f32[64,512]{1,0:T(8,128)S(1)} %bitcast.164), channel_id=1, source_target_pairs={{0,3},{1,0},{2,1},{3,2},{4,7},{5,4},{6,5},{7,6},{8,11},{9,8},{10,9... | collective-permute-start | bytes 393224 | tf_op jit(solution)/shard_map/ppermute | solution.py:113
  131.6 45.2 %copy-start.7 = (pred[128]{0:T(512)(128)(4,1)S(1)}, pred[128]{0:T(512)(128)(4,1)}, u32[]{:S(2)}) copy-start(pred[128]{0:T(512)(128)(4,1)} %iota_compare_fusion.3) | copy-start | bytes 388
  131.6 5.5 %collective-permute-start.1 = (f32[64,512]{1,0:T(8,128)S(1)}, f32[64,512]{1,0:T(8,128)S(1)}, u32[]{:S(2)}, u32[]{:S(2)}) collective-permute-start(f32[64,512]{1,0:T(8,128)S(1)} %fusion.22), channel_id=1, source_target_pairs={{0,2},{1,3},{2,0},{3,1},{4,6},{5,7},{6,4},{7,5},{8,10},{9,11},{10,... | collective-permute-start | bytes 393224 | tf_op jit(solution)/shard_map/ppermute | solution.py:113
  131.7 9.7 %collective-permute-start = (f32[64,512]{1,0:T(8,128)S(1)}, f32[64,512]{1,0:T(8,128)S(1)}, u32[]{:S(2)}, u32[]{:S(2)}) collective-permute-start(f32[64,512]{1,0:T(8,128)S(1)} %fusion.23), channel_id=1, source_target_pairs={{0,1},{1,2},{2,3},{3,0},{4,5},{5,6},{6,7},{7,4},{8,9},{9,10},{10,1... | collective-permute-start | bytes 393224 | tf_op jit(solution)/shard_map/ppermute | solution.py:113
  143.7 3.2 %collective-permute-start.8 = (f32[1,128,128]{2,1,0:T(8,128)S(1)}, f32[1,128,128]{2,1,0:T(8,128)S(1)}, u32[]{:S(2)}, u32[]{:S(2)}) collective-permute-start(f32[1,128,128]{2,1,0:T(8,128)S(1)} %bitcast.160), channel_id=1, source_target_pairs={{0,3},{1,0},{2,1},{3,2},{4,7},{5,4},{6,5},{7,6},{8,11},{9,8},{10,9... | collective-permute-start | bytes 196616 | tf_op jit(solution)/shard_map/ppermute | solution.py:49
  143.8 4.7 %collective-permute-start.7 = (f32[1,128,128]{2,1,0:T(8,128)S(1)}, f32[1,128,128]{2,1,0:T(8,128)S(1)}, u32[]{:S(2)}, u32[]{:S(2)}) collective-permute-start(f32[1,128,128]{2,1,0:T(8,128)S(1)} %bitcast.161), channel_id=1, source_target_pairs={{0,2},{1,3},{2,0},{3,1},{4,6},{5,7},{6,4},{7,5},{8,10},{9,11},{10,... | collective-permute-start | bytes 196616 | tf_op jit(solution)/shard_map/ppermute | solution.py:49
  143.9 5.7 %collective-permute-start.6 = (f32[1,128,128]{2,1,0:T(8,128)S(1)}, f32[1,128,128]{2,1,0:T(8,128)S(1)}, u32[]{:S(2)}, u32[]{:S(2)}) collective-permute-start(f32[1,128,128]{2,1,0:T(8,128)S(1)} %bitcast.162), channel_id=1, source_target_pairs={{0,1},{1,2},{2,3},{3,0},{4,5},{5,6},{6,7},{7,4},{8,9},{9,10},{10,1... | collective-permute-start | bytes 196616 | tf_op jit(solution)/shard_map/ppermute | solution.py:49
  178.0 0.7 copy-start.3
  178.7 5.5 %collective-permute-start.11 = (f32[1,256,128]{2,1,0:T(8,128)S(1)}, f32[1,256,128]{2,1,0:T(8,128)S(1)}, u32[]{:S(2)}, u32[]{:S(2)}) collective-permute-start(f32[1,256,128]{2,1,0:T(8,128)S(1)} %bitcast.156), channel_id=1, source_target_pairs={{0,3},{1,0},{2,1},{3,2},{4,7},{5,4},{6,5},{7,6},{8,11},{9,8},{10,9... | collective-permute-start | bytes 393224 | tf_op jit(solution)/shard_map/ppermute | solution.py:49
  180.4 5.4 %collective-permute-start.10 = (f32[1,256,128]{2,1,0:T(8,128)S(1)}, f32[1,256,128]{2,1,0:T(8,128)S(1)}, u32[]{:S(2)}, u32[]{:S(2)}) collective-permute-start(f32[1,256,128]{2,1,0:T(8,128)S(1)} %bitcast.157), channel_id=1, source_target_pairs={{0,2},{1,3},{2,0},{3,1},{4,6},{5,7},{6,4},{7,5},{8,10},{9,11},{10,... | collective-permute-start | bytes 393224 | tf_op jit(solution)/shard_map/ppermute | solution.py:49
  180.8 8.1 %collective-permute-start.9 = (f32[1,256,128]{2,1,0:T(8,128)S(1)}, f32[1,256,128]{2,1,0:T(8,128)S(1)}, u32[]{:S(2)}, u32[]{:S(2)}) collective-permute-start(f32[1,256,128]{2,1,0:T(8,128)S(1)} %bitcast.158), channel_id=1, source_target_pairs={{0,1},{1,2},{2,3},{3,0},{4,5},{5,6},{6,7},{7,4},{8,9},{9,10},{10,1... | collective-permute-start | bytes 393224 | tf_op jit(solution)/shard_map/ppermute | solution.py:49
  189.6 3.0 %collective-permute-start.12 = (f32[256,128]{1,0:T(8,128)S(1)}, f32[256,128]{1,0:T(8,128)S(1)}, u32[]{:S(2)}, u32[]{:S(2)}) collective-permute-start(f32[256,128]{1,0:T(8,128)S(1)} %fusion.21), channel_id=1, source_target_pairs={{0,4},{4,0},{8,12},{12,8},{16,20},{20,16},{24,28},{28,24},{32,36},... | collective-permute-start | bytes 393224 | tf_op jit(solution)/shard_map/ppermute | solution.py:22
  219.9 6.1 %collective-permute-start.13 = (f32[256,128]{0,1:T(8,128)S(1)}, f32[256,128]{0,1:T(8,128)S(1)}, u32[]{:S(2)}, u32[]{:S(2)}) collective-permute-start(f32[256,128]{0,1:T(8,128)S(1)} %fusion.15), channel_id=1, source_target_pairs={{0,8},{8,0},{4,12},{12,4},{16,24},{24,16},{20,28},{28,20},{32,40},... | collective-permute-start | bytes 393224 | tf_op jit(solution)/shard_map/ppermute | solution.py:22

commit v6 on v4

--- a/solution.py
+++ b/solution.py
@@ -56,6 +56,7 @@
 def extend_add_kernel(count_ref, load_ref, start_ref, out_ref, *, slots, probes):
     source = pl.program_id(0)
     lanes = load_ref.shape[2]
+    width = out_ref.shape[1]
     high_count = out_ref.shape[0] // probes
     info = slots * probes
 
@@ -69,13 +70,16 @@
         for slot in range(slots):
             high = load_ref[0, pl.ds(info + slot, 1), :].astype(jnp.float32).astype(jnp.int32)
             low = load_ref[0, pl.ds(info + slots + slot, 1), :].astype(jnp.float32).astype(jnp.int32)
+            target = high * lanes + low
+            block = jnp.where(target >= 0, target // width, -1)
+            offset = target % width
             vals = load_ref[0, pl.ds(slot * probes, probes), :]
             zero = jnp.zeros_like(vals)
             spread.append(
-                jnp.concatenate([jnp.where(high == h, vals, zero) for h in range(high_count)], axis=0)
+                jnp.concatenate([jnp.where(block == h, vals, zero) for h in range(high_count)], axis=0)
             )
             hot.append(
-                (lax.broadcasted_iota(jnp.int32, (lanes, lanes), 0) == low).astype(jnp.bfloat16)
+                (lax.broadcasted_iota(jnp.int32, (width, lanes), 0) == offset).astype(jnp.bfloat16)
             )
         spread = jnp.concatenate(spread, axis=1)
         hot = jnp.concatenate(hot, axis=1)
@@ -254,13 +258,14 @@
         .add(product)
         .reshape(local_probes, front_rows)
     )
-    high_count = front_rows // block_rows
-    spread = jnp.moveaxis(initial.reshape(local_probes, high_count, block_rows), 1, 0)
-    spread = spread.reshape(high_count * local_probes, block_rows)
+    width = 2 * block_rows
+    high_count = front_rows // width
+    spread = jnp.moveaxis(initial.reshape(local_probes, high_count, width), 1, 0)
+    spread = spread.reshape(high_count * local_probes, width)
     for load in loads:
         counts = jnp.sum(load[:, half * local_probes, :1] >= 0, axis=1).astype(jnp.int32)
         spread = extend_add(load, counts, spread, half, local_probes)
-    spread = spread.reshape(high_count, local_probes, block_rows)
+    spread = spread.reshape(high_count, local_probes, width)
     sample = jnp.moveaxis(spread, 0, 1).reshape(local_probes, front_rows)
 
     share_rows = front_rows // probe_count

time: 224 us -> 220 us (0.982)
  Pallas kernels: 69 us -> 65.2 us
  waiting for transfers between devices: 56.9 us -> 54.1 us
    pallas_call x1, Pallas kernels: 28.9 us -> 25.1 us  [extend_add(): pl.pallas_call(kernel, grid_spec=pltpu.PrefetchScalarGridSpec(num_scalar_...]
  transfers between devices with their start and end apart: 15 -> 15, of which waited for: 10 -> 11; matrix products, arithmetic and copies ran while one was open for 8% -> 8% of each run, Pallas kernels for 0% -> 0%
where the time goes in v6:
time: 220 us; the launch traced here: 219 us
  Pallas kernels  65.2 us (30%)
  waiting for transfers between devices  54.1 us (25%)
  starting transfers between devices  28.2 us (13%)
  other arithmetic  25.4 us (12%)
  local copies, waits for them, and re-layouts  22.5 us (10%)
  matrix products  21.4 us (10%)
    pallas_call x3, Pallas kernels, cholesky_inverse(): pl.pallas_call(cholesky_inverse_kernel, out_shape=jax.ShapeDtypeStruct((o...  40.1 us
    all_to_all x1, waiting for transfers between devices, on_device(): loads.append(lax.all_to_all(load, 'leaf', 0, 0, tiled=True))  35.2 us
    pallas_call x1, Pallas kernels, extend_add(): pl.pallas_call(kernel, grid_spec=pltpu.PrefetchScalarGridSpec(num_scalar_...  25.1 us
    dot_general x1, matrix products, on_device(): jnp.einsum('pck,cbik->cbpi', probe_cut, updates, preferred_element_type=j...  10.1 us
    ppermute x9, starting transfers between devices, gather_rows(): pieces.append(lax.ppermute(block, axis, route))  9 us
    all_to_all x1, starting transfers between devices, on_device(): loads.append(lax.all_to_all(load, 'leaf', 0, 0, tiled=True))  8.76 us
    ppermute x3, waiting for transfers between devices, exchange_shares(): got.append(lax.ppermute(outgoing, axis, route))  8.56 us
    ppermute x9, waiting for transfers between devices, gather_rows(): pieces.append(lax.ppermute(block, axis, route))  7.2 us
  transfers between devices with their start and end apart: 15, of which 11 were waited for; matrix products, arithmetic and copies ran while one was open for 8% of the time, Pallas kernels for 0%

profile of v6, /device:TPU:1, one launch (start us, length us, event | category | flops | bytes accessed | tf_op | source)
XLA Modules:
  0.0 218.6 jit_solution(14826984704429409274)
XLA Ops:
  4.7 3.7 %copy.51 = bf16[8,8,32,512]{3,2,1,0:T(8,128)(2,1)} copy(bf16[8,8,32,512]{3,1,2,0:T(8,128)(2,1)} %bitcast.150) | data formatting | bytes 4194304
  9.1 10.1 %fusion.2 = bf16[32,4,128,64]{2,3,1,0:T(8,128)(2,1)} fusion(bf16[32,4,128,512]{3,2,1,0:T(8,128)(2,1)} %bitcast.180, bf16[64,32,512,1]{2,1,0,3:T(8,128)(2,1)} %bitcast.151), kind=kOutput, calls=%fused_computation.13 | convolution fusion | flops 1074790400 | bytes 20971520 | tf_op jit(solution)/shard_map/pck,cbik->cbpi/dot_general | solution.py:216
  19.2 4.6 %gather_fusion = bf16[256,64,128]{2,1,0:T(8,128)(2,1)} fusion(bf16[128,64,128]{2,1,0:T(8,128)(2,1)} %bitcast.149, s32[1024]{0:T(1024)S(1)} %pad_clamp_fusion.2), kind=kCustom, calls=%fused_computation | custom fusion | bytes 8389632 | tf_op jit(solution)/shard_map/jit(_take)/gather | solution.py:232
  24.0 6.1 %bitcast_select_fusion = bf16[32,512,128]{2,1,0:T(8,128)(2,1)S(1)} fusion(pred[32,512]{1,0:T(8,128)(4,1)S(1)} %broadcast_in_dim.152, bf16[32,512,128]{2,1,0:T(8,128)(2,1)} %bitcast.148), kind=kLoop, calls=%fused_computation.10 | loop fusion | flops 2097152 | bytes 8404992 | tf_op jit(solution)/shard_map/jit(_take)/select_n | solution.py:232
  30.1 2.3 %pad_maximum_fusion = bf16[32,528,128]{2,1,0:T(8,128)(2,1)} fusion(bf16[32,8,128]{2,1,0:T(8,128)(2,1)S(1)} %get-tuple-element.21, bf16[32,8,128]{2,1,0:T(8,128)(2,1)S(1)} %get-tuple-element.20, bf16[32,512,128]{2,1,0:T(8,128)(2,1)S(1)} %bitcast_select_fusion), kind=kLoop, calls=%fused_computation.9 | loop fusion | flops 12976128 | bytes 8650752 | tf_op jit(solution)/shard_map/concatenate | solution.py:247
  32.4 8.8 %all-to-all-start = ((bf16[32,528,128]{2,1,0:T(8,128)(2,1)}), bf16[32,528,128]{2,1,0:T(8,128)(2,1)}, u32[]{:S(2)}, u32[]{:S(2)}) async-start(bf16[32,528,128]{2,1,0:T(8,128)(2,1)} %pad_maximum_fusion), calls=%async_computation | async-start | bytes 8650752 | tf_op jit(solution)/shard_map/all_to_all | solution.py:250
  41.1 3.8 %collective-permute-start.5 = (f32[64,128]{1,0:T(8,128)S(1)}, f32[64,128]{1,0:T(8,128)S(1)}, u32[]{:S(2)}, u32[]{:S(2)}) collective-permute-start(f32[64,128]{1,0:T(8,128)S(1)} %copy-done.4), channel_id=1, source_target_pairs={{0,3},{1,0},{2,1},{3,2},{4,7},{5,4},{6,5},{7,6},{8,11},{9,8},{10,9... | collective-permute-start | bytes 98312 | tf_op jit(solution)/shard_map/ppermute | solution.py:49
  47.3 2.9 %fusion.5 = f32[64,64,128]{2,1,0:T(8,128)} fusion(bf16[64,128,128]{2,1,0:T(8,128)(2,1)S(1)} %copy-done, bf16[64,64,128]{2,1,0:T(8,128)(2,1)S(1)} %gather_fusion.2, pred[64]{0:T(512)(128)(4,1)S(1)} %and_bitcast_fusion), kind=kOutput, calls=%fused_computation.18 | convolution fusion | flops 134742016 | bytes 5242944 | tf_op jit(solution)/shard_map/eik,pek->pei/dot_general | solution.py:254
  50.3 7.0 %scatter_fusion = f32[64,16,128]{2,0,1:T(8,128)S(1)} fusion(f32[64,16,128]{2,0,1:T(8,128)S(1)} %broadcast_in_dim.158, s32[64]{0:T(128)S(1)} %get-tuple-element.23, f32[64,64,128]{2,1,0:T(8,128)} %fusion.5), kind=kCustom, calls=%fused_computation.8 | custom fusion | flops 524288 | bytes 6291712 | tf_op jit(solution)/shard_map/scatter-add | solution.py:258
  59.5 35.2 %all-to-all-done.load_ref = bf16[32,528,128]{2,1,0:T(8,128)(2,1)} async-done(((bf16[32,528,128]{2,1,0:T(8,128)(2,1)}), bf16[32,528,128]{2,1,0:T(8,128)(2,1)}, u32[]{:S(2)}, u32[]{:S(2)}) %all-to-all-start) | async-done | bytes 4325408 | tf_op jit(solution)/shard_map/all_to_all | solution.py:250
  94.8 2.0 fusion.39.count_ref
  96.8 25.1 %shard_map.138 = f32[512,256]{1,0:T(8,128)} custom-call(s32[32]{0:T(128)} %fusion.39.count_ref, bf16[32,528,128]{2,1,0:T(8,128)(2,1)} %all-to-all-done.load_ref, f32[512,256]{1,0:T(8,128)} %bitcast.154), custom_call_target="tpu_custom_call" | custom-call | tf_op jit(solution)/shard_map/pallas_call | solution.py:94
  121.9 1.3 copy.68
  124.0 4.0 %collective-permute-start.2 = (f32[64,512]{1,0:T(8,128)S(1)}, f32[64,512]{1,0:T(8,128)S(1)}, u32[]{:S(2)}, u32[]{:S(2)}) collective-permute-start(f32[64,512]{1,0:T(8,128)S(1)} %bitcast.164), channel_id=1, source_target_pairs={{0,3},{1,0},{2,1},{3,2},{4,7},{5,4},{6,5},{7,6},{8,11},{9,8},{10,9... | collective-permute-start | bytes 393224 | tf_op jit(solution)/shard_map/ppermute | solution.py:117
  128.9 4.6 %collective-permute-done.2 = f32[64,512]{1,0:T(8,128)S(1)} collective-permute-done((f32[64,512]{1,0:T(8,128)S(1)}, f32[64,512]{1,0:T(8,128)S(1)}, u32[]{:S(2)}, u32[]{:S(2)}) %collective-permute-start.2) | collective-permute-done | bytes 131104 | tf_op jit(solution)/shard_map/ppermute | solution.py:117
  133.6 3.9 %collective-permute-done = f32[64,512]{1,0:T(8,128)S(1)} collective-permute-done((f32[64,512]{1,0:T(8,128)S(1)}, f32[64,512]{1,0:T(8,128)S(1)}, u32[]{:S(2)}, u32[]{:S(2)}) %collective-permute-start) | collective-permute-done | bytes 131104 | tf_op jit(solution)/shard_map/ppermute | solution.py:117
  140.0 1.4 collective-permute-start.6
  141.5 1.5 collective-permute-done.8
  143.0 1.6 collective-permute-done.7
  148.6 13.4 %shard_map.139 = f32[128,128]{1,0:T(8,128)} custom-call(f32[128,128]{1,0:T(8,128)} %fusion.33.gram_ref), custom_call_target="tpu_custom_call" | custom-call | tf_op jit(solution)/shard_map/pallas_call | solution.py:159
  162.0 1.2 convolution_select_fusion
  163.9 2.3 %collective-permute-start.11 = (f32[1,256,128]{2,1,0:T(8,128)S(1)}, f32[1,256,128]{2,1,0:T(8,128)S(1)}, u32[]{:S(2)}, u32[]{:S(2)}) collective-permute-start(f32[1,256,128]{2,1,0:T(8,128)S(1)} %bitcast.156), channel_id=1, source_target_pairs={{0,3},{1,0},{2,1},{3,2},{4,7},{5,4},{6,5},{7,6},{8,11},{9,8},{10,9... | collective-permute-start | bytes 393224 | tf_op jit(solution)/shard_map/ppermute | solution.py:49
  166.9 1.2 dynamic_slice.15
  168.1 1.3 dynamic_slice.17
  170.2 1.4 collective-permute-done.10
  171.7 1.6 collective-permute-done.9
  174.1 3.2 %collective-permute-start.12 = (f32[256,128]{1,0:T(8,128)S(1)}, f32[256,128]{1,0:T(8,128)S(1)}, u32[]{:S(2)}, u32[]{:S(2)}) collective-permute-start(f32[256,128]{1,0:T(8,128)S(1)} %fusion.21), channel_id=1, source_target_pairs={{0,4},{4,0},{8,12},{12,8},{16,20},{20,16},{24,28},{28,24},{32,36},... | collective-permute-start | bytes 393224 | tf_op jit(solution)/shard_map/ppermute | solution.py:22
  180.0 13.4 %shard_map.140 = f32[128,128]{1,0:T(8,128)} custom-call(f32[128,128]{1,0:T(8,128)} %fusion.35.gram_ref), custom_call_target="tpu_custom_call" | custom-call | tf_op jit(solution)/shard_map/pallas_call | solution.py:159
  194.9 2.3 %collective-permute-start.13 = (f32[256,128]{0,1:T(8,128)S(1)}, f32[256,128]{0,1:T(8,128)S(1)}, u32[]{:S(2)}, u32[]{:S(2)}) collective-permute-start(f32[256,128]{0,1:T(8,128)S(1)} %fusion.15), channel_id=1, source_target_pairs={{0,8},{8,0},{4,12},{12,4},{16,24},{24,16},{20,28},{28,20},{32,40},... | collective-permute-start | bytes 393224 | tf_op jit(solution)/shard_map/ppermute | solution.py:22
  198.6 2.2 %collective-permute-done.13 = f32[256,128]{0,1:T(8,128)S(1)} collective-permute-done((f32[256,128]{0,1:T(8,128)S(1)}, f32[256,128]{0,1:T(8,128)S(1)}, u32[]{:S(2)}, u32[]{:S(2)}) %collective-permute-start.13) | collective-permute-done | bytes 131104 | tf_op jit(solution)/shard_map/ppermute | solution.py:22
  202.3 13.4 %shard_map.141 = f32[128,128]{1,0:T(8,128)} custom-call(f32[128,128]{1,0:T(8,128)} %fusion.34.gram_ref), custom_call_target="tpu_custom_call" | custom-call | tf_op jit(solution)/shard_map/pallas_call | solution.py:159
  215.7 1.1 convolution_select_fusion.1
  (99 shorter events, 28.7 us)
Async XLA Ops:
  0.6 46.6 %copy-start = (bf16[64,128,128]{2,1,0:T(8,128)(2,1)S(1)}, bf16[64,128,128]{2,1,0:T(8,128)(2,1)}, u32[]{:S(2)}) copy-start(bf16[64,128,128]{2,1,0:T(8,128)(2,1)} %param.17) | copy-start | bytes 6291460
  0.6 7.7 %copy-start.1 = (s32[128,128]{1,0:T(8,128)S(1)}, s32[128,128]{1,0:T(8,128)}, u32[]{:S(2)}) copy-start(s32[128,128]{1,0:T(8,128)} %param.16) | copy-start | bytes 196612
  32.4 8.8 %copy-start.4 = (f32[64,128]{1,0:T(8,128)S(1)}, f32[64,128]{1,0:T(8,128)}, u32[]{:S(2)}) copy-start(f32[64,128]{1,0:T(8,128)} %param.20) | copy-start | bytes 98308
  32.4 14.0 %copy-start.5 = (s32[64,2]{0,1:T(2,128)S(1)}, s32[64,2]{0,1:T(2,128)}, u32[]{:S(2)}) copy-start(s32[64,2]{0,1:T(2,128)} %param.18) | copy-start | bytes 1540
  32.4 14.0 %copy-start.3 = (bf16[64,2048]{1,0:T(8,128)(2,1)S(1)}, bf16[64,2048]{1,0:T(8,128)(2,1)}, u32[]{:S(2)}) copy-start(bf16[64,2048]{1,0:T(8,128)(2,1)} %param.19) | copy-start | bytes 786436
  32.4 62.4 %all-to-all-start = ((bf16[32,528,128]{2,1,0:T(8,128)(2,1)}), bf16[32,528,128]{2,1,0:T(8,128)(2,1)}, u32[]{:S(2)}, u32[]{:S(2)}) async-start(bf16[32,528,128]{2,1,0:T(8,128)(2,1)} %pad_maximum_fusion), calls=%async_computation | async-start | bytes 8650752 | tf_op jit(solution)/shard_map/all_to_all | solution.py:250
  41.1 17.8 %collective-permute-start.5 = (f32[64,128]{1,0:T(8,128)S(1)}, f32[64,128]{1,0:T(8,128)S(1)}, u32[]{:S(2)}, u32[]{:S(2)}) collective-permute-start(f32[64,128]{1,0:T(8,128)S(1)} %copy-done.4), channel_id=1, source_target_pairs={{0,3},{1,0},{2,1},{3,2},{4,7},{5,4},{6,5},{7,6},{8,11},{9,8},{10,9... | collective-permute-start | bytes 98312 | tf_op jit(solution)/shard_map/ppermute | solution.py:49
  45.0 14.0 %collective-permute-start.4 = (f32[64,128]{1,0:T(8,128)S(1)}, f32[64,128]{1,0:T(8,128)S(1)}, u32[]{:S(2)}, u32[]{:S(2)}) collective-permute-start(f32[64,128]{1,0:T(8,128)S(1)} %copy-done.4), channel_id=1, source_target_pairs={{0,2},{1,3},{2,0},{3,1},{4,6},{5,7},{6,4},{7,5},{8,10},{9,11},{10,... | collective-permute-start | bytes 98312 | tf_op jit(solution)/shard_map/ppermute | solution.py:49
  45.0 14.0 %collective-permute-start.3 = (f32[64,128]{1,0:T(8,128)S(1)}, f32[64,128]{1,0:T(8,128)S(1)}, u32[]{:S(2)}, u32[]{:S(2)}) collective-permute-start(f32[64,128]{1,0:T(8,128)S(1)} %copy-done.4), channel_id=1, source_target_pairs={{0,1},{1,2},{2,3},{3,0},{4,5},{5,6},{6,7},{7,4},{8,9},{9,10},{10,1... | collective-permute-start | bytes 98312 | tf_op jit(solution)/shard_map/ppermute | solution.py:49
  124.0 9.5 %collective-permute-start.2 = (f32[64,512]{1,0:T(8,128)S(1)}, f32[64,512]{1,0:T(8,128)S(1)}, u32[]{:S(2)}, u32[]{:S(2)}) collective-permute-start(f32[64,512]{1,0:T(8,128)S(1)} %bitcast.164), channel_id=1, source_target_pairs={{0,3},{1,0},{2,1},{3,2},{4,7},{5,4},{6,5},{7,6},{8,11},{9,8},{10,9... | collective-permute-start | bytes 393224 | tf_op jit(solution)/shard_map/ppermute | solution.py:117
  128.1 5.5 %collective-permute-start.1 = (f32[64,512]{1,0:T(8,128)S(1)}, f32[64,512]{1,0:T(8,128)S(1)}, u32[]{:S(2)}, u32[]{:S(2)}) collective-permute-start(f32[64,512]{1,0:T(8,128)S(1)} %fusion.22), channel_id=1, source_target_pairs={{0,2},{1,3},{2,0},{3,1},{4,6},{5,7},{6,4},{7,5},{8,10},{9,11},{10,... | collective-permute-start | bytes 393224 | tf_op jit(solution)/shard_map/ppermute | solution.py:117
  128.2 9.3 %collective-permute-start = (f32[64,512]{1,0:T(8,128)S(1)}, f32[64,512]{1,0:T(8,128)S(1)}, u32[]{:S(2)}, u32[]{:S(2)}) collective-permute-start(f32[64,512]{1,0:T(8,128)S(1)} %fusion.23), channel_id=1, source_target_pairs={{0,1},{1,2},{2,3},{3,0},{4,5},{5,6},{6,7},{7,4},{8,9},{9,10},{10,1... | collective-permute-start | bytes 393224 | tf_op jit(solution)/shard_map/ppermute | solution.py:117
  139.8 3.2 %collective-permute-start.8 = (f32[1,128,128]{2,1,0:T(8,128)S(1)}, f32[1,128,128]{2,1,0:T(8,128)S(1)}, u32[]{:S(2)}, u32[]{:S(2)}) collective-permute-start(f32[1,128,128]{2,1,0:T(8,128)S(1)} %bitcast.160), channel_id=1, source_target_pairs={{0,3},{1,0},{2,1},{3,2},{4,7},{5,4},{6,5},{7,6},{8,11},{9,8},{10,9... | collective-permute-start | bytes 196616 | tf_op jit(solution)/shard_map/ppermute | solution.py:49
  139.9 4.7 %collective-permute-start.7 = (f32[1,128,128]{2,1,0:T(8,128)S(1)}, f32[1,128,128]{2,1,0:T(8,128)S(1)}, u32[]{:S(2)}, u32[]{:S(2)}) collective-permute-start(f32[1,128,128]{2,1,0:T(8,128)S(1)} %bitcast.161), channel_id=1, source_target_pairs={{0,2},{1,3},{2,0},{3,1},{4,6},{5,7},{6,4},{7,5},{8,10},{9,11},{10,... | collective-permute-start | bytes 196616 | tf_op jit(solution)/shard_map/ppermute | solution.py:49
  140.0 5.4 %collective-permute-start.6 = (f32[1,128,128]{2,1,0:T(8,128)S(1)}, f32[1,128,128]{2,1,0:T(8,128)S(1)}, u32[]{:S(2)}, u32[]{:S(2)}) collective-permute-start(f32[1,128,128]{2,1,0:T(8,128)S(1)} %bitcast.162), channel_id=1, source_target_pairs={{0,1},{1,2},{2,3},{3,0},{4,5},{5,6},{6,7},{7,4},{8,9},{9,10},{10,1... | collective-permute-start | bytes 196616 | tf_op jit(solution)/shard_map/ppermute | solution.py:49
  163.2 0.7 copy-start.2
  163.9 6.3 %collective-permute-start.11 = (f32[1,256,128]{2,1,0:T(8,128)S(1)}, f32[1,256,128]{2,1,0:T(8,128)S(1)}, u32[]{:S(2)}, u32[]{:S(2)}) collective-permute-start(f32[1,256,128]{2,1,0:T(8,128)S(1)} %bitcast.156), channel_id=1, source_target_pairs={{0,3},{1,0},{2,1},{3,2},{4,7},{5,4},{6,5},{7,6},{8,11},{9,8},{10,9... | collective-permute-start | bytes 393224 | tf_op jit(solution)/shard_map/ppermute | solution.py:49
  166.2 5.4 %collective-permute-start.10 = (f32[1,256,128]{2,1,0:T(8,128)S(1)}, f32[1,256,128]{2,1,0:T(8,128)S(1)}, u32[]{:S(2)}, u32[]{:S(2)}) collective-permute-start(f32[1,256,128]{2,1,0:T(8,128)S(1)} %bitcast.157), channel_id=1, source_target_pairs={{0,2},{1,3},{2,0},{3,1},{4,6},{5,7},{6,4},{7,5},{8,10},{9,11},{10,... | collective-permute-start | bytes 393224 | tf_op jit(solution)/shard_map/ppermute | solution.py:49
  166.3 7.0 %collective-permute-start.9 = (f32[1,256,128]{2,1,0:T(8,128)S(1)}, f32[1,256,128]{2,1,0:T(8,128)S(1)}, u32[]{:S(2)}, u32[]{:S(2)}) collective-permute-start(f32[1,256,128]{2,1,0:T(8,128)S(1)} %bitcast.158), channel_id=1, source_target_pairs={{0,1},{1,2},{2,3},{3,0},{4,5},{5,6},{6,7},{7,4},{8,9},{9,10},{10,1... | collective-permute-start | bytes 393224 | tf_op jit(solution)/shard_map/ppermute | solution.py:49
  174.1 4.2 %collective-permute-start.12 = (f32[256,128]{1,0:T(8,128)S(1)}, f32[256,128]{1,0:T(8,128)S(1)}, u32[]{:S(2)}, u32[]{:S(2)}) collective-permute-start(f32[256,128]{1,0:T(8,128)S(1)} %fusion.21), channel_id=1, source_target_pairs={{0,4},{4,0},{8,12},{12,8},{16,20},{20,16},{24,28},{28,24},{32,36},... | collective-permute-start | bytes 393224 | tf_op jit(solution)/shard_map/ppermute | solution.py:22
  194.9 5.9 %collective-permute-start.13 = (f32[256,128]{0,1:T(8,128)S(1)}, f32[256,128]{0,1:T(8,128)S(1)}, u32[]{:S(2)}, u32[]{:S(2)}) collective-permute-start(f32[256,128]{0,1:T(8,128)S(1)} %fusion.15), channel_id=1, source_target_pairs={{0,8},{8,0},{4,12},{12,4},{16,24},{24,16},{20,28},{28,20},{32,40},... | collective-permute-start | bytes 393224 | tf_op jit(solution)/shard_map/ppermute | solution.py:22

commit v7 on v6

--- a/solution.py
+++ b/solution.py
@@ -258,7 +258,7 @@
         .add(product)
         .reshape(local_probes, front_rows)
     )
-    width = 2 * block_rows
+    width = 4 * block_rows
     high_count = front_rows // width
     spread = jnp.moveaxis(initial.reshape(local_probes, high_count, width), 1, 0)
     spread = spread.reshape(high_count * local_probes, width)

time: 220 us -> 220 us (level)
    unnamed x14 -> x17, local copies, waits for them, and re-layouts: 3.84 us -> 4.48 us
  transfers between devices with their start and end apart: 15 -> 15, of which waited for: 11 -> 11; matrix products, arithmetic and copies ran while one was open for 8% -> 10% of each run, Pallas kernels for 0% -> 11%
where the time goes in v7:
time: 220 us; the launch traced here: 219 us
  Pallas kernels  65.1 us (30%)
  waiting for transfers between devices  53.8 us (24%)
  starting transfers between devices  28.1 us (13%)
  other arithmetic  27 us (12%)
  local copies, waits for them, and re-layouts  21.6 us (10%)
  matrix products  21.4 us (10%)
    pallas_call x3, Pallas kernels, cholesky_inverse(): pl.pallas_call(cholesky_inverse_kernel, out_shape=jax.ShapeDtypeStruct((o...  40.1 us
    all_to_all x1, waiting for transfers between devices, on_device(): loads.append(lax.all_to_all(load, 'leaf', 0, 0, tiled=True))  36 us
    pallas_call x1, Pallas kernels, extend_add(): pl.pallas_call(kernel, grid_spec=pltpu.PrefetchScalarGridSpec(num_scalar_...  25.1 us
    dot_general x1, matrix products, on_device(): jnp.einsum('pck,cbik->cbpi', probe_cut, updates, preferred_element_type=j...  10.1 us
    ppermute x9, starting transfers between devices, gather_rows(): pieces.append(lax.ppermute(block, axis, route))  9.07 us
    all_to_all x1, starting transfers between devices, on_device(): loads.append(lax.all_to_all(load, 'leaf', 0, 0, tiled=True))  8.76 us
    ppermute x3, waiting for transfers between devices, exchange_shares(): got.append(lax.ppermute(outgoing, axis, route))  7.69 us
    ppermute x9, waiting for transfers between devices, gather_rows(): pieces.append(lax.ppermute(block, axis, route))  7.07 us
  transfers between devices with their start and end apart: 15, of which 11 were waited for; matrix products, arithmetic and copies ran while one was open for 10% of the time, Pallas kernels for 11%

profile of v7, /device:TPU:1, one launch (start us, length us, event | category | flops | bytes accessed | tf_op | source)
XLA Modules:
  0.0 218.8 jit_solution(1620168741551550285)
XLA Ops:
  4.7 3.7 %copy.38 = bf16[8,8,32,512]{3,2,1,0:T(8,128)(2,1)} copy(bf16[8,8,32,512]{3,1,2,0:T(8,128)(2,1)} %bitcast.148) | data formatting | bytes 4194304
  9.1 10.1 %fusion.2 = bf16[32,4,128,64]{2,3,1,0:T(8,128)(2,1)} fusion(bf16[32,4,128,512]{3,2,1,0:T(8,128)(2,1)} %bitcast.176, bf16[64,32,512,1]{2,1,0,3:T(8,128)(2,1)} %bitcast.149), kind=kOutput, calls=%fused_computation.13 | convolution fusion | flops 1074790400 | bytes 20971520 | tf_op jit(solution)/shard_map/pck,cbik->cbpi/dot_general | solution.py:216
  19.3 4.6 %gather_fusion = bf16[256,64,128]{2,1,0:T(8,128)(2,1)} fusion(bf16[128,64,128]{2,1,0:T(8,128)(2,1)} %bitcast.147, s32[1024]{0:T(1024)S(1)} %pad_clamp_fusion.2), kind=kCustom, calls=%fused_computation | custom fusion | bytes 8389632 | tf_op jit(solution)/shard_map/jit(_take)/gather | solution.py:232
  24.0 6.1 %bitcast_select_fusion = bf16[32,512,128]{2,1,0:T(8,128)(2,1)S(1)} fusion(pred[32,512]{1,0:T(8,128)(4,1)S(1)} %broadcast_in_dim.152, bf16[32,512,128]{2,1,0:T(8,128)(2,1)} %bitcast.146), kind=kLoop, calls=%fused_computation.10 | loop fusion | flops 2097152 | bytes 8404992 | tf_op jit(solution)/shard_map/jit(_take)/select_n | solution.py:232
  30.1 2.2 %pad_maximum_fusion = bf16[32,528,128]{2,1,0:T(8,128)(2,1)} fusion(bf16[32,8,128]{2,1,0:T(8,128)(2,1)S(1)} %get-tuple-element.21, bf16[32,8,128]{2,1,0:T(8,128)(2,1)S(1)} %get-tuple-element.20, bf16[32,512,128]{2,1,0:T(8,128)(2,1)S(1)} %bitcast_select_fusion), kind=kLoop, calls=%fused_computation.9 | loop fusion | flops 12976128 | bytes 8650752 | tf_op jit(solution)/shard_map/concatenate | solution.py:247
  32.4 8.8 %all-to-all-start = ((bf16[32,528,128]{2,1,0:T(8,128)(2,1)}), bf16[32,528,128]{2,1,0:T(8,128)(2,1)}, u32[]{:S(2)}, u32[]{:S(2)}) async-start(bf16[32,528,128]{2,1,0:T(8,128)(2,1)} %pad_maximum_fusion), calls=%async_computation | async-start | bytes 8650752 | tf_op jit(solution)/shard_map/all_to_all | solution.py:250
  41.2 3.8 %collective-permute-start.5 = (f32[64,128]{1,0:T(8,128)S(1)}, f32[64,128]{1,0:T(8,128)S(1)}, u32[]{:S(2)}, u32[]{:S(2)}) collective-permute-start(f32[64,128]{1,0:T(8,128)S(1)} %copy-done.6), channel_id=1, source_target_pairs={{0,3},{1,0},{2,1},{3,2},{4,7},{5,4},{6,5},{7,6},{8,11},{9,8},{10,9... | collective-permute-start | bytes 98312 | tf_op jit(solution)/shard_map/ppermute | solution.py:49
  46.6 2.9 %fusion.5 = f32[64,64,128]{2,1,0:T(8,128)} fusion(bf16[64,128,128]{2,1,0:T(8,128)(2,1)S(1)} %copy-done, bf16[64,64,128]{2,1,0:T(8,128)(2,1)S(1)} %gather_fusion.2, pred[64]{0:T(512)(128)(4,1)S(1)} %and_bitcast_fusion), kind=kOutput, calls=%fused_computation.18 | convolution fusion | flops 134742016 | bytes 5242944 | tf_op jit(solution)/shard_map/eik,pek->pei/dot_general | solution.py:254
  49.5 7.0 %scatter_fusion = f32[64,16,128]{2,0,1:T(8,128)S(1)} fusion(f32[64,16,128]{2,0,1:T(8,128)S(1)} %broadcast_in_dim.158, s32[64]{0:T(128)S(1)} %get-tuple-element.23, f32[64,64,128]{2,1,0:T(8,128)} %fusion.5), kind=kCustom, calls=%fused_computation.8 | custom fusion | flops 524288 | bytes 6291712 | tf_op jit(solution)/shard_map/scatter-add | solution.py:258
  58.8 36.0 %all-to-all-done.load_ref = bf16[32,528,128]{2,1,0:T(8,128)(2,1)} async-done(((bf16[32,528,128]{2,1,0:T(8,128)(2,1)}), bf16[32,528,128]{2,1,0:T(8,128)(2,1)}, u32[]{:S(2)}, u32[]{:S(2)}) %all-to-all-start) | async-done | bytes 4325408 | tf_op jit(solution)/shard_map/all_to_all | solution.py:250
  94.8 2.0 fusion.36.count_ref
  96.8 25.1 %shard_map.138 = f32[256,512]{1,0:T(8,128)} custom-call(s32[32]{0:T(128)} %fusion.36.count_ref, bf16[32,528,128]{2,1,0:T(8,128)(2,1)} %all-to-all-done.load_ref, f32[256,512]{1,0:T(8,128)} %bitcast.151), custom_call_target="tpu_custom_call" | custom-call | tf_op jit(solution)/shard_map/pallas_call | solution.py:94
  121.9 1.1 select_bitcast_fusion.3
  123.0 3.8 %collective-permute-start.2 = (f32[64,512]{1,0:T(8,128)S(1)}, f32[64,512]{1,0:T(8,128)S(1)}, u32[]{:S(2)}, u32[]{:S(2)}) collective-permute-start(f32[64,512]{1,0:T(8,128)S(1)} %get-tuple-element.17), channel_id=1, source_target_pairs={{0,3},{1,0},{2,1},{3,2},{4,7},{5,4},{6,5},{7,6},{8,11},{9,8},{10,9... | collective-permute-start | bytes 393224 | tf_op jit(solution)/shard_map/ppermute | solution.py:117
  128.3 4.1 %collective-permute-done.2 = f32[64,512]{1,0:T(8,128)S(1)} collective-permute-done((f32[64,512]{1,0:T(8,128)S(1)}, f32[64,512]{1,0:T(8,128)S(1)}, u32[]{:S(2)}, u32[]{:S(2)}) %collective-permute-start.2) | collective-permute-done | bytes 131104 | tf_op jit(solution)/shard_map/ppermute | solution.py:117
  132.4 3.5 %collective-permute-done = f32[64,512]{1,0:T(8,128)S(1)} collective-permute-done((f32[64,512]{1,0:T(8,128)S(1)}, f32[64,512]{1,0:T(8,128)S(1)}, u32[]{:S(2)}, u32[]{:S(2)}) %collective-permute-start) | collective-permute-done | bytes 131104 | tf_op jit(solution)/shard_map/ppermute | solution.py:117
  140.1 1.4 collective-permute-start.6
  141.5 1.5 collective-permute-done.8
  143.1 1.6 collective-permute-done.7
  148.7 13.4 %shard_map.139 = f32[128,128]{1,0:T(8,128)} custom-call(f32[128,128]{1,0:T(8,128)} %fusion.30.gram_ref), custom_call_target="tpu_custom_call" | custom-call | tf_op jit(solution)/shard_map/pallas_call | solution.py:159
  162.1 1.2 convolution_select_fusion
  164.0 2.4 %collective-permute-start.11 = (f32[1,256,128]{2,1,0:T(8,128)S(1)}, f32[1,256,128]{2,1,0:T(8,128)S(1)}, u32[]{:S(2)}, u32[]{:S(2)}) collective-permute-start(f32[1,256,128]{2,1,0:T(8,128)S(1)} %bitcast.153), channel_id=1, source_target_pairs={{0,3},{1,0},{2,1},{3,2},{4,7},{5,4},{6,5},{7,6},{8,11},{9,8},{10,9... | collective-permute-start | bytes 393224 | tf_op jit(solution)/shard_map/ppermute | solution.py:49
  167.0 1.2 dynamic_slice.15
  168.3 1.3 dynamic_slice.17
  170.5 1.3 collective-permute-done.10
  171.8 1.5 collective-permute-done.9
  174.1 3.4 %collective-permute-start.12 = (f32[256,128]{1,0:T(8,128)S(1)}, f32[256,128]{1,0:T(8,128)S(1)}, u32[]{:S(2)}, u32[]{:S(2)}) collective-permute-start(f32[256,128]{1,0:T(8,128)S(1)} %fusion.21), channel_id=1, source_target_pairs={{0,4},{4,0},{8,12},{12,8},{16,20},{20,16},{24,28},{28,24},{32,36},... | collective-permute-start | bytes 393224 | tf_op jit(solution)/shard_map/ppermute | solution.py:22
  180.2 13.4 %shard_map.140 = f32[128,128]{1,0:T(8,128)} custom-call(f32[128,128]{1,0:T(8,128)} %fusion.32.gram_ref), custom_call_target="tpu_custom_call" | custom-call | tf_op jit(solution)/shard_map/pallas_call | solution.py:159
  195.1 2.3 %collective-permute-start.13 = (f32[256,128]{0,1:T(8,128)S(1)}, f32[256,128]{0,1:T(8,128)S(1)}, u32[]{:S(2)}, u32[]{:S(2)}) collective-permute-start(f32[256,128]{0,1:T(8,128)S(1)} %fusion.15), channel_id=1, source_target_pairs={{0,8},{8,0},{4,12},{12,4},{16,24},{24,16},{20,28},{28,20},{32,40},... | collective-permute-start | bytes 393224 | tf_op jit(solution)/shard_map/ppermute | solution.py:22
  198.8 2.2 %collective-permute-done.13 = f32[256,128]{0,1:T(8,128)S(1)} collective-permute-done((f32[256,128]{0,1:T(8,128)S(1)}, f32[256,128]{0,1:T(8,128)S(1)}, u32[]{:S(2)}, u32[]{:S(2)}) %collective-permute-start.13) | collective-permute-done | bytes 131104 | tf_op jit(solution)/shard_map/ppermute | solution.py:22
  202.5 13.3 %shard_map.141 = f32[128,128]{1,0:T(8,128)} custom-call(f32[128,128]{1,0:T(8,128)} %fusion.31.gram_ref), custom_call_target="tpu_custom_call" | custom-call | tf_op jit(solution)/shard_map/pallas_call | solution.py:159
  215.8 1.1 convolution_select_fusion.1
  (97 shorter events, 29.5 us)
Async XLA Ops:
  0.6 45.9 %copy-start = (bf16[64,128,128]{2,1,0:T(8,128)(2,1)S(1)}, bf16[64,128,128]{2,1,0:T(8,128)(2,1)}, u32[]{:S(2)}) copy-start(bf16[64,128,128]{2,1,0:T(8,128)(2,1)} %param.17) | copy-start | bytes 6291460
  0.6 7.8 %copy-start.1 = (s32[128,128]{1,0:T(8,128)S(1)}, s32[128,128]{1,0:T(8,128)}, u32[]{:S(2)}) copy-start(s32[128,128]{1,0:T(8,128)} %param.16) | copy-start | bytes 196612
  32.4 8.8 %copy-start.6 = (f32[64,128]{1,0:T(8,128)S(1)}, f32[64,128]{1,0:T(8,128)}, u32[]{:S(2)}) copy-start(f32[64,128]{1,0:T(8,128)} %param.20) | copy-start | bytes 98308
  32.4 13.3 %copy-start.7 = (s32[64,2]{0,1:T(2,128)S(1)}, s32[64,2]{0,1:T(2,128)}, u32[]{:S(2)}) copy-start(s32[64,2]{0,1:T(2,128)} %param.18) | copy-start | bytes 1540
  32.4 13.3 %copy-start.3 = (bf16[64,2048]{1,0:T(8,128)(2,1)S(1)}, bf16[64,2048]{1,0:T(8,128)(2,1)}, u32[]{:S(2)}) copy-start(bf16[64,2048]{1,0:T(8,128)(2,1)} %param.19) | copy-start | bytes 786436
  32.4 62.4 %all-to-all-start = ((bf16[32,528,128]{2,1,0:T(8,128)(2,1)}), bf16[32,528,128]{2,1,0:T(8,128)(2,1)}, u32[]{:S(2)}, u32[]{:S(2)}) async-start(bf16[32,528,128]{2,1,0:T(8,128)(2,1)} %pad_maximum_fusion), calls=%async_computation | async-start | bytes 8650752 | tf_op jit(solution)/shard_map/all_to_all | solution.py:250
  41.2 85.7 %collective-permute-start.5 = (f32[64,128]{1,0:T(8,128)S(1)}, f32[64,128]{1,0:T(8,128)S(1)}, u32[]{:S(2)}, u32[]{:S(2)}) collective-permute-start(f32[64,128]{1,0:T(8,128)S(1)} %copy-done.6), channel_id=1, source_target_pairs={{0,3},{1,0},{2,1},{3,2},{4,7},{5,4},{6,5},{7,6},{8,11},{9,8},{10,9... | collective-permute-start | bytes 98312 | tf_op jit(solution)/shard_map/ppermute | solution.py:49
  45.0 82.7 %collective-permute-start.4 = (f32[64,128]{1,0:T(8,128)S(1)}, f32[64,128]{1,0:T(8,128)S(1)}, u32[]{:S(2)}, u32[]{:S(2)}) collective-permute-start(f32[64,128]{1,0:T(8,128)S(1)} %copy-done.6), channel_id=1, source_target_pairs={{0,2},{1,3},{2,0},{3,1},{4,6},{5,7},{6,4},{7,5},{8,10},{9,11},{10,... | collective-permute-start | bytes 98312 | tf_op jit(solution)/shard_map/ppermute | solution.py:49
  45.0 82.7 %collective-permute-start.3 = (f32[64,128]{1,0:T(8,128)S(1)}, f32[64,128]{1,0:T(8,128)S(1)}, u32[]{:S(2)}, u32[]{:S(2)}) collective-permute-start(f32[64,128]{1,0:T(8,128)S(1)} %copy-done.6), channel_id=1, source_target_pairs={{0,1},{1,2},{2,3},{3,0},{4,5},{5,6},{6,7},{7,4},{8,9},{9,10},{10,1... | collective-permute-start | bytes 98312 | tf_op jit(solution)/shard_map/ppermute | solution.py:49
  123.0 9.4 %collective-permute-start.2 = (f32[64,512]{1,0:T(8,128)S(1)}, f32[64,512]{1,0:T(8,128)S(1)}, u32[]{:S(2)}, u32[]{:S(2)}) collective-permute-start(f32[64,512]{1,0:T(8,128)S(1)} %get-tuple-element.17), channel_id=1, source_target_pairs={{0,3},{1,0},{2,1},{3,2},{4,7},{5,4},{6,5},{7,6},{8,11},{9,8},{10,9... | collective-permute-start | bytes 393224 | tf_op jit(solution)/shard_map/ppermute | solution.py:117
  126.8 5.6 %collective-permute-start.1 = (f32[64,512]{1,0:T(8,128)S(1)}, f32[64,512]{1,0:T(8,128)S(1)}, u32[]{:S(2)}, u32[]{:S(2)}) collective-permute-start(f32[64,512]{1,0:T(8,128)S(1)} %get-tuple-element.18), channel_id=1, source_target_pairs={{0,2},{1,3},{2,0},{3,1},{4,6},{5,7},{6,4},{7,5},{8,10},{9,11},{10,... | collective-permute-start | bytes 393224 | tf_op jit(solution)/shard_map/ppermute | solution.py:117
  126.8 9.1 %collective-permute-start = (f32[64,512]{1,0:T(8,128)S(1)}, f32[64,512]{1,0:T(8,128)S(1)}, u32[]{:S(2)}, u32[]{:S(2)}) collective-permute-start(f32[64,512]{1,0:T(8,128)S(1)} %get-tuple-element.19), channel_id=1, source_target_pairs={{0,1},{1,2},{2,3},{3,0},{4,5},{5,6},{6,7},{7,4},{8,9},{9,10},{10,1... | collective-permute-start | bytes 393224 | tf_op jit(solution)/shard_map/ppermute | solution.py:117
  132.4 3.6 %copy-start.4 = (f32[64,512]{1,0:T(8,128)}, f32[64,512]{1,0:T(8,128)S(1)}, u32[]{:S(2)}) copy-start(f32[64,512]{1,0:T(8,128)S(1)} %collective-permute-done.1) | copy-start | bytes 393220
  136.0 0.7 copy-start.5
  139.9 3.2 %collective-permute-start.8 = (f32[1,128,128]{2,1,0:T(8,128)S(1)}, f32[1,128,128]{2,1,0:T(8,128)S(1)}, u32[]{:S(2)}, u32[]{:S(2)}) collective-permute-start(f32[1,128,128]{2,1,0:T(8,128)S(1)} %bitcast.157), channel_id=1, source_target_pairs={{0,3},{1,0},{2,1},{3,2},{4,7},{5,4},{6,5},{7,6},{8,11},{9,8},{10,9... | collective-permute-start | bytes 196616 | tf_op jit(solution)/shard_map/ppermute | solution.py:49
  140.0 4.7 %collective-permute-start.7 = (f32[1,128,128]{2,1,0:T(8,128)S(1)}, f32[1,128,128]{2,1,0:T(8,128)S(1)}, u32[]{:S(2)}, u32[]{:S(2)}) collective-permute-start(f32[1,128,128]{2,1,0:T(8,128)S(1)} %bitcast.158), channel_id=1, source_target_pairs={{0,2},{1,3},{2,0},{3,1},{4,6},{5,7},{6,4},{7,5},{8,10},{9,11},{10,... | collective-permute-start | bytes 196616 | tf_op jit(solution)/shard_map/ppermute | solution.py:49
  140.1 5.4 %collective-permute-start.6 = (f32[1,128,128]{2,1,0:T(8,128)S(1)}, f32[1,128,128]{2,1,0:T(8,128)S(1)}, u32[]{:S(2)}, u32[]{:S(2)}) collective-permute-start(f32[1,128,128]{2,1,0:T(8,128)S(1)} %bitcast.159), channel_id=1, source_target_pairs={{0,1},{1,2},{2,3},{3,0},{4,5},{5,6},{6,7},{7,4},{8,9},{9,10},{10,1... | collective-permute-start | bytes 196616 | tf_op jit(solution)/shard_map/ppermute | solution.py:49
  163.3 0.7 copy-start.2
  164.0 6.5 %collective-permute-start.11 = (f32[1,256,128]{2,1,0:T(8,128)S(1)}, f32[1,256,128]{2,1,0:T(8,128)S(1)}, u32[]{:S(2)}, u32[]{:S(2)}) collective-permute-start(f32[1,256,128]{2,1,0:T(8,128)S(1)} %bitcast.153), channel_id=1, source_target_pairs={{0,3},{1,0},{2,1},{3,2},{4,7},{5,4},{6,5},{7,6},{8,11},{9,8},{10,9... | collective-permute-start | bytes 393224 | tf_op jit(solution)/shard_map/ppermute | solution.py:49
  166.4 5.4 %collective-permute-start.10 = (f32[1,256,128]{2,1,0:T(8,128)S(1)}, f32[1,256,128]{2,1,0:T(8,128)S(1)}, u32[]{:S(2)}, u32[]{:S(2)}) collective-permute-start(f32[1,256,128]{2,1,0:T(8,128)S(1)} %bitcast.154), channel_id=1, source_target_pairs={{0,2},{1,3},{2,0},{3,1},{4,6},{5,7},{6,4},{7,5},{8,10},{9,11},{10,... | collective-permute-start | bytes 393224 | tf_op jit(solution)/shard_map/ppermute | solution.py:49
  166.4 6.9 %collective-permute-start.9 = (f32[1,256,128]{2,1,0:T(8,128)S(1)}, f32[1,256,128]{2,1,0:T(8,128)S(1)}, u32[]{:S(2)}, u32[]{:S(2)}) collective-permute-start(f32[1,256,128]{2,1,0:T(8,128)S(1)} %bitcast.155), channel_id=1, source_target_pairs={{0,1},{1,2},{2,3},{3,0},{4,5},{5,6},{6,7},{7,4},{8,9},{9,10},{10,1... | collective-permute-start | bytes 393224 | tf_op jit(solution)/shard_map/ppermute | solution.py:49
  174.1 4.4 %collective-permute-start.12 = (f32[256,128]{1,0:T(8,128)S(1)}, f32[256,128]{1,0:T(8,128)S(1)}, u32[]{:S(2)}, u32[]{:S(2)}) collective-permute-start(f32[256,128]{1,0:T(8,128)S(1)} %fusion.21), channel_id=1, source_target_pairs={{0,4},{4,0},{8,12},{12,8},{16,20},{20,16},{24,28},{28,24},{32,36},... | collective-permute-start | bytes 393224 | tf_op jit(solution)/shard_map/ppermute | solution.py:22
  195.1 5.9 %collective-permute-start.13 = (f32[256,128]{0,1:T(8,128)S(1)}, f32[256,128]{0,1:T(8,128)S(1)}, u32[]{:S(2)}, u32[]{:S(2)}) collective-permute-start(f32[256,128]{0,1:T(8,128)S(1)} %fusion.15), channel_id=1, source_target_pairs={{0,8},{8,0},{4,12},{12,4},{16,24},{24,16},{20,28},{28,20},{32,40},... | collective-permute-start | bytes 393224 | tf_op jit(solution)/shard_map/ppermute | solution.py:22

commit v8 on v7

--- a/solution.py
+++ b/solution.py
@@ -105,6 +105,35 @@
         out_shape=jax.ShapeDtypeStruct(start.shape, jnp.float32),
         compiler_params=pltpu.CompilerParams(dimension_semantics=("arbitrary",)),
     )(counts, load, start)
+
+
+def pack_kernel(source_ref, sampled_ref, info_ref, out_ref, *, slots, probes):
+    dest = pl.program_id(0)
+    for slot in range(slots):
+        block = source_ref[dest * slots + slot]
+        out_ref[0, slot * probes:(slot + 1) * probes, :] = sampled_ref[block]
+    out_ref[0, slots * probes:, :] = info_ref[0]
+
+
+def pack_payload(source, sampled, info, slots):
+    blocks, probes, lanes = sampled.shape
+    dests = info.shape[0]
+    depth = slots * probes + info.shape[1]
+    kernel = functools.partial(pack_kernel, slots=slots, probes=probes)
+    return pl.pallas_call(
+        kernel,
+        grid_spec=pltpu.PrefetchScalarGridSpec(
+            num_scalar_prefetch=1,
+            grid=(dests,),
+            in_specs=[
+                pl.BlockSpec(sampled.shape, lambda d, s: (0, 0, 0)),
+                pl.BlockSpec((1,) + info.shape[1:], lambda d, s: (d, 0, 0)),
+            ],
+            out_specs=pl.BlockSpec((1, depth, lanes), lambda d, s: (d, 0, 0)),
+        ),
+        out_shape=jax.ShapeDtypeStruct((dests, depth, lanes), sampled.dtype),
+        compiler_params=pltpu.CompilerParams(dimension_semantics=("arbitrary",)),
+    )(source, sampled, info)
 
 
 def exchange_shares(block, axis):
@@ -229,13 +258,11 @@
     source = jnp.minimum(source, block_count - 1)
     high = jnp.where(filled[:, None], child_rows[source] // block_rows, -1)
     low = jnp.where(filled[:, None], child_rows[source] % block_rows, 0)
-    send_vals = jnp.take(sampled, source, axis=0)
     half = SLOT_CAP
     info_rows = 16
     loads = []
     for part in range(1):
         picked_slots = slice(part * half, (part + 1) * half)
-        vals = send_vals.reshape(leaf_count, SLOT_CAP, local_probes, block_rows)[:, picked_slots]
         info = jnp.concatenate(
             [
                 high.reshape(leaf_count, SLOT_CAP, block_rows)[:, picked_slots],
@@ -244,9 +271,7 @@
             ],
             axis=1,
         ).astype(jnp.bfloat16)
-        load = jnp.concatenate(
-            [vals.reshape(leaf_count, half * local_probes, block_rows), info], axis=1
-        )
+        load = pack_payload(source, sampled, info, half)
         loads.append(lax.all_to_all(load, "leaf", 0, 0, tiled=True))
 
     pieces = parent_probes.reshape(local_probes, front_rows // block_rows, block_rows)

time: 220 us -> 226 us (1.027)
  Pallas kernels: 65.1 us -> 81.8 us
  other arithmetic: 27 us -> 19.9 us
  local copies, waits for them, and re-layouts: 21.6 us -> 16.5 us
    pallas_call x0 -> x1, Pallas kernels: none -> 16.7 us  [pack_payload(): pl.pallas_call(kernel, grid_spec=pltpu.PrefetchScalarGridSpec(num_scalar_...]
    select_n x2 -> x1, other arithmetic: 6.09 us -> 0.57 us  [on_device(): high = jnp.where(filled[:, None], child_rows[source] // block_rows, -1)]
    gather x1 -> x0, local copies, waits for them, and re-layouts: 4.63 us -> none  [on_device(): send_vals = jnp.take(sampled, source, axis=0)]
  transfers between devices with their start and end apart: 15 -> 15, of which waited for: 11 -> 11; matrix products, arithmetic and copies ran while one was open for 10% -> 9% of each run, Pallas kernels for 11% -> 11%
where the time goes in v8:
time: 226 us; the launch traced here: 223 us
  Pallas kernels  81.8 us (36%)
  waiting for transfers between devices  53.8 us (24%)
  starting transfers between devices  28.2 us (12%)
  matrix products  21.5 us (10%)
  other arithmetic  19.9 us (9%)
  local copies, waits for them, and re-layouts  16.5 us (7%)
    pallas_call x3, Pallas kernels, cholesky_inverse(): pl.pallas_call(cholesky_inverse_kernel, out_shape=jax.ShapeDtypeStruct((o...  40.1 us
    all_to_all x1, waiting for transfers between devices, on_device(): loads.append(lax.all_to_all(load, 'leaf', 0, 0, tiled=True))  35.9 us
    pallas_call x1, Pallas kernels, extend_add(): pl.pallas_call(kernel, grid_spec=pltpu.PrefetchScalarGridSpec(num_scalar_...  25.1 us
    pallas_call x1, Pallas kernels, pack_payload(): pl.pallas_call(kernel, grid_spec=pltpu.PrefetchScalarGridSpec(num_scalar_...  16.7 us
    dot_general x1, matrix products, on_device(): jnp.einsum('pck,cbik->cbpi', probe_cut, updates, preferred_element_type=j...  10.1 us
    ppermute x9, starting transfers between devices, gather_rows(): pieces.append(lax.ppermute(block, axis, route))  9.18 us
    all_to_all x1, starting transfers between devices, on_device(): loads.append(lax.all_to_all(load, 'leaf', 0, 0, tiled=True))  8.77 us
    ppermute x3, waiting for transfers between devices, exchange_shares(): got.append(lax.ppermute(outgoing, axis, route))  7.69 us
  transfers between devices with their start and end apart: 15, of which 11 were waited for; matrix products, arithmetic and copies ran while one was open for 9% of the time, Pallas kernels for 11%

profile of v8, /device:TPU:1, one launch (start us, length us, event | category | flops | bytes accessed | tf_op | source)
XLA Modules:
  0.0 223.4 jit_solution(2113938638784838495)
XLA Ops:
  4.8 3.7 %copy.38 = bf16[8,8,32,512]{3,2,1,0:T(8,128)(2,1)} copy(bf16[8,8,32,512]{3,1,2,0:T(8,128)(2,1)} %bitcast.143) | data formatting | bytes 4194304
  8.6 10.1 %fusion.2 = bf16[32,4,128,64]{2,3,1,0:T(8,128)(2,1)} fusion(bf16[32,4,128,512]{3,2,1,0:T(8,128)(2,1)} %bitcast.172, bf16[64,32,512,1]{2,1,0,3:T(8,128)(2,1)} %bitcast.145), kind=kOutput, calls=%fused_computation.10 | convolution fusion | flops 1074790400 | bytes 20971520 | tf_op jit(solution)/shard_map/pck,cbik->cbpi/dot_general | solution.py:245
  20.3 16.7 %shard_map.138 = bf16[32,528,128]{2,1,0:T(8,128)(2,1)} custom-call(s32[256]{0:T(256)} %get-tuple-element.25.source_ref, bf16[128,64,128]{2,1,0:T(8,128)(2,1)} %bitcast.144, bf16[32,16,128]{2,1,0:T(8,128)(2,1)} %pad_maximum_fusion.1.info_ref), custom_call_target="tpu_custom_call" | custom-call | tf_op jit(solution)/shard_map/pallas_call | solution.py:123
  37.0 8.8 %all-to-all-start = ((bf16[32,528,128]{2,1,0:T(8,128)(2,1)}), bf16[32,528,128]{2,1,0:T(8,128)(2,1)}, u32[]{:S(2)}, u32[]{:S(2)}) async-start(bf16[32,528,128]{2,1,0:T(8,128)(2,1)} %shard_map.138), calls=%async_computation | async-start | bytes 8650752 | tf_op jit(solution)/shard_map/all_to_all | solution.py:275
  45.8 3.8 %collective-permute-start.5 = (f32[64,128]{1,0:T(8,128)S(1)}, f32[64,128]{1,0:T(8,128)S(1)}, u32[]{:S(2)}, u32[]{:S(2)}) collective-permute-start(f32[64,128]{1,0:T(8,128)S(1)} %copy-done.6), channel_id=1, source_target_pairs={{0,3},{1,0},{2,1},{3,2},{4,7},{5,4},{6,5},{7,6},{8,11},{9,8},{10,9... | collective-permute-start | bytes 98312 | tf_op jit(solution)/shard_map/ppermute | solution.py:49
  51.2 2.9 %fusion.5 = f32[64,64,128]{2,1,0:T(8,128)} fusion(bf16[64,128,128]{2,1,0:T(8,128)(2,1)S(1)} %copy-done, bf16[64,64,128]{2,1,0:T(8,128)(2,1)S(1)} %gather_fusion.1, pred[64]{0:T(512)(128)(4,1)S(1)} %and_bitcast_fusion), kind=kOutput, calls=%fused_computation.15 | convolution fusion | flops 134742016 | bytes 5242944 | tf_op jit(solution)/shard_map/eik,pek->pei/dot_general | solution.py:279
  54.1 7.0 %scatter_fusion = f32[64,16,128]{2,0,1:T(8,128)S(1)} fusion(f32[64,16,128]{2,0,1:T(8,128)S(1)} %broadcast_in_dim.137, s32[64]{0:T(128)S(1)} %get-tuple-element.23, f32[64,64,128]{2,1,0:T(8,128)} %fusion.5), kind=kCustom, calls=%fused_computation.7 | custom fusion | flops 524288 | bytes 6291712 | tf_op jit(solution)/shard_map/scatter-add | solution.py:283
  63.4 35.9 %all-to-all-done.load_ref = bf16[32,528,128]{2,1,0:T(8,128)(2,1)} async-done(((bf16[32,528,128]{2,1,0:T(8,128)(2,1)}), bf16[32,528,128]{2,1,0:T(8,128)(2,1)}, u32[]{:S(2)}, u32[]{:S(2)}) %all-to-all-start) | async-done | bytes 4325408 | tf_op jit(solution)/shard_map/all_to_all | solution.py:275
  99.4 2.0 fusion.36.count_ref
  101.4 25.1 %shard_map.139 = f32[256,512]{1,0:T(8,128)} custom-call(s32[32]{0:T(128)} %fusion.36.count_ref, bf16[32,528,128]{2,1,0:T(8,128)(2,1)} %all-to-all-done.load_ref, f32[256,512]{1,0:T(8,128)} %bitcast.147), custom_call_target="tpu_custom_call" | custom-call | tf_op jit(solution)/shard_map/pallas_call | solution.py:94
  126.5 1.1 select_bitcast_fusion.3
  127.6 3.8 %collective-permute-start.2 = (f32[64,512]{1,0:T(8,128)S(1)}, f32[64,512]{1,0:T(8,128)S(1)}, u32[]{:S(2)}, u32[]{:S(2)}) collective-permute-start(f32[64,512]{1,0:T(8,128)S(1)} %get-tuple-element.17), channel_id=1, source_target_pairs={{0,3},{1,0},{2,1},{3,2},{4,7},{5,4},{6,5},{7,6},{8,11},{9,8},{10,9... | collective-permute-start | bytes 393224 | tf_op jit(solution)/shard_map/ppermute | solution.py:146
  132.9 4.1 %collective-permute-done.2 = f32[64,512]{1,0:T(8,128)S(1)} collective-permute-done((f32[64,512]{1,0:T(8,128)S(1)}, f32[64,512]{1,0:T(8,128)S(1)}, u32[]{:S(2)}, u32[]{:S(2)}) %collective-permute-start.2) | collective-permute-done | bytes 131104 | tf_op jit(solution)/shard_map/ppermute | solution.py:146
  137.0 3.5 %collective-permute-done = f32[64,512]{1,0:T(8,128)S(1)} collective-permute-done((f32[64,512]{1,0:T(8,128)S(1)}, f32[64,512]{1,0:T(8,128)S(1)}, u32[]{:S(2)}, u32[]{:S(2)}) %collective-permute-start) | collective-permute-done | bytes 131104 | tf_op jit(solution)/shard_map/ppermute | solution.py:146
  142.8 1.1 convolution_bitcast_fusion
  144.7 1.4 collective-permute-start.6
  146.2 1.5 collective-permute-done.8
  147.7 1.6 collective-permute-done.7
  153.3 13.4 %shard_map.140 = f32[128,128]{1,0:T(8,128)} custom-call(f32[128,128]{1,0:T(8,128)} %fusion.30.gram_ref), custom_call_target="tpu_custom_call" | custom-call | tf_op jit(solution)/shard_map/pallas_call | solution.py:188
  166.7 1.2 convolution_select_fusion
  168.5 2.5 %collective-permute-start.11 = (f32[1,256,128]{2,1,0:T(8,128)S(1)}, f32[1,256,128]{2,1,0:T(8,128)S(1)}, u32[]{:S(2)}, u32[]{:S(2)}) collective-permute-start(f32[1,256,128]{2,1,0:T(8,128)S(1)} %bitcast.149), channel_id=1, source_target_pairs={{0,3},{1,0},{2,1},{3,2},{4,7},{5,4},{6,5},{7,6},{8,11},{9,8},{10,9... | collective-permute-start | bytes 393224 | tf_op jit(solution)/shard_map/ppermute | solution.py:49
  171.7 1.2 dynamic_slice.15
  172.9 1.3 dynamic_slice.17
  175.1 1.3 collective-permute-done.10
  176.4 1.5 collective-permute-done.9
  178.7 3.4 %collective-permute-start.12 = (f32[256,128]{1,0:T(8,128)S(1)}, f32[256,128]{1,0:T(8,128)S(1)}, u32[]{:S(2)}, u32[]{:S(2)}) collective-permute-start(f32[256,128]{1,0:T(8,128)S(1)} %fusion.21), channel_id=1, source_target_pairs={{0,4},{4,0},{8,12},{12,8},{16,20},{20,16},{24,28},{28,24},{32,36},... | collective-permute-start | bytes 393224 | tf_op jit(solution)/shard_map/ppermute | solution.py:22
  184.8 13.4 %shard_map.141 = f32[128,128]{1,0:T(8,128)} custom-call(f32[128,128]{1,0:T(8,128)} %fusion.32.gram_ref), custom_call_target="tpu_custom_call" | custom-call | tf_op jit(solution)/shard_map/pallas_call | solution.py:188
  198.2 1.1 convolution_select_fusion.2
  199.7 2.3 %collective-permute-start.13 = (f32[256,128]{0,1:T(8,128)S(1)}, f32[256,128]{0,1:T(8,128)S(1)}, u32[]{:S(2)}, u32[]{:S(2)}) collective-permute-start(f32[256,128]{0,1:T(8,128)S(1)} %fusion.15), channel_id=1, source_target_pairs={{0,8},{8,0},{4,12},{12,4},{16,24},{24,16},{20,28},{28,20},{32,40},... | collective-permute-start | bytes 393224 | tf_op jit(solution)/shard_map/ppermute | solution.py:22
  203.4 2.2 collective-permute-done.13
  207.1 13.3 %shard_map.142 = f32[128,128]{1,0:T(8,128)} custom-call(f32[128,128]{1,0:T(8,128)} %fusion.31.gram_ref), custom_call_target="tpu_custom_call" | custom-call | tf_op jit(solution)/shard_map/pallas_call | solution.py:188
  220.4 1.1 convolution_select_fusion.1
  (93 shorter events, 28.1 us)
Async XLA Ops:
  0.6 50.5 %copy-start = (bf16[64,128,128]{2,1,0:T(8,128)(2,1)S(1)}, bf16[64,128,128]{2,1,0:T(8,128)(2,1)}, u32[]{:S(2)}) copy-start(bf16[64,128,128]{2,1,0:T(8,128)(2,1)} %param.17) | copy-start | bytes 6291460
  8.5 10.2 %copy-start.1 = (s32[128,128]{1,0:T(8,128)S(1)}, s32[128,128]{1,0:T(8,128)}, u32[]{:S(2)}) copy-start(s32[128,128]{1,0:T(8,128)} %param.16) | copy-start | bytes 196612
  37.0 8.8 %copy-start.6 = (f32[64,128]{1,0:T(8,128)S(1)}, f32[64,128]{1,0:T(8,128)}, u32[]{:S(2)}) copy-start(f32[64,128]{1,0:T(8,128)} %param.20) | copy-start | bytes 98308
  37.0 13.3 %copy-start.7 = (s32[64,2]{0,1:T(2,128)S(1)}, s32[64,2]{0,1:T(2,128)}, u32[]{:S(2)}) copy-start(s32[64,2]{0,1:T(2,128)} %param.18) | copy-start | bytes 1540
  37.0 13.3 %copy-start.3 = (bf16[64,2048]{1,0:T(8,128)(2,1)S(1)}, bf16[64,2048]{1,0:T(8,128)(2,1)}, u32[]{:S(2)}) copy-start(bf16[64,2048]{1,0:T(8,128)(2,1)} %param.19) | copy-start | bytes 786436
  37.0 62.4 %all-to-all-start = ((bf16[32,528,128]{2,1,0:T(8,128)(2,1)}), bf16[32,528,128]{2,1,0:T(8,128)(2,1)}, u32[]{:S(2)}, u32[]{:S(2)}) async-start(bf16[32,528,128]{2,1,0:T(8,128)(2,1)} %shard_map.138), calls=%async_computation | async-start | bytes 8650752 | tf_op jit(solution)/shard_map/all_to_all | solution.py:275
  45.8 85.7 %collective-permute-start.5 = (f32[64,128]{1,0:T(8,128)S(1)}, f32[64,128]{1,0:T(8,128)S(1)}, u32[]{:S(2)}, u32[]{:S(2)}) collective-permute-start(f32[64,128]{1,0:T(8,128)S(1)} %copy-done.6), channel_id=1, source_target_pairs={{0,3},{1,0},{2,1},{3,2},{4,7},{5,4},{6,5},{7,6},{8,11},{9,8},{10,9... | collective-permute-start | bytes 98312 | tf_op jit(solution)/shard_map/ppermute | solution.py:49
  49.6 82.7 %collective-permute-start.4 = (f32[64,128]{1,0:T(8,128)S(1)}, f32[64,128]{1,0:T(8,128)S(1)}, u32[]{:S(2)}, u32[]{:S(2)}) collective-permute-start(f32[64,128]{1,0:T(8,128)S(1)} %copy-done.6), channel_id=1, source_target_pairs={{0,2},{1,3},{2,0},{3,1},{4,6},{5,7},{6,4},{7,5},{8,10},{9,11},{10,... | collective-permute-start | bytes 98312 | tf_op jit(solution)/shard_map/ppermute | solution.py:49
  49.6 82.7 %collective-permute-start.3 = (f32[64,128]{1,0:T(8,128)S(1)}, f32[64,128]{1,0:T(8,128)S(1)}, u32[]{:S(2)}, u32[]{:S(2)}) collective-permute-start(f32[64,128]{1,0:T(8,128)S(1)} %copy-done.6), channel_id=1, source_target_pairs={{0,1},{1,2},{2,3},{3,0},{4,5},{5,6},{6,7},{7,4},{8,9},{9,10},{10,1... | collective-permute-start | bytes 98312 | tf_op jit(solution)/shard_map/ppermute | solution.py:49
  127.6 9.4 %collective-permute-start.2 = (f32[64,512]{1,0:T(8,128)S(1)}, f32[64,512]{1,0:T(8,128)S(1)}, u32[]{:S(2)}, u32[]{:S(2)}) collective-permute-start(f32[64,512]{1,0:T(8,128)S(1)} %get-tuple-element.17), channel_id=1, source_target_pairs={{0,3},{1,0},{2,1},{3,2},{4,7},{5,4},{6,5},{7,6},{8,11},{9,8},{10,9... | collective-permute-start | bytes 393224 | tf_op jit(solution)/shard_map/ppermute | solution.py:146
  131.4 5.6 %collective-permute-start.1 = (f32[64,512]{1,0:T(8,128)S(1)}, f32[64,512]{1,0:T(8,128)S(1)}, u32[]{:S(2)}, u32[]{:S(2)}) collective-permute-start(f32[64,512]{1,0:T(8,128)S(1)} %get-tuple-element.18), channel_id=1, source_target_pairs={{0,2},{1,3},{2,0},{3,1},{4,6},{5,7},{6,4},{7,5},{8,10},{9,11},{10,... | collective-permute-start | bytes 393224 | tf_op jit(solution)/shard_map/ppermute | solution.py:146
  131.4 9.1 %collective-permute-start = (f32[64,512]{1,0:T(8,128)S(1)}, f32[64,512]{1,0:T(8,128)S(1)}, u32[]{:S(2)}, u32[]{:S(2)}) collective-permute-start(f32[64,512]{1,0:T(8,128)S(1)} %get-tuple-element.19), channel_id=1, source_target_pairs={{0,1},{1,2},{2,3},{3,0},{4,5},{5,6},{6,7},{7,4},{8,9},{9,10},{10,1... | collective-permute-start | bytes 393224 | tf_op jit(solution)/shard_map/ppermute | solution.py:146
  137.0 3.6 %copy-start.4 = (f32[64,512]{1,0:T(8,128)}, f32[64,512]{1,0:T(8,128)S(1)}, u32[]{:S(2)}) copy-start(f32[64,512]{1,0:T(8,128)S(1)} %collective-permute-done.1) | copy-start | bytes 393220
  140.6 0.7 copy-start.5
  144.5 3.2 %collective-permute-start.8 = (f32[1,128,128]{2,1,0:T(8,128)S(1)}, f32[1,128,128]{2,1,0:T(8,128)S(1)}, u32[]{:S(2)}, u32[]{:S(2)}) collective-permute-start(f32[1,128,128]{2,1,0:T(8,128)S(1)} %bitcast.153), channel_id=1, source_target_pairs={{0,3},{1,0},{2,1},{3,2},{4,7},{5,4},{6,5},{7,6},{8,11},{9,8},{10,9... | collective-permute-start | bytes 196616 | tf_op jit(solution)/shard_map/ppermute | solution.py:49
  144.6 4.7 %collective-permute-start.7 = (f32[1,128,128]{2,1,0:T(8,128)S(1)}, f32[1,128,128]{2,1,0:T(8,128)S(1)}, u32[]{:S(2)}, u32[]{:S(2)}) collective-permute-start(f32[1,128,128]{2,1,0:T(8,128)S(1)} %bitcast.154), channel_id=1, source_target_pairs={{0,2},{1,3},{2,0},{3,1},{4,6},{5,7},{6,4},{7,5},{8,10},{9,11},{10,... | collective-permute-start | bytes 196616 | tf_op jit(solution)/shard_map/ppermute | solution.py:49
  144.7 5.4 %collective-permute-start.6 = (f32[1,128,128]{2,1,0:T(8,128)S(1)}, f32[1,128,128]{2,1,0:T(8,128)S(1)}, u32[]{:S(2)}, u32[]{:S(2)}) collective-permute-start(f32[1,128,128]{2,1,0:T(8,128)S(1)} %bitcast.155), channel_id=1, source_target_pairs={{0,1},{1,2},{2,3},{3,0},{4,5},{5,6},{6,7},{7,4},{8,9},{9,10},{10,1... | collective-permute-start | bytes 196616 | tf_op jit(solution)/shard_map/ppermute | solution.py:49
  167.9 10.0 %copy-start.2 = (f32[512,128]{1,0:T(8,128)}, f32[512,128]{1,0:T(8,128)S(1)}, u32[]{:S(2)}) copy-start(f32[512,128]{1,0:T(8,128)S(1)} %convolution_select_fusion) | copy-start | bytes 786436
  168.5 6.6 %collective-permute-start.11 = (f32[1,256,128]{2,1,0:T(8,128)S(1)}, f32[1,256,128]{2,1,0:T(8,128)S(1)}, u32[]{:S(2)}, u32[]{:S(2)}) collective-permute-start(f32[1,256,128]{2,1,0:T(8,128)S(1)} %bitcast.149), channel_id=1, source_target_pairs={{0,3},{1,0},{2,1},{3,2},{4,7},{5,4},{6,5},{7,6},{8,11},{9,8},{10,9... | collective-permute-start | bytes 393224 | tf_op jit(solution)/shard_map/ppermute | solution.py:49
  171.0 5.4 %collective-permute-start.10 = (f32[1,256,128]{2,1,0:T(8,128)S(1)}, f32[1,256,128]{2,1,0:T(8,128)S(1)}, u32[]{:S(2)}, u32[]{:S(2)}) collective-permute-start(f32[1,256,128]{2,1,0:T(8,128)S(1)} %bitcast.150), channel_id=1, source_target_pairs={{0,2},{1,3},{2,0},{3,1},{4,6},{5,7},{6,4},{7,5},{8,10},{9,11},{10,... | collective-permute-start | bytes 393224 | tf_op jit(solution)/shard_map/ppermute | solution.py:49
  171.0 6.9 %collective-permute-start.9 = (f32[1,256,128]{2,1,0:T(8,128)S(1)}, f32[1,256,128]{2,1,0:T(8,128)S(1)}, u32[]{:S(2)}, u32[]{:S(2)}) collective-permute-start(f32[1,256,128]{2,1,0:T(8,128)S(1)} %bitcast.151), channel_id=1, source_target_pairs={{0,1},{1,2},{2,3},{3,0},{4,5},{5,6},{6,7},{7,4},{8,9},{9,10},{10,1... | collective-permute-start | bytes 393224 | tf_op jit(solution)/shard_map/ppermute | solution.py:49
  178.7 4.4 %collective-permute-start.12 = (f32[256,128]{1,0:T(8,128)S(1)}, f32[256,128]{1,0:T(8,128)S(1)}, u32[]{:S(2)}, u32[]{:S(2)}) collective-permute-start(f32[256,128]{1,0:T(8,128)S(1)} %fusion.21), channel_id=1, source_target_pairs={{0,4},{4,0},{8,12},{12,8},{16,20},{20,16},{24,28},{28,24},{32,36},... | collective-permute-start | bytes 393224 | tf_op jit(solution)/shard_map/ppermute | solution.py:22
  199.7 5.9 %collective-permute-start.13 = (f32[256,128]{0,1:T(8,128)S(1)}, f32[256,128]{0,1:T(8,128)S(1)}, u32[]{:S(2)}, u32[]{:S(2)}) collective-permute-start(f32[256,128]{0,1:T(8,128)S(1)} %fusion.15), channel_id=1, source_target_pairs={{0,8},{8,0},{4,12},{12,4},{16,24},{24,16},{20,28},{28,20},{32,40},... | collective-permute-start | bytes 393224 | tf_op jit(solution)/shard_map/ppermute | solution.py:22

commit v9 on v7

--- a/solution.py
+++ b/solution.py
@@ -53,7 +53,7 @@
     return stacked.reshape((count * block.shape[0],) + block.shape[1:])
 
 
-def extend_add_kernel(count_ref, load_ref, start_ref, out_ref, *, slots, probes):
+def extend_add_kernel(load_ref, start_ref, out_ref, *, slots, probes):
     source = pl.program_id(0)
     lanes = load_ref.shape[2]
     width = out_ref.shape[1]
@@ -64,8 +64,7 @@
     def _():
         out_ref[...] = start_ref[...]
 
-    @pl.when(count_ref[source] > 0)
-    def _():
+    def accumulate():
         spread, hot = [], []
         for slot in range(slots):
             high = load_ref[0, pl.ds(info + slot, 1), :].astype(jnp.float32).astype(jnp.int32)
@@ -87,24 +86,23 @@
             spread, hot, (((1,), (1,)), ((), ())), preferred_element_type=jnp.float32
         )
 
-
-def extend_add(load, counts, start, slots, probes):
+    accumulate()
+
+
+def extend_add(load, start, slots, probes):
     sources, depth, lanes = load.shape
     kernel = functools.partial(extend_add_kernel, slots=slots, probes=probes)
     return pl.pallas_call(
         kernel,
-        grid_spec=pltpu.PrefetchScalarGridSpec(
-            num_scalar_prefetch=1,
-            grid=(sources,),
-            in_specs=[
-                pl.BlockSpec((1, depth, lanes), lambda s, c: (s, 0, 0)),
-                pl.BlockSpec(start.shape, lambda s, c: (0, 0)),
-            ],
-            out_specs=pl.BlockSpec(start.shape, lambda s, c: (0, 0)),
-        ),
+        grid=(sources,),
+        in_specs=[
+            pl.BlockSpec((1, depth, lanes), lambda s: (s, 0, 0)),
+            pl.BlockSpec(start.shape, lambda s: (0, 0)),
+        ],
+        out_specs=pl.BlockSpec(start.shape, lambda s: (0, 0)),
         out_shape=jax.ShapeDtypeStruct(start.shape, jnp.float32),
         compiler_params=pltpu.CompilerParams(dimension_semantics=("arbitrary",)),
-    )(counts, load, start)
+    )(load, start)
 
 
 def exchange_shares(block, axis):
@@ -263,8 +261,7 @@
     spread = jnp.moveaxis(initial.reshape(local_probes, high_count, width), 1, 0)
     spread = spread.reshape(high_count * local_probes, width)
     for load in loads:
-        counts = jnp.sum(load[:, half * local_probes, :1] >= 0, axis=1).astype(jnp.int32)
-        spread = extend_add(load, counts, spread, half, local_probes)
+        spread = extend_add(load, spread, half, local_probes)
     spread = spread.reshape(high_count, local_probes, width)
     sample = jnp.moveaxis(spread, 0, 1).reshape(local_probes, front_rows)
 

time: 220 us -> 217 us (0.986)
  transfers between devices with their start and end apart: 15 -> 15, of which waited for: 11 -> 11; matrix products, arithmetic and copies ran while one was open for 10% -> 9% of each run, Pallas kernels for 11% -> 11%
where the time goes in v9:
time: 217 us; the launch traced here: 216 us
  Pallas kernels  64.4 us (30%)
  waiting for transfers between devices  54 us (25%)
  starting transfers between devices  28.1 us (13%)
  other arithmetic  24.9 us (11%)
  local copies, waits for them, and re-layouts  21.5 us (10%)
  matrix products  21.4 us (10%)
    pallas_call x3, Pallas kernels, cholesky_inverse(): pl.pallas_call(cholesky_inverse_kernel, out_shape=jax.ShapeDtypeStruct((o...  40.1 us
    all_to_all x1, waiting for transfers between devices, on_device(): loads.append(lax.all_to_all(load, 'leaf', 0, 0, tiled=True))  36 us
    pallas_call x1, Pallas kernels, extend_add(): pl.pallas_call(kernel, grid=(sources,), in_specs=[pl.BlockSpec((1, depth,...  24.3 us
    dot_general x1, matrix products, on_device(): jnp.einsum('pck,cbik->cbpi', probe_cut, updates, preferred_element_type=j...  10.1 us
    ppermute x9, starting transfers between devices, gather_rows(): pieces.append(lax.ppermute(block, axis, route))  9.08 us
    all_to_all x1, starting transfers between devices, on_device(): loads.append(lax.all_to_all(load, 'leaf', 0, 0, tiled=True))  8.75 us
    ppermute x3, waiting for transfers between devices, exchange_shares(): got.append(lax.ppermute(outgoing, axis, route))  7.69 us
    ppermute x9, waiting for transfers between devices, gather_rows(): pieces.append(lax.ppermute(block, axis, route))  7.14 us
  transfers between devices with their start and end apart: 15, of which 11 were waited for; matrix products, arithmetic and copies ran while one was open for 9% of the time, Pallas kernels for 11%

profile of v9, /device:TPU:1, one launch (start us, length us, event | category | flops | bytes accessed | tf_op | source)
XLA Modules:
  0.0 216.1 jit_solution(16639512786102051169)
XLA Ops:
  4.7 3.7 %copy.38 = bf16[8,8,32,512]{3,2,1,0:T(8,128)(2,1)} copy(bf16[8,8,32,512]{3,1,2,0:T(8,128)(2,1)} %bitcast.148) | data formatting | bytes 4194304
  9.1 10.1 %fusion.2 = bf16[32,4,128,64]{2,3,1,0:T(8,128)(2,1)} fusion(bf16[32,4,128,512]{3,2,1,0:T(8,128)(2,1)} %bitcast.176, bf16[64,32,512,1]{2,1,0,3:T(8,128)(2,1)} %bitcast.149), kind=kOutput, calls=%fused_computation.13 | convolution fusion | flops 1074790400 | bytes 20971520 | tf_op jit(solution)/shard_map/pck,cbik->cbpi/dot_general | solution.py:214
  19.2 4.6 %gather_fusion = bf16[256,64,128]{2,1,0:T(8,128)(2,1)} fusion(bf16[128,64,128]{2,1,0:T(8,128)(2,1)} %bitcast.147, s32[1024]{0:T(1024)S(1)} %pad_clamp_fusion.2), kind=kCustom, calls=%fused_computation | custom fusion | bytes 8389632 | tf_op jit(solution)/shard_map/jit(_take)/gather | solution.py:230
  24.0 6.1 %bitcast_select_fusion = bf16[32,512,128]{2,1,0:T(8,128)(2,1)S(1)} fusion(pred[32,512]{1,0:T(8,128)(4,1)S(1)} %broadcast_in_dim.152, bf16[32,512,128]{2,1,0:T(8,128)(2,1)} %bitcast.146), kind=kLoop, calls=%fused_computation.10 | loop fusion | flops 2097152 | bytes 8404992 | tf_op jit(solution)/shard_map/jit(_take)/select_n | solution.py:230
  30.1 2.2 %pad_maximum_fusion = bf16[32,528,128]{2,1,0:T(8,128)(2,1)} fusion(bf16[32,8,128]{2,1,0:T(8,128)(2,1)S(1)} %get-tuple-element.21, bf16[32,8,128]{2,1,0:T(8,128)(2,1)S(1)} %get-tuple-element.20, bf16[32,512,128]{2,1,0:T(8,128)(2,1)S(1)} %bitcast_select_fusion), kind=kLoop, calls=%fused_computation.9 | loop fusion | flops 12976128 | bytes 8650752 | tf_op jit(solution)/shard_map/concatenate | solution.py:245
  32.4 8.8 %all-to-all-start = ((bf16[32,528,128]{2,1,0:T(8,128)(2,1)}), bf16[32,528,128]{2,1,0:T(8,128)(2,1)}, u32[]{:S(2)}, u32[]{:S(2)}) async-start(bf16[32,528,128]{2,1,0:T(8,128)(2,1)} %pad_maximum_fusion), calls=%async_computation | async-start | bytes 8650752 | tf_op jit(solution)/shard_map/all_to_all | solution.py:248
  41.1 3.8 %collective-permute-start.5 = (f32[64,128]{1,0:T(8,128)S(1)}, f32[64,128]{1,0:T(8,128)S(1)}, u32[]{:S(2)}, u32[]{:S(2)}) collective-permute-start(f32[64,128]{1,0:T(8,128)S(1)} %copy-done.6), channel_id=1, source_target_pairs={{0,3},{1,0},{2,1},{3,2},{4,7},{5,4},{6,5},{7,6},{8,11},{9,8},{10,9... | collective-permute-start | bytes 98312 | tf_op jit(solution)/shard_map/ppermute | solution.py:49
  46.5 2.9 %fusion.5 = f32[64,64,128]{2,1,0:T(8,128)} fusion(bf16[64,128,128]{2,1,0:T(8,128)(2,1)S(1)} %copy-done, bf16[64,64,128]{2,1,0:T(8,128)(2,1)S(1)} %gather_fusion.2, pred[64]{0:T(512)(128)(4,1)S(1)} %and_bitcast_fusion), kind=kOutput, calls=%fused_computation.18 | convolution fusion | flops 134742016 | bytes 5242944 | tf_op jit(solution)/shard_map/eik,pek->pei/dot_general | solution.py:252
  49.5 7.0 %scatter_fusion = f32[64,16,128]{2,0,1:T(8,128)S(1)} fusion(f32[64,16,128]{2,0,1:T(8,128)S(1)} %broadcast_in_dim.158, s32[64]{0:T(128)S(1)} %get-tuple-element.23, f32[64,64,128]{2,1,0:T(8,128)} %fusion.5), kind=kCustom, calls=%fused_computation.8 | custom fusion | flops 524288 | bytes 6291712 | tf_op jit(solution)/shard_map/scatter-add | solution.py:256
  58.7 36.0 %all-to-all-done.load_ref = bf16[32,528,128]{2,1,0:T(8,128)(2,1)} async-done(((bf16[32,528,128]{2,1,0:T(8,128)(2,1)}), bf16[32,528,128]{2,1,0:T(8,128)(2,1)}, u32[]{:S(2)}, u32[]{:S(2)}) %all-to-all-start) | async-done | bytes 4325408 | tf_op jit(solution)/shard_map/all_to_all | solution.py:248
  94.8 24.3 %shard_map.138 = f32[256,512]{1,0:T(8,128)} custom-call(bf16[32,528,128]{2,1,0:T(8,128)(2,1)} %all-to-all-done.load_ref, f32[256,512]{1,0:T(8,128)} %bitcast.151), custom_call_target="tpu_custom_call" | custom-call | tf_op jit(solution)/shard_map/pallas_call | solution.py:95
  119.1 1.1 select_bitcast_fusion.3
  120.2 3.8 %collective-permute-start.2 = (f32[64,512]{1,0:T(8,128)S(1)}, f32[64,512]{1,0:T(8,128)S(1)}, u32[]{:S(2)}, u32[]{:S(2)}) collective-permute-start(f32[64,512]{1,0:T(8,128)S(1)} %get-tuple-element.17), channel_id=1, source_target_pairs={{0,3},{1,0},{2,1},{3,2},{4,7},{5,4},{6,5},{7,6},{8,11},{9,8},{10,9... | collective-permute-start | bytes 393224 | tf_op jit(solution)/shard_map/ppermute | solution.py:115
  125.5 4.1 %collective-permute-done.2 = f32[64,512]{1,0:T(8,128)S(1)} collective-permute-done((f32[64,512]{1,0:T(8,128)S(1)}, f32[64,512]{1,0:T(8,128)S(1)}, u32[]{:S(2)}, u32[]{:S(2)}) %collective-permute-start.2) | collective-permute-done | bytes 131104 | tf_op jit(solution)/shard_map/ppermute | solution.py:115
  129.7 3.5 %collective-permute-done = f32[64,512]{1,0:T(8,128)S(1)} collective-permute-done((f32[64,512]{1,0:T(8,128)S(1)}, f32[64,512]{1,0:T(8,128)S(1)}, u32[]{:S(2)}, u32[]{:S(2)}) %collective-permute-start) | collective-permute-done | bytes 131104 | tf_op jit(solution)/shard_map/ppermute | solution.py:115
  137.3 1.4 collective-permute-start.6
  138.8 1.5 collective-permute-done.8
  140.3 1.6 collective-permute-done.7
  146.0 13.4 %shard_map.139 = f32[128,128]{1,0:T(8,128)} custom-call(f32[128,128]{1,0:T(8,128)} %fusion.30.gram_ref), custom_call_target="tpu_custom_call" | custom-call | tf_op jit(solution)/shard_map/pallas_call | solution.py:157
  159.3 1.2 convolution_select_fusion
  161.3 2.4 %collective-permute-start.11 = (f32[1,256,128]{2,1,0:T(8,128)S(1)}, f32[1,256,128]{2,1,0:T(8,128)S(1)}, u32[]{:S(2)}, u32[]{:S(2)}) collective-permute-start(f32[1,256,128]{2,1,0:T(8,128)S(1)} %bitcast.153), channel_id=1, source_target_pairs={{0,3},{1,0},{2,1},{3,2},{4,7},{5,4},{6,5},{7,6},{8,11},{9,8},{10,9... | collective-permute-start | bytes 393224 | tf_op jit(solution)/shard_map/ppermute | solution.py:49
  164.3 1.2 dynamic_slice.15
  165.5 1.2 dynamic_slice.17
  167.7 1.3 collective-permute-done.10
  169.1 1.5 collective-permute-done.9
  171.4 3.4 %collective-permute-start.12 = (f32[256,128]{1,0:T(8,128)S(1)}, f32[256,128]{1,0:T(8,128)S(1)}, u32[]{:S(2)}, u32[]{:S(2)}) collective-permute-start(f32[256,128]{1,0:T(8,128)S(1)} %fusion.21), channel_id=1, source_target_pairs={{0,4},{4,0},{8,12},{12,8},{16,20},{20,16},{24,28},{28,24},{32,36},... | collective-permute-start | bytes 393224 | tf_op jit(solution)/shard_map/ppermute | solution.py:22
  177.5 13.4 %shard_map.140 = f32[128,128]{1,0:T(8,128)} custom-call(f32[128,128]{1,0:T(8,128)} %fusion.32.gram_ref), custom_call_target="tpu_custom_call" | custom-call | tf_op jit(solution)/shard_map/pallas_call | solution.py:157
  190.8 1.1 convolution_select_fusion.2
  192.4 2.3 %collective-permute-start.13 = (f32[256,128]{0,1:T(8,128)S(1)}, f32[256,128]{0,1:T(8,128)S(1)}, u32[]{:S(2)}, u32[]{:S(2)}) collective-permute-start(f32[256,128]{0,1:T(8,128)S(1)} %fusion.15), channel_id=1, source_target_pairs={{0,8},{8,0},{4,12},{12,4},{16,24},{24,16},{20,28},{28,20},{32,40},... | collective-permute-start | bytes 393224 | tf_op jit(solution)/shard_map/ppermute | solution.py:22
  195.9 2.3 %collective-permute-done.13 = f32[256,128]{0,1:T(8,128)S(1)} collective-permute-done((f32[256,128]{0,1:T(8,128)S(1)}, f32[256,128]{0,1:T(8,128)S(1)}, u32[]{:S(2)}, u32[]{:S(2)}) %collective-permute-start.13) | collective-permute-done | bytes 131104 | tf_op jit(solution)/shard_map/ppermute | solution.py:22
  199.7 13.4 %shard_map.141 = f32[128,128]{1,0:T(8,128)} custom-call(f32[128,128]{1,0:T(8,128)} %fusion.31.gram_ref), custom_call_target="tpu_custom_call" | custom-call | tf_op jit(solution)/shard_map/pallas_call | solution.py:157
  213.1 1.1 convolution_select_fusion.1
  (96 shorter events, 28.3 us)
Async XLA Ops:
  0.6 45.9 %copy-start = (bf16[64,128,128]{2,1,0:T(8,128)(2,1)S(1)}, bf16[64,128,128]{2,1,0:T(8,128)(2,1)}, u32[]{:S(2)}) copy-start(bf16[64,128,128]{2,1,0:T(8,128)(2,1)} %param.17) | copy-start | bytes 6291460
  0.6 7.8 %copy-start.1 = (s32[128,128]{1,0:T(8,128)S(1)}, s32[128,128]{1,0:T(8,128)}, u32[]{:S(2)}) copy-start(s32[128,128]{1,0:T(8,128)} %param.16) | copy-start | bytes 196612
  32.3 8.8 %copy-start.6 = (f32[64,128]{1,0:T(8,128)S(1)}, f32[64,128]{1,0:T(8,128)}, u32[]{:S(2)}) copy-start(f32[64,128]{1,0:T(8,128)} %param.20) | copy-start | bytes 98308
  32.3 13.3 %copy-start.7 = (s32[64,2]{0,1:T(2,128)S(1)}, s32[64,2]{0,1:T(2,128)}, u32[]{:S(2)}) copy-start(s32[64,2]{0,1:T(2,128)} %param.18) | copy-start | bytes 1540
  32.4 13.3 %copy-start.3 = (bf16[64,2048]{1,0:T(8,128)(2,1)S(1)}, bf16[64,2048]{1,0:T(8,128)(2,1)}, u32[]{:S(2)}) copy-start(bf16[64,2048]{1,0:T(8,128)(2,1)} %param.19) | copy-start | bytes 786436
  32.4 62.4 %all-to-all-start = ((bf16[32,528,128]{2,1,0:T(8,128)(2,1)}), bf16[32,528,128]{2,1,0:T(8,128)(2,1)}, u32[]{:S(2)}, u32[]{:S(2)}) async-start(bf16[32,528,128]{2,1,0:T(8,128)(2,1)} %pad_maximum_fusion), calls=%async_computation | async-start | bytes 8650752 | tf_op jit(solution)/shard_map/all_to_all | solution.py:248
  41.1 82.9 %collective-permute-start.5 = (f32[64,128]{1,0:T(8,128)S(1)}, f32[64,128]{1,0:T(8,128)S(1)}, u32[]{:S(2)}, u32[]{:S(2)}) collective-permute-start(f32[64,128]{1,0:T(8,128)S(1)} %copy-done.6), channel_id=1, source_target_pairs={{0,3},{1,0},{2,1},{3,2},{4,7},{5,4},{6,5},{7,6},{8,11},{9,8},{10,9... | collective-permute-start | bytes 98312 | tf_op jit(solution)/shard_map/ppermute | solution.py:49
  44.9 80.0 %collective-permute-start.4 = (f32[64,128]{1,0:T(8,128)S(1)}, f32[64,128]{1,0:T(8,128)S(1)}, u32[]{:S(2)}, u32[]{:S(2)}) collective-permute-start(f32[64,128]{1,0:T(8,128)S(1)} %copy-done.6), channel_id=1, source_target_pairs={{0,2},{1,3},{2,0},{3,1},{4,6},{5,7},{6,4},{7,5},{8,10},{9,11},{10,... | collective-permute-start | bytes 98312 | tf_op jit(solution)/shard_map/ppermute | solution.py:49
  44.9 80.0 %collective-permute-start.3 = (f32[64,128]{1,0:T(8,128)S(1)}, f32[64,128]{1,0:T(8,128)S(1)}, u32[]{:S(2)}, u32[]{:S(2)}) collective-permute-start(f32[64,128]{1,0:T(8,128)S(1)} %copy-done.6), channel_id=1, source_target_pairs={{0,1},{1,2},{2,3},{3,0},{4,5},{5,6},{6,7},{7,4},{8,9},{9,10},{10,1... | collective-permute-start | bytes 98312 | tf_op jit(solution)/shard_map/ppermute | solution.py:49
  120.2 9.4 %collective-permute-start.2 = (f32[64,512]{1,0:T(8,128)S(1)}, f32[64,512]{1,0:T(8,128)S(1)}, u32[]{:S(2)}, u32[]{:S(2)}) collective-permute-start(f32[64,512]{1,0:T(8,128)S(1)} %get-tuple-element.17), channel_id=1, source_target_pairs={{0,3},{1,0},{2,1},{3,2},{4,7},{5,4},{6,5},{7,6},{8,11},{9,8},{10,9... | collective-permute-start | bytes 393224 | tf_op jit(solution)/shard_map/ppermute | solution.py:115
  124.1 5.6 %collective-permute-start.1 = (f32[64,512]{1,0:T(8,128)S(1)}, f32[64,512]{1,0:T(8,128)S(1)}, u32[]{:S(2)}, u32[]{:S(2)}) collective-permute-start(f32[64,512]{1,0:T(8,128)S(1)} %get-tuple-element.18), channel_id=1, source_target_pairs={{0,2},{1,3},{2,0},{3,1},{4,6},{5,7},{6,4},{7,5},{8,10},{9,11},{10,... | collective-permute-start | bytes 393224 | tf_op jit(solution)/shard_map/ppermute | solution.py:115
  124.1 9.1 %collective-permute-start = (f32[64,512]{1,0:T(8,128)S(1)}, f32[64,512]{1,0:T(8,128)S(1)}, u32[]{:S(2)}, u32[]{:S(2)}) collective-permute-start(f32[64,512]{1,0:T(8,128)S(1)} %get-tuple-element.19), channel_id=1, source_target_pairs={{0,1},{1,2},{2,3},{3,0},{4,5},{5,6},{6,7},{7,4},{8,9},{9,10},{10,1... | collective-permute-start | bytes 393224 | tf_op jit(solution)/shard_map/ppermute | solution.py:115
  129.7 3.6 %copy-start.4 = (f32[64,512]{1,0:T(8,128)}, f32[64,512]{1,0:T(8,128)S(1)}, u32[]{:S(2)}) copy-start(f32[64,512]{1,0:T(8,128)S(1)} %collective-permute-done.1) | copy-start | bytes 393220
  133.2 0.7 copy-start.5
  137.1 3.2 %collective-permute-start.8 = (f32[1,128,128]{2,1,0:T(8,128)S(1)}, f32[1,128,128]{2,1,0:T(8,128)S(1)}, u32[]{:S(2)}, u32[]{:S(2)}) collective-permute-start(f32[1,128,128]{2,1,0:T(8,128)S(1)} %bitcast.157), channel_id=1, source_target_pairs={{0,3},{1,0},{2,1},{3,2},{4,7},{5,4},{6,5},{7,6},{8,11},{9,8},{10,9... | collective-permute-start | bytes 196616 | tf_op jit(solution)/shard_map/ppermute | solution.py:49
  137.2 4.7 %collective-permute-start.7 = (f32[1,128,128]{2,1,0:T(8,128)S(1)}, f32[1,128,128]{2,1,0:T(8,128)S(1)}, u32[]{:S(2)}, u32[]{:S(2)}) collective-permute-start(f32[1,128,128]{2,1,0:T(8,128)S(1)} %bitcast.158), channel_id=1, source_target_pairs={{0,2},{1,3},{2,0},{3,1},{4,6},{5,7},{6,4},{7,5},{8,10},{9,11},{10,... | collective-permute-start | bytes 196616 | tf_op jit(solution)/shard_map/ppermute | solution.py:49
  137.3 5.4 %collective-permute-start.6 = (f32[1,128,128]{2,1,0:T(8,128)S(1)}, f32[1,128,128]{2,1,0:T(8,128)S(1)}, u32[]{:S(2)}, u32[]{:S(2)}) collective-permute-start(f32[1,128,128]{2,1,0:T(8,128)S(1)} %bitcast.159), channel_id=1, source_target_pairs={{0,1},{1,2},{2,3},{3,0},{4,5},{5,6},{6,7},{7,4},{8,9},{9,10},{10,1... | collective-permute-start | bytes 196616 | tf_op jit(solution)/shard_map/ppermute | solution.py:49
  160.5 0.7 copy-start.2
  161.3 6.5 %collective-permute-start.11 = (f32[1,256,128]{2,1,0:T(8,128)S(1)}, f32[1,256,128]{2,1,0:T(8,128)S(1)}, u32[]{:S(2)}, u32[]{:S(2)}) collective-permute-start(f32[1,256,128]{2,1,0:T(8,128)S(1)} %bitcast.153), channel_id=1, source_target_pairs={{0,3},{1,0},{2,1},{3,2},{4,7},{5,4},{6,5},{7,6},{8,11},{9,8},{10,9... | collective-permute-start | bytes 393224 | tf_op jit(solution)/shard_map/ppermute | solution.py:49
  163.6 5.4 %collective-permute-start.10 = (f32[1,256,128]{2,1,0:T(8,128)S(1)}, f32[1,256,128]{2,1,0:T(8,128)S(1)}, u32[]{:S(2)}, u32[]{:S(2)}) collective-permute-start(f32[1,256,128]{2,1,0:T(8,128)S(1)} %bitcast.154), channel_id=1, source_target_pairs={{0,2},{1,3},{2,0},{3,1},{4,6},{5,7},{6,4},{7,5},{8,10},{9,11},{10,... | collective-permute-start | bytes 393224 | tf_op jit(solution)/shard_map/ppermute | solution.py:49
  163.6 6.9 %collective-permute-start.9 = (f32[1,256,128]{2,1,0:T(8,128)S(1)}, f32[1,256,128]{2,1,0:T(8,128)S(1)}, u32[]{:S(2)}, u32[]{:S(2)}) collective-permute-start(f32[1,256,128]{2,1,0:T(8,128)S(1)} %bitcast.155), channel_id=1, source_target_pairs={{0,1},{1,2},{2,3},{3,0},{4,5},{5,6},{6,7},{7,4},{8,9},{9,10},{10,1... | collective-permute-start | bytes 393224 | tf_op jit(solution)/shard_map/ppermute | solution.py:49
  171.4 4.4 %collective-permute-start.12 = (f32[256,128]{1,0:T(8,128)S(1)}, f32[256,128]{1,0:T(8,128)S(1)}, u32[]{:S(2)}, u32[]{:S(2)}) collective-permute-start(f32[256,128]{1,0:T(8,128)S(1)} %fusion.21), channel_id=1, source_target_pairs={{0,4},{4,0},{8,12},{12,8},{16,20},{20,16},{24,28},{28,24},{32,36},... | collective-permute-start | bytes 393224 | tf_op jit(solution)/shard_map/ppermute | solution.py:22
  192.4 5.9 %collective-permute-start.13 = (f32[256,128]{0,1:T(8,128)S(1)}, f32[256,128]{0,1:T(8,128)S(1)}, u32[]{:S(2)}, u32[]{:S(2)}) collective-permute-start(f32[256,128]{0,1:T(8,128)S(1)} %fusion.15), channel_id=1, source_target_pairs={{0,8},{8,0},{4,12},{12,4},{16,24},{24,16},{20,28},{28,20},{32,40},... | collective-permute-start | bytes 393224 | tf_op jit(solution)/shard_map/ppermute | solution.py:22

commit v10 on v9

--- a/solution.py
+++ b/solution.py
@@ -121,7 +121,7 @@
 
 def cholesky_inverse_kernel(gram_ref, inverse_ref, work_ref, rest_ref):
     order = gram_ref.shape[0]
-    tile = 8
+    tile = 16
     sub = lax.broadcasted_iota(jnp.int32, (order, order), 0)
     lane = lax.broadcasted_iota(jnp.int32, (order, order), 1)
     lane_one = lax.broadcasted_iota(jnp.int32, (1, order), 1)

time: 217 us -> 218 us (level)
  no operation moved by 1% of the time
where the time goes in v10:
time: 218 us; the launch traced here: 216 us
  Pallas kernels  64.5 us (30%)
  waiting for transfers between devices  54 us (25%)
  starting transfers between devices  28.1 us (13%)
  other arithmetic  24.9 us (11%)
  local copies, waits for them, and re-layouts  21.5 us (10%)
  matrix products  21.4 us (10%)
    pallas_call x3, Pallas kernels, cholesky_inverse(): pl.pallas_call(cholesky_inverse_kernel, out_shape=jax.ShapeDtypeStruct((o...  40.2 us
    all_to_all x1, waiting for transfers between devices, on_device(): loads.append(lax.all_to_all(load, 'leaf', 0, 0, tiled=True))  36 us
    pallas_call x1, Pallas kernels, extend_add(): pl.pallas_call(kernel, grid=(sources,), in_specs=[pl.BlockSpec((1, depth,...  24.3 us
    dot_general x1, matrix products, on_device(): jnp.einsum('pck,cbik->cbpi', probe_cut, updates, preferred_element_type=j...  10.1 us
    ppermute x9, starting transfers between devices, gather_rows(): pieces.append(lax.ppermute(block, axis, route))  9.08 us
    all_to_all x1, starting transfers between devices, on_device(): loads.append(lax.all_to_all(load, 'leaf', 0, 0, tiled=True))  8.76 us
    ppermute x3, waiting for transfers between devices, exchange_shares(): got.append(lax.ppermute(outgoing, axis, route))  7.69 us
    ppermute x9, waiting for transfers between devices, gather_rows(): pieces.append(lax.ppermute(block, axis, route))  7.13 us
  transfers between devices with their start and end apart: 15, of which 11 were waited for; matrix products, arithmetic and copies ran while one was open for 9% of the time, Pallas kernels for 11%

profile of v10, /device:TPU:1, one launch (start us, length us, event | category | flops | bytes accessed | tf_op | source)
XLA Modules:
  0.0 216.2 jit_solution(13748969376555668029)
XLA Ops:
  4.7 3.7 %copy.38 = bf16[8,8,32,512]{3,2,1,0:T(8,128)(2,1)} copy(bf16[8,8,32,512]{3,1,2,0:T(8,128)(2,1)} %bitcast.148) | data formatting | bytes 4194304
  9.1 10.1 %fusion.2 = bf16[32,4,128,64]{2,3,1,0:T(8,128)(2,1)} fusion(bf16[32,4,128,512]{3,2,1,0:T(8,128)(2,1)} %bitcast.176, bf16[64,32,512,1]{2,1,0,3:T(8,128)(2,1)} %bitcast.149), kind=kOutput, calls=%fused_computation.13 | convolution fusion | flops 1074790400 | bytes 20971520 | tf_op jit(solution)/shard_map/pck,cbik->cbpi/dot_general | solution.py:214
  19.2 4.6 %gather_fusion = bf16[256,64,128]{2,1,0:T(8,128)(2,1)} fusion(bf16[128,64,128]{2,1,0:T(8,128)(2,1)} %bitcast.147, s32[1024]{0:T(1024)S(1)} %pad_clamp_fusion.2), kind=kCustom, calls=%fused_computation | custom fusion | bytes 8389632 | tf_op jit(solution)/shard_map/jit(_take)/gather | solution.py:230
  24.0 6.1 %bitcast_select_fusion = bf16[32,512,128]{2,1,0:T(8,128)(2,1)S(1)} fusion(pred[32,512]{1,0:T(8,128)(4,1)S(1)} %broadcast_in_dim.152, bf16[32,512,128]{2,1,0:T(8,128)(2,1)} %bitcast.146), kind=kLoop, calls=%fused_computation.10 | loop fusion | flops 2097152 | bytes 8404992 | tf_op jit(solution)/shard_map/jit(_take)/select_n | solution.py:230
  30.1 2.2 %pad_maximum_fusion = bf16[32,528,128]{2,1,0:T(8,128)(2,1)} fusion(bf16[32,8,128]{2,1,0:T(8,128)(2,1)S(1)} %get-tuple-element.21, bf16[32,8,128]{2,1,0:T(8,128)(2,1)S(1)} %get-tuple-element.20, bf16[32,512,128]{2,1,0:T(8,128)(2,1)S(1)} %bitcast_select_fusion), kind=kLoop, calls=%fused_computation.9 | loop fusion | flops 12976128 | bytes 8650752 | tf_op jit(solution)/shard_map/concatenate | solution.py:245
  32.3 8.8 %all-to-all-start = ((bf16[32,528,128]{2,1,0:T(8,128)(2,1)}), bf16[32,528,128]{2,1,0:T(8,128)(2,1)}, u32[]{:S(2)}, u32[]{:S(2)}) async-start(bf16[32,528,128]{2,1,0:T(8,128)(2,1)} %pad_maximum_fusion), calls=%async_computation | async-start | bytes 8650752 | tf_op jit(solution)/shard_map/all_to_all | solution.py:248
  41.1 3.8 %collective-permute-start.5 = (f32[64,128]{1,0:T(8,128)S(1)}, f32[64,128]{1,0:T(8,128)S(1)}, u32[]{:S(2)}, u32[]{:S(2)}) collective-permute-start(f32[64,128]{1,0:T(8,128)S(1)} %copy-done.6), channel_id=1, source_target_pairs={{0,3},{1,0},{2,1},{3,2},{4,7},{5,4},{6,5},{7,6},{8,11},{9,8},{10,9... | collective-permute-start | bytes 98312 | tf_op jit(solution)/shard_map/ppermute | solution.py:49
  46.5 2.9 %fusion.5 = f32[64,64,128]{2,1,0:T(8,128)} fusion(bf16[64,128,128]{2,1,0:T(8,128)(2,1)S(1)} %copy-done, bf16[64,64,128]{2,1,0:T(8,128)(2,1)S(1)} %gather_fusion.2, pred[64]{0:T(512)(128)(4,1)S(1)} %and_bitcast_fusion), kind=kOutput, calls=%fused_computation.18 | convolution fusion | flops 134742016 | bytes 5242944 | tf_op jit(solution)/shard_map/eik,pek->pei/dot_general | solution.py:252
  49.5 7.0 %scatter_fusion = f32[64,16,128]{2,0,1:T(8,128)S(1)} fusion(f32[64,16,128]{2,0,1:T(8,128)S(1)} %broadcast_in_dim.158, s32[64]{0:T(128)S(1)} %get-tuple-element.23, f32[64,64,128]{2,1,0:T(8,128)} %fusion.5), kind=kCustom, calls=%fused_computation.8 | custom fusion | flops 524288 | bytes 6291712 | tf_op jit(solution)/shard_map/scatter-add | solution.py:256
  58.8 36.0 %all-to-all-done.load_ref = bf16[32,528,128]{2,1,0:T(8,128)(2,1)} async-done(((bf16[32,528,128]{2,1,0:T(8,128)(2,1)}), bf16[32,528,128]{2,1,0:T(8,128)(2,1)}, u32[]{:S(2)}, u32[]{:S(2)}) %all-to-all-start) | async-done | bytes 4325408 | tf_op jit(solution)/shard_map/all_to_all | solution.py:248
  94.8 24.3 %shard_map.138 = f32[256,512]{1,0:T(8,128)} custom-call(bf16[32,528,128]{2,1,0:T(8,128)(2,1)} %all-to-all-done.load_ref, f32[256,512]{1,0:T(8,128)} %bitcast.151), custom_call_target="tpu_custom_call" | custom-call | tf_op jit(solution)/shard_map/pallas_call | solution.py:95
  119.1 1.1 select_bitcast_fusion.3
  120.2 3.8 %collective-permute-start.2 = (f32[64,512]{1,0:T(8,128)S(1)}, f32[64,512]{1,0:T(8,128)S(1)}, u32[]{:S(2)}, u32[]{:S(2)}) collective-permute-start(f32[64,512]{1,0:T(8,128)S(1)} %get-tuple-element.17), channel_id=1, source_target_pairs={{0,3},{1,0},{2,1},{3,2},{4,7},{5,4},{6,5},{7,6},{8,11},{9,8},{10,9... | collective-permute-start | bytes 393224 | tf_op jit(solution)/shard_map/ppermute | solution.py:115
  125.5 4.1 %collective-permute-done.2 = f32[64,512]{1,0:T(8,128)S(1)} collective-permute-done((f32[64,512]{1,0:T(8,128)S(1)}, f32[64,512]{1,0:T(8,128)S(1)}, u32[]{:S(2)}, u32[]{:S(2)}) %collective-permute-start.2) | collective-permute-done | bytes 131104 | tf_op jit(solution)/shard_map/ppermute | solution.py:115
  129.7 3.5 %collective-permute-done = f32[64,512]{1,0:T(8,128)S(1)} collective-permute-done((f32[64,512]{1,0:T(8,128)S(1)}, f32[64,512]{1,0:T(8,128)S(1)}, u32[]{:S(2)}, u32[]{:S(2)}) %collective-permute-start) | collective-permute-done | bytes 131104 | tf_op jit(solution)/shard_map/ppermute | solution.py:115
  137.3 1.4 collective-permute-start.6
  138.8 1.5 collective-permute-done.8
  140.3 1.6 collective-permute-done.7
  146.0 13.4 %shard_map.139 = f32[128,128]{1,0:T(8,128)} custom-call(f32[128,128]{1,0:T(8,128)} %fusion.30.gram_ref), custom_call_target="tpu_custom_call" | custom-call | tf_op jit(solution)/shard_map/pallas_call | solution.py:157
  159.4 1.2 convolution_select_fusion
  161.3 2.4 %collective-permute-start.11 = (f32[1,256,128]{2,1,0:T(8,128)S(1)}, f32[1,256,128]{2,1,0:T(8,128)S(1)}, u32[]{:S(2)}, u32[]{:S(2)}) collective-permute-start(f32[1,256,128]{2,1,0:T(8,128)S(1)} %bitcast.153), channel_id=1, source_target_pairs={{0,3},{1,0},{2,1},{3,2},{4,7},{5,4},{6,5},{7,6},{8,11},{9,8},{10,9... | collective-permute-start | bytes 393224 | tf_op jit(solution)/shard_map/ppermute | solution.py:49
  164.3 1.2 dynamic_slice.15
  165.5 1.2 dynamic_slice.17
  167.8 1.3 collective-permute-done.10
  169.1 1.5 collective-permute-done.9
  171.4 3.4 %collective-permute-start.12 = (f32[256,128]{1,0:T(8,128)S(1)}, f32[256,128]{1,0:T(8,128)S(1)}, u32[]{:S(2)}, u32[]{:S(2)}) collective-permute-start(f32[256,128]{1,0:T(8,128)S(1)} %fusion.21), channel_id=1, source_target_pairs={{0,4},{4,0},{8,12},{12,8},{16,20},{20,16},{24,28},{28,24},{32,36},... | collective-permute-start | bytes 393224 | tf_op jit(solution)/shard_map/ppermute | solution.py:22
  177.5 13.4 %shard_map.140 = f32[128,128]{1,0:T(8,128)} custom-call(f32[128,128]{1,0:T(8,128)} %fusion.32.gram_ref), custom_call_target="tpu_custom_call" | custom-call | tf_op jit(solution)/shard_map/pallas_call | solution.py:157
  190.9 1.1 convolution_select_fusion.2
  192.4 2.3 %collective-permute-start.13 = (f32[256,128]{0,1:T(8,128)S(1)}, f32[256,128]{0,1:T(8,128)S(1)}, u32[]{:S(2)}, u32[]{:S(2)}) collective-permute-start(f32[256,128]{0,1:T(8,128)S(1)} %fusion.15), channel_id=1, source_target_pairs={{0,8},{8,0},{4,12},{12,4},{16,24},{24,16},{20,28},{28,20},{32,40},... | collective-permute-start | bytes 393224 | tf_op jit(solution)/shard_map/ppermute | solution.py:22
  196.0 2.3 %collective-permute-done.13 = f32[256,128]{0,1:T(8,128)S(1)} collective-permute-done((f32[256,128]{0,1:T(8,128)S(1)}, f32[256,128]{0,1:T(8,128)S(1)}, u32[]{:S(2)}, u32[]{:S(2)}) %collective-permute-start.13) | collective-permute-done | bytes 131104 | tf_op jit(solution)/shard_map/ppermute | solution.py:22
  199.8 13.4 %shard_map.141 = f32[128,128]{1,0:T(8,128)} custom-call(f32[128,128]{1,0:T(8,128)} %fusion.31.gram_ref), custom_call_target="tpu_custom_call" | custom-call | tf_op jit(solution)/shard_map/pallas_call | solution.py:157
  213.2 1.1 convolution_select_fusion.1
  (96 shorter events, 28.3 us)
Async XLA Ops:
  0.6 45.9 %copy-start = (bf16[64,128,128]{2,1,0:T(8,128)(2,1)S(1)}, bf16[64,128,128]{2,1,0:T(8,128)(2,1)}, u32[]{:S(2)}) copy-start(bf16[64,128,128]{2,1,0:T(8,128)(2,1)} %param.17) | copy-start | bytes 6291460
  0.6 7.8 %copy-start.1 = (s32[128,128]{1,0:T(8,128)S(1)}, s32[128,128]{1,0:T(8,128)}, u32[]{:S(2)}) copy-start(s32[128,128]{1,0:T(8,128)} %param.16) | copy-start | bytes 196612
  32.3 8.8 %copy-start.6 = (f32[64,128]{1,0:T(8,128)S(1)}, f32[64,128]{1,0:T(8,128)}, u32[]{:S(2)}) copy-start(f32[64,128]{1,0:T(8,128)} %param.20) | copy-start | bytes 98308
  32.3 13.3 %copy-start.7 = (s32[64,2]{0,1:T(2,128)S(1)}, s32[64,2]{0,1:T(2,128)}, u32[]{:S(2)}) copy-start(s32[64,2]{0,1:T(2,128)} %param.18) | copy-start | bytes 1540
  32.3 13.3 %copy-start.3 = (bf16[64,2048]{1,0:T(8,128)(2,1)S(1)}, bf16[64,2048]{1,0:T(8,128)(2,1)}, u32[]{:S(2)}) copy-start(bf16[64,2048]{1,0:T(8,128)(2,1)} %param.19) | copy-start | bytes 786436
  32.3 62.4 %all-to-all-start = ((bf16[32,528,128]{2,1,0:T(8,128)(2,1)}), bf16[32,528,128]{2,1,0:T(8,128)(2,1)}, u32[]{:S(2)}, u32[]{:S(2)}) async-start(bf16[32,528,128]{2,1,0:T(8,128)(2,1)} %pad_maximum_fusion), calls=%async_computation | async-start | bytes 8650752 | tf_op jit(solution)/shard_map/all_to_all | solution.py:248
  41.1 82.9 %collective-permute-start.5 = (f32[64,128]{1,0:T(8,128)S(1)}, f32[64,128]{1,0:T(8,128)S(1)}, u32[]{:S(2)}, u32[]{:S(2)}) collective-permute-start(f32[64,128]{1,0:T(8,128)S(1)} %copy-done.6), channel_id=1, source_target_pairs={{0,3},{1,0},{2,1},{3,2},{4,7},{5,4},{6,5},{7,6},{8,11},{9,8},{10,9... | collective-permute-start | bytes 98312 | tf_op jit(solution)/shard_map/ppermute | solution.py:49
  44.9 80.0 %collective-permute-start.4 = (f32[64,128]{1,0:T(8,128)S(1)}, f32[64,128]{1,0:T(8,128)S(1)}, u32[]{:S(2)}, u32[]{:S(2)}) collective-permute-start(f32[64,128]{1,0:T(8,128)S(1)} %copy-done.6), channel_id=1, source_target_pairs={{0,2},{1,3},{2,0},{3,1},{4,6},{5,7},{6,4},{7,5},{8,10},{9,11},{10,... | collective-permute-start | bytes 98312 | tf_op jit(solution)/shard_map/ppermute | solution.py:49
  45.0 80.0 %collective-permute-start.3 = (f32[64,128]{1,0:T(8,128)S(1)}, f32[64,128]{1,0:T(8,128)S(1)}, u32[]{:S(2)}, u32[]{:S(2)}) collective-permute-start(f32[64,128]{1,0:T(8,128)S(1)} %copy-done.6), channel_id=1, source_target_pairs={{0,1},{1,2},{2,3},{3,0},{4,5},{5,6},{6,7},{7,4},{8,9},{9,10},{10,1... | collective-permute-start | bytes 98312 | tf_op jit(solution)/shard_map/ppermute | solution.py:49
  120.2 9.4 %collective-permute-start.2 = (f32[64,512]{1,0:T(8,128)S(1)}, f32[64,512]{1,0:T(8,128)S(1)}, u32[]{:S(2)}, u32[]{:S(2)}) collective-permute-start(f32[64,512]{1,0:T(8,128)S(1)} %get-tuple-element.17), channel_id=1, source_target_pairs={{0,3},{1,0},{2,1},{3,2},{4,7},{5,4},{6,5},{7,6},{8,11},{9,8},{10,9... | collective-permute-start | bytes 393224 | tf_op jit(solution)/shard_map/ppermute | solution.py:115
  124.1 5.6 %collective-permute-start.1 = (f32[64,512]{1,0:T(8,128)S(1)}, f32[64,512]{1,0:T(8,128)S(1)}, u32[]{:S(2)}, u32[]{:S(2)}) collective-permute-start(f32[64,512]{1,0:T(8,128)S(1)} %get-tuple-element.18), channel_id=1, source_target_pairs={{0,2},{1,3},{2,0},{3,1},{4,6},{5,7},{6,4},{7,5},{8,10},{9,11},{10,... | collective-permute-start | bytes 393224 | tf_op jit(solution)/shard_map/ppermute | solution.py:115
  124.1 9.1 %collective-permute-start = (f32[64,512]{1,0:T(8,128)S(1)}, f32[64,512]{1,0:T(8,128)S(1)}, u32[]{:S(2)}, u32[]{:S(2)}) collective-permute-start(f32[64,512]{1,0:T(8,128)S(1)} %get-tuple-element.19), channel_id=1, source_target_pairs={{0,1},{1,2},{2,3},{3,0},{4,5},{5,6},{6,7},{7,4},{8,9},{9,10},{10,1... | collective-permute-start | bytes 393224 | tf_op jit(solution)/shard_map/ppermute | solution.py:115
  129.7 3.6 %copy-start.4 = (f32[64,512]{1,0:T(8,128)}, f32[64,512]{1,0:T(8,128)S(1)}, u32[]{:S(2)}) copy-start(f32[64,512]{1,0:T(8,128)S(1)} %collective-permute-done.1) | copy-start | bytes 393220
  133.2 0.7 copy-start.5
  137.1 3.2 %collective-permute-start.8 = (f32[1,128,128]{2,1,0:T(8,128)S(1)}, f32[1,128,128]{2,1,0:T(8,128)S(1)}, u32[]{:S(2)}, u32[]{:S(2)}) collective-permute-start(f32[1,128,128]{2,1,0:T(8,128)S(1)} %bitcast.157), channel_id=1, source_target_pairs={{0,3},{1,0},{2,1},{3,2},{4,7},{5,4},{6,5},{7,6},{8,11},{9,8},{10,9... | collective-permute-start | bytes 196616 | tf_op jit(solution)/shard_map/ppermute | solution.py:49
  137.2 4.7 %collective-permute-start.7 = (f32[1,128,128]{2,1,0:T(8,128)S(1)}, f32[1,128,128]{2,1,0:T(8,128)S(1)}, u32[]{:S(2)}, u32[]{:S(2)}) collective-permute-start(f32[1,128,128]{2,1,0:T(8,128)S(1)} %bitcast.158), channel_id=1, source_target_pairs={{0,2},{1,3},{2,0},{3,1},{4,6},{5,7},{6,4},{7,5},{8,10},{9,11},{10,... | collective-permute-start | bytes 196616 | tf_op jit(solution)/shard_map/ppermute | solution.py:49
  137.3 5.4 %collective-permute-start.6 = (f32[1,128,128]{2,1,0:T(8,128)S(1)}, f32[1,128,128]{2,1,0:T(8,128)S(1)}, u32[]{:S(2)}, u32[]{:S(2)}) collective-permute-start(f32[1,128,128]{2,1,0:T(8,128)S(1)} %bitcast.159), channel_id=1, source_target_pairs={{0,1},{1,2},{2,3},{3,0},{4,5},{5,6},{6,7},{7,4},{8,9},{9,10},{10,1... | collective-permute-start | bytes 196616 | tf_op jit(solution)/shard_map/ppermute | solution.py:49
  160.6 0.7 copy-start.2
  161.3 6.5 %collective-permute-start.11 = (f32[1,256,128]{2,1,0:T(8,128)S(1)}, f32[1,256,128]{2,1,0:T(8,128)S(1)}, u32[]{:S(2)}, u32[]{:S(2)}) collective-permute-start(f32[1,256,128]{2,1,0:T(8,128)S(1)} %bitcast.153), channel_id=1, source_target_pairs={{0,3},{1,0},{2,1},{3,2},{4,7},{5,4},{6,5},{7,6},{8,11},{9,8},{10,9... | collective-permute-start | bytes 393224 | tf_op jit(solution)/shard_map/ppermute | solution.py:49
  163.7 5.4 %collective-permute-start.10 = (f32[1,256,128]{2,1,0:T(8,128)S(1)}, f32[1,256,128]{2,1,0:T(8,128)S(1)}, u32[]{:S(2)}, u32[]{:S(2)}) collective-permute-start(f32[1,256,128]{2,1,0:T(8,128)S(1)} %bitcast.154), channel_id=1, source_target_pairs={{0,2},{1,3},{2,0},{3,1},{4,6},{5,7},{6,4},{7,5},{8,10},{9,11},{10,... | collective-permute-start | bytes 393224 | tf_op jit(solution)/shard_map/ppermute | solution.py:49
  163.7 6.9 %collective-permute-start.9 = (f32[1,256,128]{2,1,0:T(8,128)S(1)}, f32[1,256,128]{2,1,0:T(8,128)S(1)}, u32[]{:S(2)}, u32[]{:S(2)}) collective-permute-start(f32[1,256,128]{2,1,0:T(8,128)S(1)} %bitcast.155), channel_id=1, source_target_pairs={{0,1},{1,2},{2,3},{3,0},{4,5},{5,6},{6,7},{7,4},{8,9},{9,10},{10,1... | collective-permute-start | bytes 393224 | tf_op jit(solution)/shard_map/ppermute | solution.py:49
  171.4 4.4 %collective-permute-start.12 = (f32[256,128]{1,0:T(8,128)S(1)}, f32[256,128]{1,0:T(8,128)S(1)}, u32[]{:S(2)}, u32[]{:S(2)}) collective-permute-start(f32[256,128]{1,0:T(8,128)S(1)} %fusion.21), channel_id=1, source_target_pairs={{0,4},{4,0},{8,12},{12,8},{16,20},{20,16},{24,28},{28,24},{32,36},... | collective-permute-start | bytes 393224 | tf_op jit(solution)/shard_map/ppermute | solution.py:22
  192.4 5.9 %collective-permute-start.13 = (f32[256,128]{0,1:T(8,128)S(1)}, f32[256,128]{0,1:T(8,128)S(1)}, u32[]{:S(2)}, u32[]{:S(2)}) collective-permute-start(f32[256,128]{0,1:T(8,128)S(1)} %fusion.15), channel_id=1, source_target_pairs={{0,8},{8,0},{4,12},{12,4},{16,24},{24,16},{20,28},{28,20},{32,40},... | collective-permute-start | bytes 393224 | tf_op jit(solution)/shard_map/ppermute | solution.py:22
